TPU v7x, 256 devices: a whole 4x4x8 slice. The times are simulated.
256 devices in a mesh: prow: 8 (over x_lo, y), pcol: 32 (over x_hi, z, core).
Axes of the slice: x: 4 (x_hi: 2, x_lo: 2; x = x_hi * 2 + x_lo), y: 4, z: 8, core: 2. Of those that a mesh axis runs over, the one named last changes fastest.
Arguments:
- ancestor_inv: bfloat16 [24576, 24576], P('pcol', 'prow'), as said below
- tile_pattern: int32 [192, 192], P('pcol', 'prow'), may hold values from 0 to 1, as said below
- factor_block: bfloat16 [3, 24576, 256], P(None, 'pcol'), may hold values from -0.47851562 to 0.47851562
- row_blocks: int32 [3, 96], replicated, may hold values from 0 to 191, as said below
- diag_base: float32 [3, 256, 256], replicated, may hold values from -6 to 6
Outputs:
- ainv_col: bfloat16 [3, 24576, 256], P(None, 'pcol')
- ainv_row: bfloat16 [3, 256, 24576], P(None, None, 'prow')
- ainv_diag: float32 [3, 256, 256], replicated
Inputs may be any that keep to these rules, and one draw needn't show every extreme that they name: ancestor_inv is symmetric. `tile_pattern`: symmetric, with ones on the diagonal. `row_blocks`: each row is strictly increasing, begins with 0 and ends with 191.
All inputs are finite; a program needn't handle non-finite values.
Results may differ from a plain program's by a relative error of at most 0.005.
Values may be sent and summed in bfloat16 or wider, within the bound.
No kernel may reach another device: no remote copies, remote signals or barrier semaphores. Data moves between devices by JAX's collectives and lax.ppermute only.
A program may use at most 64 MiB of HBM per device.

v0:
```python
import jax
import jax.numpy as jnp
from jax import lax
from jax.sharding import PartitionSpec as P

BLK = 128


def spread(shard, axis, root):
    mine = lax.axis_index(axis) == root
    return lax.psum(jnp.where(mine, shard, jnp.zeros_like(shard)), axis)


def expand_tiles(pattern):
    tile_rows, tile_cols = pattern.shape
    widened = jnp.broadcast_to(
        pattern.astype(jnp.bfloat16)[:, None, :, None], (tile_rows, BLK, tile_cols, BLK)
    )
    return widened.reshape(tile_rows * BLK, tile_cols * BLK)


def structure_rows(row_blocks, row_start, how_many):
    row_ids = row_start + jnp.arange(how_many, dtype=jnp.int32)
    matches = row_blocks[:, None, :] == (row_ids // BLK)[None, :, None]
    return jnp.any(matches, axis=2).astype(jnp.float32)


def shards(ancestor_inv, tile_pattern, factor_block, row_blocks, diag_base):
    col_rows = ancestor_inv.shape[0]
    row_cols = ancestor_inv.shape[1]
    supers = factor_block.shape[0]
    kwidth = factor_block.shape[2]
    prow_idx = lax.axis_index("prow")
    pcol_idx = lax.axis_index("pcol")
    group_ratio = lax.axis_size("pcol") // lax.axis_size("prow")
    inverse_tiles = ancestor_inv * expand_tiles(tile_pattern)
    own_sel = structure_rows(row_blocks, pcol_idx * col_rows, col_rows)
    local_lower = factor_block * own_sel[:, :, None].astype(jnp.bfloat16)
    running = jnp.zeros((supers, col_rows, kwidth), jnp.float32)
    for turn in range(group_ratio):
        slot = turn
        arrived = spread(local_lower, "pcol", prow_idx * group_ratio + slot)
        slab_cols = lax.dynamic_slice_in_dim(inverse_tiles, slot * col_rows, col_rows, 1)
        running = running + jnp.einsum(
            "ij,sjk->sik", slab_cols, arrived, preferred_element_type=jnp.float32
        )
    summed = lax.psum(running, "prow")
    col_exact = -summed * own_sel[:, :, None]
    column = col_exact.astype(jnp.bfloat16)
    row_out = jnp.zeros((supers, kwidth, row_cols), jnp.bfloat16)
    for turn in range(group_ratio):
        slot = turn
        arrived = spread(column, "pcol", prow_idx * group_ratio + slot)
        row_out = lax.dynamic_update_slice_in_dim(
            row_out, jnp.swapaxes(arrived, 1, 2), slot * col_rows, 2
        )
    contrib = jnp.einsum("sik,sil->skl", local_lower.astype(jnp.float32), col_exact)
    diagonal = diag_base - lax.psum(contrib, "pcol")
    return (column, row_out, diagonal)


def solution(mesh):
    in_specs = (P("pcol", "prow"), P("pcol", "prow"), P(None, "pcol", None), P(), P())
    out_specs = (P(None, "pcol", None), P(None, None, "prow"), P())
    return jax.shard_map(shards, mesh=mesh, in_specs=in_specs, out_specs=out_specs, check_vma=False)
```

profile of v0, /device:TPU:4, one launch (start us, length us, event | category | flops | bytes accessed | tf_op | source)
XLA Modules:
  0.0 961.8 jit_solution(11419968180689164165)
XLA Ops:
  7.2 0.0 all-reduce.14.cloned.1.call-start
  7.2 0.9 compare_reduce_fusion
  8.1 0.0 copy-start.8
  8.1 1.6 copy.11
  9.7 0.0 copy-done.8
  9.7 2.4 broadcast_select_fusion
  12.1 0.0 copy-start.9
  12.1 0.0 all-reduce.14.cloned.1.call-update
  12.1 0.0 all-reduce.8.cloned.1.call-start
  12.2 0.6 copy-done.9
  12.8 0.7 broadcast_in_dim.2
  13.5 5.1 bitcast_multiply_fusion
  18.6 277.1 %all-reduce.14.cloned.1.call-done = (bf16[3,768,256]{1,2,0:T(8,128)(2,1)}, bf16[3,768,256]{1,2,0:T(8,128)(2,1)}, bf16[3,768,256]{1,2,0:T(8,128)(2,1)}, bf16[3,768,256]{1,2,0:T(8,128)(2,1)}) async-done(((bf16[3,768,256]{1,2,0:T(8,128)(2,1)}, bf16[3,768,256]{1,2,0:T(8,128)(2,1)}, bf16[3,768,256]{1,2,0:T(8,128)(2,1)}, bf16[3,768,256]{1,2,0:T(8,128)(2,1)}), (bf16[3,768,256]{1,2,0:T(8,128)(2,1)}, ...) | async-done | bytes 4718608 | tf_op jit(solution)/shard_map/psum | solution.py:11
  295.7 0.0 copy-start.1
  295.7 2.9 fusion.2
  298.6 0.2 copy-done.1
  298.8 0.0 copy-start.10
  298.8 2.5 fusion.4
  301.3 0.0 copy-done.10
  301.3 0.0 copy-start.3
  301.3 1.1 fusion.3
  302.4 0.1 copy-done.3
  302.6 2.6 add_bitcast_fusion
  305.1 0.0 all-reduce.8.cloned.1.call-update
  305.1 0.0 all-reduce.10.cloned.1.call-start
  305.2 88.2 %all-reduce.8.cloned.1.call-done = f32[3,768,256]{1,2,0:T(8,128)} async-done(((f32[3,768,256]{1,2,0:T(8,128)}), f32[3,768,256]{1,2,0:T(8,128)}) %all-reduce.8.cloned.1.call-update) | async-done | bytes 2359312 | tf_op jit(solution)/shard_map/psum | solution.py:47
  393.4 0.0 copy-start
  393.4 3.2 fusion
  396.6 0.0 all-reduce.10.cloned.1.call-update
  396.6 0.0 all-reduce.12.cloned.1.call-start
  396.7 0.0 copy-done
  396.7 1.4 select_bitcast_fusion
  398.1 1.9 select_bitcast_fusion.1
  400.0 0.0 all-reduce.12.cloned.1.call-update
  400.0 0.0 copy-start.7
  400.0 1.5 copy.13
  401.5 263.7 %all-reduce.10.cloned.1.call-done = f32[3,256,256]{2,1,0:T(8,128)} async-done(((f32[3,256,256]{2,1,0:T(8,128)}), f32[3,256,256]{2,1,0:T(8,128)}) %all-reduce.10.cloned.1.call-update) | async-done | bytes 786448 | tf_op jit(solution)/shard_map/psum | solution.py:58
  665.1 0.0 copy-done.7
  665.2 2.1 sub.10
  667.3 281.1 %all-reduce.12.cloned.1.call-done = (bf16[3,256,768]{2,1,0:T(8,128)(2,1)}, bf16[3,256,768]{2,1,0:T(8,128)(2,1)}, bf16[3,256,768]{2,1,0:T(8,128)(2,1)}, bf16[3,256,768]{2,1,0:T(8,128)(2,1)}) async-done(((bf16[3,256,768]{2,1,0:T(8,128)(2,1)}, bf16[3,256,768]{2,1,0:T(8,128)(2,1)}, bf16[3,256,768]{2,1,0:T(8,128)(2,1)}, bf16[3,256,768]{2,1,0:T(8,128)(2,1)}), (bf16[3,256,768]{2,1,0:T(8,128)(2,1)}, ...) | async-done | bytes 4718608 | tf_op jit(solution)/shard_map/psum | solution.py:11
  948.4 0.0 copy-start.6
  948.4 2.0 dynamic_update_slice.12
  950.3 0.0 copy-done.6
  950.3 0.0 copy-start.5
  950.3 0.1 constant_dynamic-update-slice_fusion.2
  950.5 1.1 copy-done.5
  951.6 0.0 copy-start.4
  951.6 0.1 constant_dynamic-update-slice_fusion.1
  951.8 1.1 copy-done.4
  952.9 0.1 constant_dynamic-update-slice_fusion
  953.0 0.0 copy-start.2
  953.0 2.2 copy-done.2
  (3 shorter events, 0.0 us)
Async XLA Ops:
  7.2 288.6 %all-reduce.14.cloned.1.call-start = ((), (), s32[]{:S(2)}) async-start(), calls=%async_computation.3 | async-start | bytes 9437184 | tf_op jit(solution)/shard_map/psum | solution.py:11
  8.1 1.6 copy-start.8
  12.1 0.7 copy-start.9
  12.1 381.2 %all-reduce.8.cloned.1.call-start = ((), (), s32[]{:S(2)}) async-start(), calls=%async_computation | async-start | bytes 4718592 | tf_op jit(solution)/shard_map/psum | solution.py:47
  295.7 3.1 copy-start.1
  298.8 2.5 copy-start.10
  301.3 1.3 copy-start.3
  305.1 360.0 %all-reduce.10.cloned.1.call-start = ((), (), s32[]{:S(2)}) async-start(), calls=%async_computation.1 | async-start | bytes 1572864 | tf_op jit(solution)/shard_map/psum | solution.py:58
  393.4 3.3 copy-start
  396.6 551.7 %all-reduce.12.cloned.1.call-start = ((), (), s32[]{:S(2)}) async-start(), calls=%async_computation.2 | async-start | bytes 9437184 | tf_op jit(solution)/shard_map/psum | solution.py:11
  400.0 265.1 %copy-start.7 = (f32[3,256,256]{2,1,0:T(8,128)S(1)}, f32[3,256,256]{2,1,0:T(8,128)}, u32[]{:S(2)}) copy-start(f32[3,256,256]{2,1,0:T(8,128)} %param.9) | copy-start | bytes 2359300
  948.4 2.0 copy-start.6
  950.3 1.3 copy-start.5
  951.6 1.3 copy-start.4
  953.0 2.2 copy-start.2
Sparse Core Ops, SparseCore 0:
  12.3 283.4 all-reduce.13
  305.3 88.0 all-reduce.7
  396.8 268.3 all-reduce.9
  668.5 279.8 all-reduce.11
where the time goes:
time: 964 us; the launch traced here: 962 us
  waiting for transfers between devices  910 us (94%)
  between operations  13.9 us (1%)
  other arithmetic  13.8 us (1%)
  matrix products  12.3 us (1%)
  local copies, waits for them, and re-layouts  11.4 us (1%)
    psum x2, waiting for transfers between devices, spread(): return lax.psum(jnp.where(mine, shard, jnp.zeros_like(shard)), axis)  558 us
    psum x1, waiting for transfers between devices, shards(): diagonal = diag_base - lax.psum(contrib, 'pcol')  264 us
    psum x1, waiting for transfers between devices, shards(): summed = lax.psum(running, 'prow')  88.2 us
  transfers between devices with their start and end apart: 4, of which 4 were waited for; matrix products, arithmetic and copies ran while one was open for 1% of the time, Pallas kernels for 0%

commit v1 on v0

v1 whole, which is shorter than its diff:
```python
import jax
import jax.numpy as jnp
from jax import lax
from jax.sharding import Mesh
from jax.sharding import PartitionSpec as P

BLK = 128
COLS = ("pg", "pr")
ALL = ("prow", "pg", "pr")


def expand_tiles(pattern):
    tile_rows, tile_cols = pattern.shape
    widened = jnp.broadcast_to(
        pattern.astype(jnp.bfloat16)[:, None, :, None], (tile_rows, BLK, tile_cols, BLK)
    )
    return widened.reshape(tile_rows * BLK, tile_cols * BLK)


def structure_rows(row_blocks, row_start, how_many):
    row_ids = row_start + jnp.arange(how_many, dtype=jnp.int32)
    matches = row_blocks[:, None, :] == (row_ids // BLK)[None, :, None]
    return jnp.any(matches, axis=2).astype(jnp.float32)


def swap_perm(n_row, n_grp, n_sub):
    pairs = []
    for q in range(n_row):
        for g in range(n_grp):
            for r in range(n_sub):
                pairs.append(((q * n_grp + g) * n_sub + r, (g * n_grp + q) * n_sub + r))
    return pairs


def gather_cols(block, perm):
    moved = lax.ppermute(block, ALL, perm)
    return lax.all_gather(moved, "pr", axis=0, tiled=False)


def shards(ancestor_inv, tile_pattern, factor_block, row_blocks, diag_base):
    col_rows = ancestor_inv.shape[0]
    n_row = lax.axis_size("prow")
    n_grp = lax.axis_size("pg")
    n_sub = lax.axis_size("pr")
    perm = swap_perm(n_row, n_grp, n_sub)
    supers, _, kwidth = factor_block.shape
    pcol_idx = lax.axis_index("pg") * n_sub + lax.axis_index("pr")
    inverse_tiles = ancestor_inv * expand_tiles(tile_pattern)
    own_sel = structure_rows(row_blocks, pcol_idx * col_rows, col_rows)
    local_lower = factor_block * own_sel[:, :, None].astype(jnp.bfloat16)
    lower_cols = gather_cols(local_lower, perm)
    tiles4 = inverse_tiles.reshape(col_rows, n_sub, col_rows)
    partial = jnp.einsum(
        "irj,rsjk->sik", tiles4, lower_cols, preferred_element_type=jnp.float32
    )
    summed = lax.psum(partial, "prow")
    col_exact = -summed * own_sel[:, :, None]
    column = col_exact.astype(jnp.bfloat16)
    column_cols = gather_cols(column, perm)
    row_out = jnp.transpose(column_cols, (1, 3, 0, 2)).reshape(supers, kwidth, n_sub * col_rows)
    contrib = jnp.einsum(
        "rsjk,rsjl->skl", lower_cols, column_cols, preferred_element_type=jnp.float32
    )
    diagonal = diag_base - lax.psum(contrib, "prow")
    return (column, row_out, diagonal)


def solution(mesh):
    n_row, n_col = mesh.devices.shape
    n_sub = n_col // n_row
    split = Mesh(mesh.devices.reshape(n_row, n_row, n_sub), ALL)
    in_specs = (P(COLS, "prow"), P(COLS, "prow"), P(None, COLS, None), P(), P())
    out_specs = (P(None, COLS, None), P(None, None, "prow"), P())
    return jax.shard_map(shards, mesh=split, in_specs=in_specs, out_specs=out_specs, check_vma=False)
```

time: 964 us -> 526 us (0.55)
  waiting for transfers between devices: 910 us -> 455 us
  local copies, waits for them, and re-layouts: 11.4 us -> 26.6 us
    psum x4 -> x2, waiting for transfers between devices: 910 us -> 159 us  [the longest x1 89.6 us: shards(): summed = lax.psum(partial, 'prow')]
    ppermute x0 -> x2, waiting for transfers between devices: none -> 202 us  [gather_cols(): moved = lax.ppermute(block, ALL, perm)]
    all_gather x0 -> x2, waiting for transfers between devices: none -> 93.7 us  [gather_cols(): return lax.all_gather(moved, 'pr', axis=0, tiled=False)]
    reshape x0 -> x1, local copies, waits for them, and re-layouts: none -> 9.76 us  [shards(): tiles4 = inverse_tiles.reshape(col_rows, n_sub, col_rows)]
  transfers between devices with their start and end apart: 4 -> 6, of which waited for: 4 -> 6; matrix products, arithmetic and copies ran while one was open for 1% -> 5% of each run, Pallas kernels for 0% -> 0%
where the time goes in v1:
time: 526 us; the launch traced here: 525 us
  waiting for transfers between devices  455 us (87%)
  local copies, waits for them, and re-layouts  26.6 us (5%)
  matrix products  15.4 us (3%)
  between operations  13.8 us (3%)
  other arithmetic  10.1 us (2%)
    ppermute x2, waiting for transfers between devices, gather_cols(): moved = lax.ppermute(block, ALL, perm)  202 us
    all_gather x2, waiting for transfers between devices, gather_cols(): return lax.all_gather(moved, 'pr', axis=0, tiled=False)  93.7 us
    psum x1, waiting for transfers between devices, shards(): summed = lax.psum(partial, 'prow')  89.6 us
    psum x1, waiting for transfers between devices, shards(): diagonal = diag_base - lax.psum(contrib, 'prow')  69.2 us
  transfers between devices with their start and end apart: 6, of which 6 were waited for; matrix products, arithmetic and copies ran while one was open for 5% of the time, Pallas kernels for 0%

profile of v1, /device:TPU:4, one launch (start us, length us, event | category | flops | bytes accessed | tf_op | source)
XLA Modules:
  0.0 525.5 jit_solution(17421905209928271445)
XLA Ops:
  7.2 0.0 all-gather.5.cloned.1.call-start
  7.2 0.9 compare_reduce_fusion
  8.1 1.6 broadcast_multiply_fusion
  9.8 2.4 collective-permute-start
  12.2 103.0 %collective-permute-done = bf16[3,768,256]{2,1,0:T(8,128)(2,1)S(1)} collective-permute-done((bf16[3,768,256]{2,1,0:T(8,128)(2,1)S(1)}, bf16[3,768,256]{2,1,0:T(8,128)(2,1)S(1)}, u32[]{:S(2)}, u32[]{:S(2)}) %collective-permute-start) | collective-permute-done | bytes 1179680 | tf_op jit(solution)/shard_map/ppermute | solution.py:36
  115.2 0.0 copy-start.1
  115.2 1.0 copy-done.1
  116.2 0.0 all-gather.5.cloned.1.call-update
  116.2 0.0 all-reduce.3.cloned.1.call-start
  116.3 0.0 copy-start
  116.3 0.8 convert_element_type.26
  117.2 0.7 broadcast_in_dim.2
  117.8 0.8 copy-done
  118.7 2.8 bitcast_multiply_fusion
  121.5 9.8 %reshape.44 = bf16[768,4,768]{2,1,0:T(4,128)(2,1)} reshape(bf16[768,3072]{1,0:T(8,128)(2,1)} %bitcast_multiply_fusion) | data formatting | bytes 9437184 | tf_op jit(solution)/shard_map/reshape | solution.py:52
  131.2 40.8 %all-gather.5.cloned.1.call-done = bf16[12,768,256]{2,1,0:T(8,128)(2,1)} async-done(((bf16[3,768,256]{2,1,0:T(8,128)(2,1)}), bf16[12,768,256]{2,1,0:T(8,128)(2,1)}) %all-gather.5.cloned.1.call-update) | async-done | bytes 4718608 | tf_op jit(solution)/shard_map/all_gather | solution.py:37
  172.0 9.0 %fusion.2 = f32[3,768,256]{1,2,0:T(8,128)} fusion(bf16[4,3,768,256]{3,2,1,0:T(8,128)(2,1)} %bitcast.24, bf16[768,4,768,1]{2,1,0,3:T(4,128)(2,1)} %bitcast.23), kind=kOutput, calls=%fused_computation.4 | convolution fusion | flops 3623878656 | bytes 11796480 | tf_op jit(solution)/shard_map/irj,rsjk->sik/dot_general | solution.py:53
  181.1 0.0 all-reduce.3.cloned.1.call-update
  181.1 0.0 all-gather.7.cloned.1.call-start
  181.2 89.6 %all-reduce.3.cloned.1.call-done = f32[3,768,256]{1,2,0:T(8,128)} async-done(((f32[3,768,256]{1,2,0:T(8,128)}), f32[3,768,256]{1,2,0:T(8,128)}) %all-reduce.3.cloned.1.call-update) | async-done | bytes 2359312 | tf_op jit(solution)/shard_map/psum | solution.py:56
  270.8 1.9 multiply_convert_fusion
  272.6 1.9 collective-permute-start.1
  274.6 99.3 %collective-permute-done.1 = bf16[3,768,256]{1,2,0:T(8,128)(2,1)S(1)} collective-permute-done((bf16[3,768,256]{1,2,0:T(8,128)(2,1)S(1)}, bf16[3,768,256]{1,2,0:T(8,128)(2,1)S(1)}, u32[]{:S(2)}, u32[]{:S(2)}) %collective-permute-start.1) | collective-permute-done | bytes 1179680 | tf_op jit(solution)/shard_map/ppermute | solution.py:36
  373.9 1.4 copy.32
  375.4 0.0 all-gather.7.cloned.1.call-update
  375.4 0.0 all-reduce.5.cloned.1.call-start
  375.4 52.9 %all-gather.7.cloned.1.call-done = bf16[12,768,256]{2,1,0:T(8,128)(2,1)} async-done(((bf16[3,768,256]{2,1,0:T(8,128)(2,1)}), bf16[12,768,256]{2,1,0:T(8,128)(2,1)}) %all-gather.7.cloned.1.call-update) | async-done | bytes 4718608 | tf_op jit(solution)/shard_map/all_gather | solution.py:37
  428.3 6.4 %convolution_bitcast_fusion = f32[3,256,256]{2,1,0:T(8,128)} fusion(bf16[4,3,768,256]{3,2,1,0:T(8,128)(2,1)} %bitcast.25, bf16[4,3,768,256]{3,2,1,0:T(8,128)(2,1)} %bitcast.21), kind=kOutput, calls=%fused_computation.5 | convolution fusion | flops 1207959552 | bytes 10223616 | tf_op jit(solution)/shard_map/rsjk,rsjl->skl/dot_general | solution.py:61
  434.7 0.0 all-reduce.5.cloned.1.call-update
  434.7 1.5 copy.35
  436.2 4.8 copy.33
  440.9 0.0 copy-start.2
  440.9 6.7 %copy.36 = bf16[3,256,3072]{2,1,0:T(8,128)(2,1)} copy(bf16[3,256,3072]{1,2,0:T(8,128)(2,1)} %bitcast.20) | data formatting | bytes 9437184
  447.6 69.2 %all-reduce.5.cloned.1.call-done = f32[3,256,256]{2,1,0:T(8,128)} async-done(((f32[3,256,256]{2,1,0:T(8,128)}), f32[3,256,256]{2,1,0:T(8,128)}) %all-reduce.5.cloned.1.call-update) | async-done | bytes 786448 | tf_op jit(solution)/shard_map/psum | solution.py:64
  516.8 0.0 copy-done.2
  516.8 2.1 sub.10
  (2 shorter events, 0.0 us)
Async XLA Ops:
  7.2 164.9 %all-gather.5.cloned.1.call-start = ((), (), s32[]{:S(2)}) async-start(), calls=%async_computation.2 | async-start | bytes 5898240 | tf_op jit(solution)/shard_map/all_gather | solution.py:37
  9.8 105.4 %collective-permute-start = (bf16[3,768,256]{2,1,0:T(8,128)(2,1)S(1)}, bf16[3,768,256]{2,1,0:T(8,128)(2,1)S(1)}, u32[]{:S(2)}, u32[]{:S(2)}) collective-permute-start(bf16[3,768,256]{2,1,0:T(8,128)(2,1)S(1)} %broadcast_multiply_fusion), channel_id=1, source_target_pairs={{0,0},{1,1},{2,2},{3,3},{4,32},{5,33},{6,34},{7,35},{8,64},{9,65},... | collective-permute-start | bytes 3538952 | tf_op jit(solution)/shard_map/ppermute | solution.py:36
  115.2 1.0 copy-start.1
  116.2 154.5 %all-reduce.3.cloned.1.call-start = ((), (), s32[]{:S(2)}) async-start(), calls=%async_computation | async-start | bytes 4718592 | tf_op jit(solution)/shard_map/psum | solution.py:56
  116.3 2.4 copy-start
  181.1 247.2 %all-gather.7.cloned.1.call-start = ((), (), s32[]{:S(2)}) async-start(), calls=%async_computation.3 | async-start | bytes 5898240 | tf_op jit(solution)/shard_map/all_gather | solution.py:37
  272.6 101.3 %collective-permute-start.1 = (bf16[3,768,256]{1,2,0:T(8,128)(2,1)S(1)}, bf16[3,768,256]{1,2,0:T(8,128)(2,1)S(1)}, u32[]{:S(2)}, u32[]{:S(2)}) collective-permute-start(bf16[3,768,256]{1,2,0:T(8,128)(2,1)S(1)} %multiply_convert_fusion), channel_id=1, source_target_pairs={{0,0},{1,1},{2,2},{3,3},{4,32},{5,33},{6,34},{7,35},{8,64},{9,65},... | collective-permute-start | bytes 3538952 | tf_op jit(solution)/shard_map/ppermute | solution.py:36
  375.4 141.5 %all-reduce.5.cloned.1.call-start = ((), (), s32[]{:S(2)}) async-start(), calls=%async_computation.1 | async-start | bytes 1572864 | tf_op jit(solution)/shard_map/psum | solution.py:64
  440.9 75.9 %copy-start.2 = (f32[3,256,256]{2,1,0:T(8,128)S(1)}, f32[3,256,256]{2,1,0:T(8,128)}, u32[]{:S(2)}) copy-start(f32[3,256,256]{2,1,0:T(8,128)} %param.9) | copy-start | bytes 2359300
Sparse Core Ops, SparseCore 0:
  116.4 55.6 all-gather.4
  181.2 89.5 all-reduce.2
  375.5 52.7 all-gather.6
  434.8 81.9 all-reduce.4

commit v2 on v1

--- a/solution.py
+++ b/solution.py
@@ -23,18 +23,35 @@
     return jnp.any(matches, axis=2).astype(jnp.float32)
 
 
-def swap_perm(n_row, n_grp, n_sub):
-    pairs = []
-    for q in range(n_row):
-        for g in range(n_grp):
-            for r in range(n_sub):
-                pairs.append(((q * n_grp + g) * n_sub + r, (g * n_grp + q) * n_sub + r))
-    return pairs
+def index_of(n_row, n_grp, n_sub, q, g, r):
+    return (q * n_grp + g) * n_sub + r
 
 
-def gather_cols(block, perm):
-    moved = lax.ppermute(block, ALL, perm)
-    return lax.all_gather(moved, "pr", axis=0, tiled=False)
+def swap_perm(n_row, n_grp, n_sub):
+    return [
+        (index_of(n_row, n_grp, n_sub, q, g, r), index_of(n_row, n_grp, n_sub, g, q, r))
+        for q in range(n_row) for g in range(n_grp) for r in range(n_sub)
+    ]
+
+
+def flip_perm(n_row, n_grp, n_sub, bit):
+    return [
+        (index_of(n_row, n_grp, n_sub, q, g, r), index_of(n_row, n_grp, n_sub, q, g, r ^ bit))
+        for q in range(n_row) for g in range(n_grp) for r in range(n_sub)
+    ]
+
+
+def gather_cols(block, perms):
+    swap, far, near = perms
+    sub = lax.axis_index("pr")
+    high = sub // 2
+    low = sub % 2
+    mine = lax.ppermute(block, ALL, swap)
+    other = lax.ppermute(mine, ALL, far)
+    pair = jnp.where(high == 0, jnp.stack([mine, other]), jnp.stack([other, mine]))
+    twin = lax.ppermute(pair, ALL, near)
+    quad = jnp.where(low == 0, jnp.stack([pair, twin], 1), jnp.stack([twin, pair], 1))
+    return quad.reshape((4,) + block.shape)
 
 
 def shards(ancestor_inv, tile_pattern, factor_block, row_blocks, diag_base):
@@ -42,7 +59,11 @@
     n_row = lax.axis_size("prow")
     n_grp = lax.axis_size("pg")
     n_sub = lax.axis_size("pr")
-    perm = swap_perm(n_row, n_grp, n_sub)
+    perm = (
+        swap_perm(n_row, n_grp, n_sub),
+        flip_perm(n_row, n_grp, n_sub, 2),
+        flip_perm(n_row, n_grp, n_sub, 1),
+    )
     supers, _, kwidth = factor_block.shape
     pcol_idx = lax.axis_index("pg") * n_sub + lax.axis_index("pr")
     inverse_tiles = ancestor_inv * expand_tiles(tile_pattern)

time: 526 us -> 513 us (0.975)
  waiting for transfers between devices: 455 us -> 415 us
  local copies, waits for them, and re-layouts: 26.6 us -> 38.3 us
  other arithmetic: 10.1 us -> 21.1 us
    all_gather x2 -> x0, waiting for transfers between devices: 93.7 us -> none  [gather_cols(): return lax.all_gather(moved, 'pr', axis=0, tiled=False)]
    ppermute x2 -> x6, waiting for transfers between devices: 202 us -> 256 us  [the longest x2 202 us: gather_cols(): mine = lax.ppermute(block, ALL, swap)]
    select_n x0 -> x2, local copies, waits for them, and re-layouts: none -> 13.3 us  [gather_cols(): jnp.where(low == 0, jnp.stack([pair, twin], 1), jnp.stack([twin, pair], 1))]
    select_n x0 -> x6, other arithmetic: none -> 11.1 us  [the longest x2 8.13 us: gather_cols(): jnp.where(low == 0, jnp.stack([pair, twin], 1), jnp.stack([twin, pair], 1))]
  transfers between devices with their start and end apart: 6 -> 8, of which waited for: 6 -> 7; matrix products, arithmetic and copies ran while one was open for 5% -> 6% of each run, Pallas kernels for 0% -> 0%
where the time goes in v2:
time: 513 us; the launch traced here: 512 us
  waiting for transfers between devices  415 us (81%)
  local copies, waits for them, and re-layouts  38.3 us (7%)
  other arithmetic  21.1 us (4%)
  matrix products  15.4 us (3%)
  between operations  14.2 us (3%)
  starting transfers between devices  8.19 us (2%)
    ppermute x2, waiting for transfers between devices, gather_cols(): mine = lax.ppermute(block, ALL, swap)  202 us
    psum x1, waiting for transfers between devices, shards(): summed = lax.psum(partial, 'prow')  91.6 us
    psum x1, waiting for transfers between devices, shards(): diagonal = diag_base - lax.psum(contrib, 'prow')  67.2 us
    ppermute x2, waiting for transfers between devices, gather_cols(): other = lax.ppermute(mine, ALL, far)  49.5 us
    select_n x2, local copies, waits for them, and re-layouts, gather_cols(): jnp.where(low == 0, jnp.stack([pair, twin], 1), jnp.stack([twin, pair], 1))  13.3 us
  transfers between devices with their start and end apart: 8, of which 7 were waited for; matrix products, arithmetic and copies ran while one was open for 6% of the time, Pallas kernels for 0%

profile of v2, /device:TPU:4, one launch (start us, length us, event | category | flops | bytes accessed | tf_op | source)
XLA Modules:
  0.0 512.0 jit_solution(4340441077436857681)
XLA Ops:
  7.2 0.0 all-reduce.3.cloned.1.call-start
  7.2 0.9 compare_reduce_fusion
  8.1 1.6 copy.35
  9.7 0.1 broadcast_multiply_fusion
  9.8 2.4 collective-permute-start
  12.2 103.0 %collective-permute-done = bf16[3,768,256]{1,2,0:T(8,128)(2,1)S(1)} collective-permute-done((bf16[3,768,256]{1,2,0:T(8,128)(2,1)S(1)}, bf16[3,768,256]{1,2,0:T(8,128)(2,1)S(1)}, u32[]{:S(2)}, u32[]{:S(2)}) %collective-permute-start) | collective-permute-done | bytes 1179680 | tf_op jit(solution)/shard_map/ppermute | solution.py:49
  115.2 1.9 collective-permute-start.1
  117.2 25.1 %collective-permute-done.1 = bf16[3,768,256]{1,2,0:T(8,128)(2,1)S(1)} collective-permute-done((bf16[3,768,256]{1,2,0:T(8,128)(2,1)S(1)}, bf16[3,768,256]{1,2,0:T(8,128)(2,1)S(1)}, u32[]{:S(2)}, u32[]{:S(2)}) %collective-permute-start.1) | collective-permute-done | bytes 1179680 | tf_op jit(solution)/shard_map/ppermute | solution.py:50
  142.3 0.0 copy-start.1
  142.3 1.8 maximum_select_fusion.2
  144.0 0.0 collective-permute-start.2
  144.0 0.0 copy-done.1
  144.0 0.7 broadcast_in_dim.2
  144.7 5.1 %bitcast_multiply_fusion = bf16[768,3072]{1,0:T(8,128)(2,1)} fusion(bf16[768,3072]{1,0:T(8,128)(2,1)} %param.5, bf16[96,8,24,128]{3,2,1,0:T(8,128)(2,1)S(1)} %bitcast.37), kind=kLoop, calls=%fused_computation | loop fusion | flops 2359296 | bytes 14155776 | tf_op jit(solution)/shard_map/mul | solution.py:69
  149.9 9.8 %reshape.172 = bf16[768,4,768]{2,1,0:T(4,128)(2,1)} reshape(bf16[768,3072]{1,0:T(8,128)(2,1)} %bitcast_multiply_fusion) | data formatting | bytes 9437184 | tf_op jit(solution)/shard_map/reshape | solution.py:73
  159.6 0.4 fusion.2
  160.0 0.0 collective-permute-done.2
  160.0 5.6 %maximum_select_fusion = bf16[2,2,3,768,256]{3,4,2,0,1:T(8,128)(2,1)} fusion(bf16[2,1,3,768,256]{3,4,2,0,1:T(8,128)(2,1)} %bitcast.6, bf16[2,1,3,768,256]{3,4,2,0,1:T(8,128)(2,1)S(1)} %fusion.2, pred[]{:T(512)S(6)} %eq.24), kind=kLoop, calls=%fused_computation.1 | loop fusion | flops 7077888 | bytes 9437185 | tf_op jit(solution)/shard_map/jit(_where)/select_n | solution.py:53
  165.6 6.7 %copy.38 = bf16[2,2,3,768,256]{4,3,2,1,0:T(8,128)(2,1)} copy(bf16[2,2,3,768,256]{3,4,2,0,1:T(8,128)(2,1)} %maximum_select_fusion) | data formatting | bytes 9437184 | tf_op jit(solution)/shard_map/jit(_where)/select_n | solution.py:53
  172.3 9.0 %fusion.3 = f32[3,768,256]{1,2,0:T(8,128)} fusion(bf16[4,3,768,256]{3,2,1,0:T(8,128)(2,1)} %bitcast.49, bf16[768,4,768,1]{2,1,0,3:T(4,128)(2,1)} %bitcast.51), kind=kOutput, calls=%fused_computation.12 | convolution fusion | flops 3623878656 | bytes 11796480 | tf_op jit(solution)/shard_map/irj,rsjk->sik/dot_general | solution.py:74
  181.3 0.0 all-reduce.3.cloned.1.call-update
  181.4 0.0 all-reduce.5.cloned.1.call-start
  181.4 91.6 %all-reduce.3.cloned.1.call-done = f32[3,768,256]{1,2,0:T(8,128)} async-done(((f32[3,768,256]{1,2,0:T(8,128)}), f32[3,768,256]{1,2,0:T(8,128)}) %all-reduce.3.cloned.1.call-update) | async-done | bytes 2359312 | tf_op jit(solution)/shard_map/psum | solution.py:77
  273.0 1.9 multiply_convert_fusion
  274.8 1.9 collective-permute-start.3
  276.7 99.3 %collective-permute-done.3 = bf16[3,768,256]{1,2,0:T(8,128)(2,1)S(1)} collective-permute-done((bf16[3,768,256]{1,2,0:T(8,128)(2,1)S(1)}, bf16[3,768,256]{1,2,0:T(8,128)(2,1)S(1)}, u32[]{:S(2)}, u32[]{:S(2)}) %collective-permute-start.3) | collective-permute-done | bytes 1179680 | tf_op jit(solution)/shard_map/ppermute | solution.py:49
  376.1 1.6 collective-permute-start.4
  377.7 24.4 %collective-permute-done.4 = bf16[3,768,256]{1,2,0:T(8,128)(2,1)S(1)} collective-permute-done((bf16[3,768,256]{1,2,0:T(8,128)(2,1)S(1)}, bf16[3,768,256]{1,2,0:T(8,128)(2,1)S(1)}, u32[]{:S(2)}, u32[]{:S(2)}) %collective-permute-start.4) | collective-permute-done | bytes 1179680 | tf_op jit(solution)/shard_map/ppermute | solution.py:50
  402.1 0.4 maximum_select_fusion.4
  402.5 0.3 collective-permute-start.5
  402.8 0.4 maximum_select_fusion.3
  403.1 4.1 collective-permute-done.5
  407.3 2.5 maximum_select_fusion.1
  409.8 6.7 %copy.41 = bf16[2,2,3,768,256]{4,3,2,1,0:T(8,128)(2,1)} copy(bf16[2,2,3,768,256]{3,4,2,0,1:T(8,128)(2,1)} %maximum_select_fusion.1) | data formatting | bytes 9437184 | tf_op jit(solution)/shard_map/jit(_where)/select_n | solution.py:53
  416.5 6.4 %convolution_bitcast_fusion = f32[3,256,256]{2,1,0:T(8,128)} fusion(bf16[4,3,768,256]{3,2,1,0:T(8,128)(2,1)} %bitcast.50, bf16[4,3,768,256]{3,2,1,0:T(8,128)(2,1)} %bitcast.38), kind=kOutput, calls=%fused_computation.13 | convolution fusion | flops 1207959552 | bytes 10223616 | tf_op jit(solution)/shard_map/rsjk,rsjl->skl/dot_general | solution.py:82
  422.9 0.0 all-reduce.5.cloned.1.call-update
  422.9 1.5 copy.44
  424.4 4.8 copy.42
  429.1 0.0 copy-start
  429.1 6.7 %copy.45 = bf16[3,256,3072]{2,1,0:T(8,128)(2,1)} copy(bf16[3,256,3072]{1,2,0:T(8,128)(2,1)} %bitcast.40) | data formatting | bytes 9437184
  435.8 67.2 %all-reduce.5.cloned.1.call-done = f32[3,256,256]{2,1,0:T(8,128)} async-done(((f32[3,256,256]{2,1,0:T(8,128)}), f32[3,256,256]{2,1,0:T(8,128)}) %all-reduce.5.cloned.1.call-update) | async-done | bytes 786448 | tf_op jit(solution)/shard_map/psum | solution.py:85
  503.0 0.0 copy-done
  503.0 2.1 sub.16
  (3 shorter events, 0.0 us)
Async XLA Ops:
  7.2 265.8 %all-reduce.3.cloned.1.call-start = ((), (), s32[]{:S(2)}) async-start(), calls=%async_computation | async-start | bytes 4718592 | tf_op jit(solution)/shard_map/psum | solution.py:77
  9.8 105.4 %collective-permute-start = (bf16[3,768,256]{1,2,0:T(8,128)(2,1)S(1)}, bf16[3,768,256]{1,2,0:T(8,128)(2,1)S(1)}, u32[]{:S(2)}, u32[]{:S(2)}) collective-permute-start(bf16[3,768,256]{1,2,0:T(8,128)(2,1)S(1)} %broadcast_multiply_fusion), channel_id=1, source_target_pairs={{0,0},{1,1},{2,2},{3,3},{4,32},{5,33},{6,34},{7,35},{8,64},{9,65},... | collective-permute-start | bytes 3538952 | tf_op jit(solution)/shard_map/ppermute | solution.py:49
  115.2 27.0 %collective-permute-start.1 = (bf16[3,768,256]{1,2,0:T(8,128)(2,1)S(1)}, bf16[3,768,256]{1,2,0:T(8,128)(2,1)S(1)}, u32[]{:S(2)}, u32[]{:S(2)}) collective-permute-start(bf16[3,768,256]{1,2,0:T(8,128)(2,1)S(1)} %collective-permute-done), channel_id=1, source_target_pairs={{0,2},{1,3},{2,0},{3,1},{4,6},{5,7},{6,4},{7,5},{8,10},{9,11},{10,... | collective-permute-start | bytes 3538952 | tf_op jit(solution)/shard_map/ppermute | solution.py:50
  142.3 1.8 copy-start.1
  144.0 16.0 %collective-permute-start.2 = (bf16[2,3,768,256]{2,3,1,0:T(8,128)(2,1)}, bf16[2,3,768,256]{2,3,1,0:T(8,128)(2,1)}, u32[]{:S(2)}, u32[]{:S(2)}) collective-permute-start(bf16[2,3,768,256]{2,3,1,0:T(8,128)(2,1)} %maximum_select_fusion.2), channel_id=1, source_target_pairs={{0,1},{1,0},{2,3},{3,2},{4,5},{5,4},{6,7},{7,6},{8,9},{9,8},{10,11... | collective-permute-start | bytes 7077896 | tf_op jit(solution)/shard_map/ppermute | solution.py:52
  181.4 321.6 %all-reduce.5.cloned.1.call-start = ((), (), s32[]{:S(2)}) async-start(), calls=%async_computation.1 | async-start | bytes 1572864 | tf_op jit(solution)/shard_map/psum | solution.py:85
  274.8 101.3 %collective-permute-start.3 = (bf16[3,768,256]{1,2,0:T(8,128)(2,1)S(1)}, bf16[3,768,256]{1,2,0:T(8,128)(2,1)S(1)}, u32[]{:S(2)}, u32[]{:S(2)}) collective-permute-start(bf16[3,768,256]{1,2,0:T(8,128)(2,1)S(1)} %multiply_convert_fusion), channel_id=1, source_target_pairs={{0,0},{1,1},{2,2},{3,3},{4,32},{5,33},{6,34},{7,35},{8,64},{9,65},... | collective-permute-start | bytes 3538952 | tf_op jit(solution)/shard_map/ppermute | solution.py:49
  376.1 26.0 %collective-permute-start.4 = (bf16[3,768,256]{1,2,0:T(8,128)(2,1)S(1)}, bf16[3,768,256]{1,2,0:T(8,128)(2,1)S(1)}, u32[]{:S(2)}, u32[]{:S(2)}) collective-permute-start(bf16[3,768,256]{1,2,0:T(8,128)(2,1)S(1)} %collective-permute-done.3), channel_id=1, source_target_pairs={{0,2},{1,3},{2,0},{3,1},{4,6},{5,7},{6,4},{7,5},{8,10},{9,11},{10,... | collective-permute-start | bytes 3538952 | tf_op jit(solution)/shard_map/ppermute | solution.py:50
  402.5 4.8 collective-permute-start.5
  429.1 73.9 %copy-start = (f32[3,256,256]{2,1,0:T(8,128)S(1)}, f32[3,256,256]{2,1,0:T(8,128)}, u32[]{:S(2)}) copy-start(f32[3,256,256]{2,1,0:T(8,128)} %param.9) | copy-start | bytes 2359300
Sparse Core Ops, SparseCore 0:
  181.5 91.4 all-reduce.2
  423.0 79.9 all-reduce.4

commit v3 on v2

--- a/solution.py
+++ b/solution.py
@@ -27,9 +27,14 @@
     return (q * n_grp + g) * n_sub + r
 
 
+def skew(q, g, n_row):
+    side = 4 if n_row % 4 == 0 else 1
+    return q - q % side + (g + q) % side
+
+
 def swap_perm(n_row, n_grp, n_sub):
     return [
-        (index_of(n_row, n_grp, n_sub, q, g, r), index_of(n_row, n_grp, n_sub, g, q, r))
+        (index_of(n_row, n_grp, n_sub, q, g, r), index_of(n_row, n_grp, n_sub, g, skew(q, g, n_row), r))
         for q in range(n_row) for g in range(n_grp) for r in range(n_sub)
     ]
 

time: 513 us -> 422 us (0.82)
  waiting for transfers between devices: 415 us -> 323 us
    ppermute x2, waiting for transfers between devices: 202 us -> 50.7 us  [gather_cols(): mine = lax.ppermute(block, ALL, swap)]
    psum x1, waiting for transfers between devices: 67.2 us -> 103 us  [shards(): diagonal = diag_base - lax.psum(contrib, 'prow')]
    psum x1, waiting for transfers between devices: 91.6 us -> 120 us  [shards(): summed = lax.psum(partial, 'prow')]
  transfers between devices with their start and end apart: 8 -> 8, of which waited for: 7 -> 7; matrix products, arithmetic and copies ran while one was open for 6% -> 7% of each run, Pallas kernels for 0% -> 0%
where the time goes in v3:
time: 422 us; the launch traced here: 421 us
  waiting for transfers between devices  323 us (77%)
  local copies, waits for them, and re-layouts  38.3 us (9%)
  other arithmetic  21.1 us (5%)
  matrix products  15.4 us (4%)
  between operations  14.2 us (3%)
  starting transfers between devices  8.19 us (2%)
    psum x1, waiting for transfers between devices, shards(): summed = lax.psum(partial, 'prow')  120 us
    psum x1, waiting for transfers between devices, shards(): diagonal = diag_base - lax.psum(contrib, 'prow')  103 us
    ppermute x2, waiting for transfers between devices, gather_cols(): mine = lax.ppermute(block, ALL, swap)  50.7 us
    ppermute x2, waiting for transfers between devices, gather_cols(): other = lax.ppermute(mine, ALL, far)  46.2 us
    select_n x2, local copies, waits for them, and re-layouts, gather_cols(): jnp.where(low == 0, jnp.stack([pair, twin], 1), jnp.stack([twin, pair], 1))  13.3 us
    reshape x1, local copies, waits for them, and re-layouts, shards(): tiles4 = inverse_tiles.reshape(col_rows, n_sub, col_rows)  9.78 us
    unnamed x7, local copies, waits for them, and re-layouts  9.71 us
    dot_general x1, matrix products, shards(): jnp.einsum('irj,rsjk->sik', tiles4, lower_cols, preferred_element_type=jn...  9.04 us
  transfers between devices with their start and end apart: 8, of which 7 were waited for; matrix products, arithmetic and copies ran while one was open for 7% of the time, Pallas kernels for 0%

profile of v3, /device:TPU:4, one launch (start us, length us, event | category | flops | bytes accessed | tf_op | source)
XLA Modules:
  0.0 420.6 jit_solution(4909730786191957056)
XLA Ops:
  7.2 0.0 all-reduce.3.cloned.1.call-start
  7.2 0.9 compare_reduce_fusion
  8.1 1.6 copy.35
  9.7 0.1 broadcast_multiply_fusion
  9.8 2.4 collective-permute-start
  12.2 27.2 %collective-permute-done = bf16[3,768,256]{1,2,0:T(8,128)(2,1)S(1)} collective-permute-done((bf16[3,768,256]{1,2,0:T(8,128)(2,1)S(1)}, bf16[3,768,256]{1,2,0:T(8,128)(2,1)S(1)}, u32[]{:S(2)}, u32[]{:S(2)}) %collective-permute-start) | collective-permute-done | bytes 1179680 | tf_op jit(solution)/shard_map/ppermute | solution.py:54
  39.4 1.9 collective-permute-start.1
  41.3 25.1 %collective-permute-done.1 = bf16[3,768,256]{1,2,0:T(8,128)(2,1)S(1)} collective-permute-done((bf16[3,768,256]{1,2,0:T(8,128)(2,1)S(1)}, bf16[3,768,256]{1,2,0:T(8,128)(2,1)S(1)}, u32[]{:S(2)}, u32[]{:S(2)}) %collective-permute-start.1) | collective-permute-done | bytes 1179680 | tf_op jit(solution)/shard_map/ppermute | solution.py:55
  66.4 0.0 copy-start.1
  66.4 1.8 maximum_select_fusion.2
  68.2 0.0 collective-permute-start.2
  68.2 0.0 copy-done.1
  68.2 0.7 broadcast_in_dim.2
  68.9 5.1 %bitcast_multiply_fusion = bf16[768,3072]{1,0:T(8,128)(2,1)} fusion(bf16[768,3072]{1,0:T(8,128)(2,1)} %param.5, bf16[96,8,24,128]{3,2,1,0:T(8,128)(2,1)S(1)} %bitcast.37), kind=kLoop, calls=%fused_computation | loop fusion | flops 2359296 | bytes 14155776 | tf_op jit(solution)/shard_map/mul | solution.py:74
  74.0 9.8 %reshape.172 = bf16[768,4,768]{2,1,0:T(4,128)(2,1)} reshape(bf16[768,3072]{1,0:T(8,128)(2,1)} %bitcast_multiply_fusion) | data formatting | bytes 9437184 | tf_op jit(solution)/shard_map/reshape | solution.py:78
  83.8 0.4 fusion.2
  84.2 0.0 collective-permute-done.2
  84.2 5.6 %maximum_select_fusion = bf16[2,2,3,768,256]{3,4,2,0,1:T(8,128)(2,1)} fusion(bf16[2,1,3,768,256]{3,4,2,0,1:T(8,128)(2,1)} %bitcast.6, bf16[2,1,3,768,256]{3,4,2,0,1:T(8,128)(2,1)S(1)} %fusion.2, pred[]{:T(512)S(6)} %eq.24), kind=kLoop, calls=%fused_computation.1 | loop fusion | flops 7077888 | bytes 9437185 | tf_op jit(solution)/shard_map/jit(_where)/select_n | solution.py:58
  89.8 6.7 %copy.38 = bf16[2,2,3,768,256]{4,3,2,1,0:T(8,128)(2,1)} copy(bf16[2,2,3,768,256]{3,4,2,0,1:T(8,128)(2,1)} %maximum_select_fusion) | data formatting | bytes 9437184 | tf_op jit(solution)/shard_map/jit(_where)/select_n | solution.py:58
  96.4 9.0 %fusion.3 = f32[3,768,256]{1,2,0:T(8,128)} fusion(bf16[4,3,768,256]{3,2,1,0:T(8,128)(2,1)} %bitcast.49, bf16[768,4,768,1]{2,1,0,3:T(4,128)(2,1)} %bitcast.51), kind=kOutput, calls=%fused_computation.12 | convolution fusion | flops 3623878656 | bytes 11796480 | tf_op jit(solution)/shard_map/irj,rsjk->sik/dot_general | solution.py:79
  105.5 0.0 all-reduce.3.cloned.1.call-update
  105.5 0.0 all-reduce.5.cloned.1.call-start
  105.6 119.5 %all-reduce.3.cloned.1.call-done = f32[3,768,256]{1,2,0:T(8,128)} async-done(((f32[3,768,256]{1,2,0:T(8,128)}), f32[3,768,256]{1,2,0:T(8,128)}) %all-reduce.3.cloned.1.call-update) | async-done | bytes 2359312 | tf_op jit(solution)/shard_map/psum | solution.py:82
  225.1 1.9 multiply_convert_fusion
  226.9 1.9 collective-permute-start.3
  228.9 23.5 %collective-permute-done.3 = bf16[3,768,256]{1,2,0:T(8,128)(2,1)S(1)} collective-permute-done((bf16[3,768,256]{1,2,0:T(8,128)(2,1)S(1)}, bf16[3,768,256]{1,2,0:T(8,128)(2,1)S(1)}, u32[]{:S(2)}, u32[]{:S(2)}) %collective-permute-start.3) | collective-permute-done | bytes 1179680 | tf_op jit(solution)/shard_map/ppermute | solution.py:54
  252.4 1.6 collective-permute-start.4
  253.9 21.1 %collective-permute-done.4 = bf16[3,768,256]{1,2,0:T(8,128)(2,1)S(1)} collective-permute-done((bf16[3,768,256]{1,2,0:T(8,128)(2,1)S(1)}, bf16[3,768,256]{1,2,0:T(8,128)(2,1)S(1)}, u32[]{:S(2)}, u32[]{:S(2)}) %collective-permute-start.4) | collective-permute-done | bytes 1179680 | tf_op jit(solution)/shard_map/ppermute | solution.py:55
  275.1 0.4 maximum_select_fusion.4
  275.4 0.3 collective-permute-start.5
  275.7 0.4 maximum_select_fusion.3
  276.1 4.1 collective-permute-done.5
  280.2 2.5 maximum_select_fusion.1
  282.8 6.7 %copy.41 = bf16[2,2,3,768,256]{4,3,2,1,0:T(8,128)(2,1)} copy(bf16[2,2,3,768,256]{3,4,2,0,1:T(8,128)(2,1)} %maximum_select_fusion.1) | data formatting | bytes 9437184 | tf_op jit(solution)/shard_map/jit(_where)/select_n | solution.py:58
  289.5 6.4 %convolution_bitcast_fusion = f32[3,256,256]{2,1,0:T(8,128)} fusion(bf16[4,3,768,256]{3,2,1,0:T(8,128)(2,1)} %bitcast.50, bf16[4,3,768,256]{3,2,1,0:T(8,128)(2,1)} %bitcast.38), kind=kOutput, calls=%fused_computation.13 | convolution fusion | flops 1207959552 | bytes 10223616 | tf_op jit(solution)/shard_map/rsjk,rsjl->skl/dot_general | solution.py:87
  295.9 0.0 all-reduce.5.cloned.1.call-update
  295.9 1.5 copy.44
  297.3 4.8 %copy.42 = bf16[3,256,4,768]{1,3,2,0:T(8,128)(2,1)} copy(bf16[3,256,4,768]{1,3,0,2:T(8,128)(2,1)} %bitcast.39) | data formatting | bytes 9437184 | tf_op jit(solution)/shard_map/transpose | solution.py:86
  302.1 0.0 copy-start
  302.1 6.7 %copy.45 = bf16[3,256,3072]{2,1,0:T(8,128)(2,1)} copy(bf16[3,256,3072]{1,2,0:T(8,128)(2,1)} %bitcast.40) | data formatting | bytes 9437184
  308.8 102.9 %all-reduce.5.cloned.1.call-done = f32[3,256,256]{2,1,0:T(8,128)} async-done(((f32[3,256,256]{2,1,0:T(8,128)}), f32[3,256,256]{2,1,0:T(8,128)}) %all-reduce.5.cloned.1.call-update) | async-done | bytes 786448 | tf_op jit(solution)/shard_map/psum | solution.py:90
  411.7 0.0 copy-done
  411.7 2.1 sub.16
  (3 shorter events, 0.0 us)
Async XLA Ops:
  7.2 217.9 %all-reduce.3.cloned.1.call-start = ((), (), s32[]{:S(2)}) async-start(), calls=%async_computation | async-start | bytes 4718592 | tf_op jit(solution)/shard_map/psum | solution.py:82
  9.8 29.6 %collective-permute-start = (bf16[3,768,256]{1,2,0:T(8,128)(2,1)S(1)}, bf16[3,768,256]{1,2,0:T(8,128)(2,1)S(1)}, u32[]{:S(2)}, u32[]{:S(2)}) collective-permute-start(bf16[3,768,256]{1,2,0:T(8,128)(2,1)S(1)} %broadcast_multiply_fusion), channel_id=1, source_target_pairs={{0,0},{1,1},{2,2},{3,3},{4,36},{5,37},{6,38},{7,39},{8,72},{9,73},... | collective-permute-start | bytes 3538952 | tf_op jit(solution)/shard_map/ppermute | solution.py:54
  39.4 27.0 %collective-permute-start.1 = (bf16[3,768,256]{1,2,0:T(8,128)(2,1)S(1)}, bf16[3,768,256]{1,2,0:T(8,128)(2,1)S(1)}, u32[]{:S(2)}, u32[]{:S(2)}) collective-permute-start(bf16[3,768,256]{1,2,0:T(8,128)(2,1)S(1)} %collective-permute-done), channel_id=1, source_target_pairs={{0,2},{1,3},{2,0},{3,1},{4,6},{5,7},{6,4},{7,5},{8,10},{9,11},{10,... | collective-permute-start | bytes 3538952 | tf_op jit(solution)/shard_map/ppermute | solution.py:55
  66.4 1.8 copy-start.1
  68.2 16.0 %collective-permute-start.2 = (bf16[2,3,768,256]{2,3,1,0:T(8,128)(2,1)}, bf16[2,3,768,256]{2,3,1,0:T(8,128)(2,1)}, u32[]{:S(2)}, u32[]{:S(2)}) collective-permute-start(bf16[2,3,768,256]{2,3,1,0:T(8,128)(2,1)} %maximum_select_fusion.2), channel_id=1, source_target_pairs={{0,1},{1,0},{2,3},{3,2},{4,5},{5,4},{6,7},{7,6},{8,9},{9,8},{10,11... | collective-permute-start | bytes 7077896 | tf_op jit(solution)/shard_map/ppermute | solution.py:57
  105.5 306.2 %all-reduce.5.cloned.1.call-start = ((), (), s32[]{:S(2)}) async-start(), calls=%async_computation.1 | async-start | bytes 1572864 | tf_op jit(solution)/shard_map/psum | solution.py:90
  226.9 25.4 %collective-permute-start.3 = (bf16[3,768,256]{1,2,0:T(8,128)(2,1)S(1)}, bf16[3,768,256]{1,2,0:T(8,128)(2,1)S(1)}, u32[]{:S(2)}, u32[]{:S(2)}) collective-permute-start(bf16[3,768,256]{1,2,0:T(8,128)(2,1)S(1)} %multiply_convert_fusion), channel_id=1, source_target_pairs={{0,0},{1,1},{2,2},{3,3},{4,36},{5,37},{6,38},{7,39},{8,72},{9,73},... | collective-permute-start | bytes 3538952 | tf_op jit(solution)/shard_map/ppermute | solution.py:54
  252.4 22.7 %collective-permute-start.4 = (bf16[3,768,256]{1,2,0:T(8,128)(2,1)S(1)}, bf16[3,768,256]{1,2,0:T(8,128)(2,1)S(1)}, u32[]{:S(2)}, u32[]{:S(2)}) collective-permute-start(bf16[3,768,256]{1,2,0:T(8,128)(2,1)S(1)} %collective-permute-done.3), channel_id=1, source_target_pairs={{0,2},{1,3},{2,0},{3,1},{4,6},{5,7},{6,4},{7,5},{8,10},{9,11},{10,... | collective-permute-start | bytes 3538952 | tf_op jit(solution)/shard_map/ppermute | solution.py:55
  275.4 4.8 %collective-permute-start.5 = (bf16[2,3,768,256]{2,3,1,0:T(8,128)(2,1)S(1)}, bf16[2,3,768,256]{2,3,1,0:T(8,128)(2,1)S(1)}, u32[]{:S(2)}, u32[]{:S(2)}) collective-permute-start(bf16[2,3,768,256]{2,3,1,0:T(8,128)(2,1)S(1)} %maximum_select_fusion.4), channel_id=1, source_target_pairs={{0,1},{1,0},{2,3},{3,2},{4,5},{5,4},{6,7},{7,6},{8,9},{9,8},{10,11... | collective-permute-start | bytes 7077896 | tf_op jit(solution)/shard_map/ppermute | solution.py:57
  302.1 109.6 %copy-start = (f32[3,256,256]{2,1,0:T(8,128)S(1)}, f32[3,256,256]{2,1,0:T(8,128)}, u32[]{:S(2)}) copy-start(f32[3,256,256]{2,1,0:T(8,128)} %param.9) | copy-start | bytes 2359300
Sparse Core Ops, SparseCore 0:
  105.6 119.3 all-reduce.2
  296.0 115.6 all-reduce.4

commit v4 on v3

--- a/solution.py
+++ b/solution.py
@@ -48,19 +48,19 @@
 
 def gather_cols(block, perms):
     swap, far, near = perms
-    sub = lax.axis_index("pr")
-    high = sub // 2
-    low = sub % 2
     mine = lax.ppermute(block, ALL, swap)
     other = lax.ppermute(mine, ALL, far)
-    pair = jnp.where(high == 0, jnp.stack([mine, other]), jnp.stack([other, mine]))
+    pair = jnp.stack([mine, other])
     twin = lax.ppermute(pair, ALL, near)
-    quad = jnp.where(low == 0, jnp.stack([pair, twin], 1), jnp.stack([twin, pair], 1))
-    return quad.reshape((4,) + block.shape)
+    return jnp.stack([pair, twin])
+
+
+def flip_if(x, cond, axis):
+    return jnp.where(cond, jnp.flip(x, axis), x)
 
 
 def shards(ancestor_inv, tile_pattern, factor_block, row_blocks, diag_base):
-    col_rows = ancestor_inv.shape[0]
+    col_rows, row_cols = ancestor_inv.shape
     n_row = lax.axis_size("prow")
     n_grp = lax.axis_size("pg")
     n_sub = lax.axis_size("pr")
@@ -70,25 +70,43 @@
         flip_perm(n_row, n_grp, n_sub, 1),
     )
     supers, _, kwidth = factor_block.shape
-    pcol_idx = lax.axis_index("pg") * n_sub + lax.axis_index("pr")
-    inverse_tiles = ancestor_inv * expand_tiles(tile_pattern)
+    width = supers * kwidth
+    sub = lax.axis_index("pr")
+    zbit = sub // 2 == 1
+    kbit = sub % 2 == 1
+    pcol_idx = lax.axis_index("pg") * n_sub + sub
     own_sel = structure_rows(row_blocks, pcol_idx * col_rows, col_rows)
-    local_lower = factor_block * own_sel[:, :, None].astype(jnp.bfloat16)
-    lower_cols = gather_cols(local_lower, perm)
-    tiles4 = inverse_tiles.reshape(col_rows, n_sub, col_rows)
-    partial = jnp.einsum(
-        "irj,rsjk->sik", tiles4, lower_cols, preferred_element_type=jnp.float32
-    )
+    sel_rows = jnp.transpose(own_sel)[:, :, None]
+    local_lower = jnp.transpose(factor_block, (1, 0, 2)) * sel_rows.astype(jnp.bfloat16)
+    lower_cols = gather_cols(local_lower.reshape(col_rows, width), perm)
+    mask = expand_tiles(tile_pattern)
+    zint = zbit.astype(jnp.int32)
+    kint = kbit.astype(jnp.int32)
+    pieces = []
+    for a in range(2):
+        for b in range(2):
+            start = (2 * (zint ^ b) + (kint ^ a)) * col_rows
+            pieces.append(
+                lax.dynamic_slice_in_dim(ancestor_inv, start, col_rows, 1)
+                * lax.dynamic_slice_in_dim(mask, start, col_rows, 1)
+            )
+    tiles = jnp.concatenate(pieces, axis=1)
+    partial = jnp.dot(tiles, lower_cols.reshape(row_cols, width), preferred_element_type=jnp.float32)
     summed = lax.psum(partial, "prow")
-    col_exact = -summed * own_sel[:, :, None]
+    col_exact = -summed.reshape(col_rows, supers, kwidth) * sel_rows
     column = col_exact.astype(jnp.bfloat16)
-    column_cols = gather_cols(column, perm)
-    row_out = jnp.transpose(column_cols, (1, 3, 0, 2)).reshape(supers, kwidth, n_sub * col_rows)
+    column_cols = gather_cols(column.reshape(col_rows, width), perm)
     contrib = jnp.einsum(
-        "rsjk,rsjl->skl", lower_cols, column_cols, preferred_element_type=jnp.float32
+        "jsk,jsl->skl",
+        lower_cols.reshape(row_cols, supers, kwidth),
+        column_cols.reshape(row_cols, supers, kwidth),
+        preferred_element_type=jnp.float32,
     )
     diagonal = diag_base - lax.psum(contrib, "prow")
-    return (column, row_out, diagonal)
+    ordered = flip_if(flip_if(column_cols, kbit, 0), zbit, 1)
+    ordered = ordered.reshape(2, 2, col_rows, supers, kwidth)
+    row_out = jnp.transpose(ordered, (3, 4, 1, 0, 2)).reshape(supers, kwidth, row_cols)
+    return (jnp.transpose(column, (1, 0, 2)), row_out, diagonal)
 
 
 def solution(mesh):

time: 422 us -> 447 us (1.059)
  local copies, waits for them, and re-layouts: 38.3 us -> 71.2 us
  waiting for transfers between devices: 323 us -> 302 us
  other arithmetic: 21.1 us -> 35.3 us
    another operation x0 -> x2, local copies, waits for them, and re-layouts: none -> 16.1 us  [gather_cols(): return jnp.stack([pair, twin])]
    psum x1, waiting for transfers between devices: 103 us -> 88 us  [shards(): diagonal = diag_base - lax.psum(contrib, 'prow')]
    reshape x1 -> x2, local copies, waits for them, and re-layouts: 9.78 us -> 22.6 us  [the longest x1 11.4 us: shards(): column_cols.reshape(row_cols, supers, kwidth)]
    another operation x0 -> x4, other arithmetic: none -> 12 us  [gather_cols(): return jnp.stack([pair, twin])]
    select_n x2 -> x1, local copies, waits for them, and re-layouts: 13.3 us -> 6.64 us  [flip_if(): return jnp.where(cond, jnp.flip(x, axis), x)]
    unnamed x7 -> x12, local copies, waits for them, and re-layouts: 9.71 us -> 13.3 us
    select_n x6 -> x2, other arithmetic: 11.1 us -> 7.97 us  [flip_if(): return jnp.where(cond, jnp.flip(x, axis), x)]
  transfers between devices with their start and end apart: 8 -> 8, of which waited for: 7 -> 6; matrix products, arithmetic and copies ran while one was open for 7% -> 15% of each run, Pallas kernels for 0% -> 0%
where the time goes in v4:
time: 447 us; the launch traced here: 445 us
  waiting for transfers between devices  302 us (68%)
  local copies, waits for them, and re-layouts  71.2 us (16%)
  other arithmetic  35.3 us (8%)
  matrix products  14.5 us (3%)
  between operations  14.1 us (3%)
  starting transfers between devices  7.91 us (2%)
    psum x1, waiting for transfers between devices, shards(): summed = lax.psum(partial, 'prow')  117 us
    psum x1, waiting for transfers between devices, shards(): diagonal = diag_base - lax.psum(contrib, 'prow')  88 us
    ppermute x2, waiting for transfers between devices, gather_cols(): mine = lax.ppermute(block, ALL, swap)  50.7 us
    ppermute x2, waiting for transfers between devices, gather_cols(): other = lax.ppermute(mine, ALL, far)  46.2 us
    another operation x2, local copies, waits for them, and re-layouts, gather_cols(): return jnp.stack([pair, twin])  16.1 us
    unnamed x12, local copies, waits for them, and re-layouts  13.3 us
    another operation x4, other arithmetic, gather_cols(): return jnp.stack([pair, twin])  12 us
    reshape x1, local copies, waits for them, and re-layouts, shards(): column_cols.reshape(row_cols, supers, kwidth)  11.4 us
  transfers between devices with their start and end apart: 8, of which 6 were waited for; matrix products, arithmetic and copies ran while one was open for 15% of the time, Pallas kernels for 0%

profile of v4, /device:TPU:4, one launch (start us, length us, event | category | flops | bytes accessed | tf_op | source)
XLA Modules:
  0.0 445.2 jit_solution(2524777750960907079)
XLA Ops:
  7.2 0.0 all-reduce.3.cloned.1.call-start
  7.2 0.9 compare_reduce_fusion
  8.1 1.6 copy.37
  9.7 0.1 bitcast_multiply_fusion
  9.8 2.4 collective-permute-start
  12.2 27.2 %collective-permute-done = bf16[768,768]{0,1:T(8,128)(2,1)S(1)} collective-permute-done((bf16[768,768]{0,1:T(8,128)(2,1)S(1)}, bf16[768,768]{0,1:T(8,128)(2,1)S(1)}, u32[]{:S(2)}, u32[]{:S(2)}) %collective-permute-start) | collective-permute-done | bytes 1179680 | tf_op jit(solution)/shard_map/ppermute | solution.py:51
  39.4 1.9 collective-permute-start.1
  41.3 25.1 %collective-permute-done.1 = bf16[768,768]{0,1:T(8,128)(2,1)S(1)} collective-permute-done((bf16[768,768]{0,1:T(8,128)(2,1)S(1)}, bf16[768,768]{0,1:T(8,128)(2,1)S(1)}, u32[]{:S(2)}, u32[]{:S(2)}) %collective-permute-start.1) | collective-permute-done | bytes 1179680 | tf_op jit(solution)/shard_map/ppermute | solution.py:52
  66.4 0.0 copy-start.3
  66.4 1.7 fusion.17
  68.1 0.0 collective-permute-start.2
  68.1 0.0 copy-done.3
  68.1 0.7 broadcast_in_dim.2
  68.8 3.6 copy.59
  72.4 6.3 %dynamic-slice_multiply_fusion.3 = (bf16[768,768]{1,0:T(8,128)(2,1)S(1)}, bf16[768,768]{1,0:T(8,128)(2,1)}, bf16[768,768]{1,0:T(8,128)(2,1)}, bf16[768,768]{1,0:T(8,128)(2,1)}) fusion(bf16[768,3072]{1,0:T(8,128)(2,1)} %bitcast.40, s32[]{:T(128)S(6)} %select_n.52, bf16[768,3072]{1,0:T(8,128)(2,1)} %param.5, s32[]{:T(128)S(6)} %select_n.55, s32[]{:T(128)S(6)} %select_n.54, ...), kind=kLoop, calls=%fused_computation.24 | loop fusion | flops 9437184 | bytes 14155792 | tf_op jit(solution)/shard_map/mul | solution.py:90
  78.7 0.0 collective-permute-done.2
  78.7 4.3 pad_maximum_fusion
  83.0 0.0 copy-start
  83.0 0.0 copy-start.1
  83.0 6.8 %copy.40 = bf16[2,2,768,768]{3,2,1,0:T(8,128)(2,1)} copy(bf16[2,2,768,768]{2,3,1,0:T(8,128)(2,1)} %pad_maximum_fusion) | data formatting | bytes 9437184 | tf_op jit(solution)/shard_map/stack | solution.py:55
  89.8 0.0 copy-done
  89.8 0.0 copy-done.1
  89.8 8.0 %fusion = f32[768,768]{1,0:T(8,128)} fusion(bf16[3072,768]{1,0:T(8,128)(2,1)} %bitcast.43, bf16[768,768]{1,0:T(8,128)(2,1)S(1)} %copy-done, bf16[768,768]{1,0:T(8,128)(2,1)S(1)} %copy-done.1, bf16[768,768]{1,0:T(8,128)(2,1)} %get-tuple-element.15, bf16[768,768]{1,0:T(8,128)(2,1)S(1)} %get-tuple-element.12), kind=kOutput, calls=%fused_computation.3 | convolution fusion | flops 3642753024 | bytes 11796480 | tf_op jit(solution)/shard_map/dot_general | solution.py:94
  97.7 0.0 all-reduce.3.cloned.1.call-update
  97.7 0.0 all-reduce.5.cloned.1.call-start
  97.8 0.2 mul.73
  98.0 2.0 copy.42
  100.0 117.3 %all-reduce.3.cloned.1.call-done = f32[768,768]{1,0:T(8,128)} async-done(((f32[768,768]{1,0:T(8,128)}), f32[768,768]{1,0:T(8,128)}) %all-reduce.3.cloned.1.call-update) | async-done | bytes 2359312 | tf_op jit(solution)/shard_map/psum | solution.py:95
  217.2 4.1 multiply_convert_fusion
  221.4 1.9 collective-permute-start.3
  223.3 23.5 %collective-permute-done.3 = bf16[768,768]{1,0:T(8,128)(2,1)S(1)} collective-permute-done((bf16[768,768]{1,0:T(8,128)(2,1)S(1)}, bf16[768,768]{1,0:T(8,128)(2,1)S(1)}, u32[]{:S(2)}, u32[]{:S(2)}) %collective-permute-start.3) | collective-permute-done | bytes 1179680 | tf_op jit(solution)/shard_map/ppermute | solution.py:51
  246.8 1.6 collective-permute-start.4
  248.3 21.1 %collective-permute-done.4 = bf16[768,768]{1,0:T(8,128)(2,1)S(1)} collective-permute-done((bf16[768,768]{1,0:T(8,128)(2,1)S(1)}, bf16[768,768]{1,0:T(8,128)(2,1)S(1)}, u32[]{:S(2)}, u32[]{:S(2)}) %collective-permute-start.4) | collective-permute-done | bytes 1179680 | tf_op jit(solution)/shard_map/ppermute | solution.py:52
  269.5 1.8 fusion.16
  271.3 0.0 collective-permute-start.5
  271.3 9.3 %copy.45 = bf16[2,2,768,768]{2,1,0,3:T(2,128)(2,1)} copy(bf16[2,2,768,768]{2,3,1,0:T(8,128)(2,1)} %pad_maximum_fusion) | data formatting | bytes 9437184 | tf_op jit(solution)/shard_map/stack | solution.py:55
  280.6 11.3 %reshape.60 = bf16[3072,3,256]{0,2,1:T(8,128)(2,1)} reshape(bf16[2,2,768,768]{2,1,0,3:T(2,128)(2,1)} %copy.45) | data formatting | bytes 9437184 | tf_op jit(solution)/shard_map/reshape | solution.py:101
  291.8 3.0 copy.41
  294.9 1.8 fusion.10
  296.7 1.5 copy.48
  298.2 0.0 collective-permute-done.5
  298.2 4.3 pad_maximum_fusion.1
  302.5 11.4 %reshape.62 = bf16[3072,3,256]{2,1,0:T(4,128)(2,1)} reshape(bf16[2,2,768,768]{3,2,1,0:T(8,128)(2,1)} %pad_maximum_fusion.1) | data formatting | bytes 9437184 | tf_op jit(solution)/shard_map/reshape | solution.py:102
  313.8 6.5 %fusion.8 = f32[3,256,256]{2,1,0:T(8,128)} fusion(bf16[3072,3,256]{0,2,1:T(8,128)(2,1)} %reshape.60, bf16[3072,3,256]{2,1,0:T(4,128)(2,1)} %reshape.62), kind=kOutput, calls=%fused_computation.13 | convolution fusion | flops 1207959552 | bytes 10223616 | tf_op jit(solution)/shard_map/jsk,jsl->skl/dot_general | solution.py:99
  320.3 0.0 all-reduce.5.cloned.1.call-update
  320.4 4.8 %reverse_select_fusion.1 = bf16[2,2,768,768]{3,2,1,0:T(8,128)(2,1)S(1)} fusion(bf16[2,2,768,768]{3,2,1,0:T(8,128)(2,1)} %pad_maximum_fusion.1, pred[]{:T(512)S(6)} %eq.22), kind=kLoop, calls=%fused_computation.1 | loop fusion | flops 2359296 | bytes 9437185 | tf_op jit(solution)/shard_map/jit(_where)/select_n | solution.py:59
  325.2 3.1 reverse_select_fusion
  328.3 6.6 %copy.43 = bf16[2,2,768,768]{2,3,1,0:T(8,128)(2,1)} copy(bf16[2,2,768,768]{3,2,1,0:T(8,128)(2,1)} %reverse_select_fusion) | data formatting | bytes 9437184 | tf_op jit(solution)/shard_map/jit(_where)/select_n | solution.py:59
  335.0 6.6 %copy.44 = bf16[3,256,2,2,768]{1,4,3,2,0:T(8,128)(2,1)} copy(bf16[3,256,2,2,768]{4,1,0,2,3:T(8,128)(2,1)} %bitcast.38) | data formatting | bytes 9437184 | tf_op jit(solution)/shard_map/transpose | solution.py:108
  341.6 0.0 copy-start.2
  341.6 6.7 %copy.49 = bf16[3,256,3072]{2,1,0:T(8,128)(2,1)} copy(bf16[3,256,3072]{1,2,0:T(8,128)(2,1)} %bitcast.39) | data formatting | bytes 9437184
  348.3 88.0 %all-reduce.5.cloned.1.call-done = f32[3,256,256]{2,1,0:T(8,128)} async-done(((f32[3,256,256]{2,1,0:T(8,128)}), f32[3,256,256]{2,1,0:T(8,128)}) %all-reduce.5.cloned.1.call-update) | async-done | bytes 786448 | tf_op jit(solution)/shard_map/psum | solution.py:105
  436.3 0.0 copy-done.2
  436.3 2.1 sub.15
  (3 shorter events, 0.0 us)
Async XLA Ops:
  7.2 210.1 %all-reduce.3.cloned.1.call-start = ((), (), s32[]{:S(2)}) async-start(), calls=%async_computation | async-start | bytes 4718592 | tf_op jit(solution)/shard_map/psum | solution.py:95
  9.8 29.6 %collective-permute-start = (bf16[768,768]{0,1:T(8,128)(2,1)S(1)}, bf16[768,768]{0,1:T(8,128)(2,1)S(1)}, u32[]{:S(2)}, u32[]{:S(2)}) collective-permute-start(bf16[768,768]{0,1:T(8,128)(2,1)S(1)} %bitcast.48), channel_id=1, source_target_pairs={{0,0},{1,1},{2,2},{3,3},{4,36},{5,37},{6,38},{7,39},{8,72},{9,73},... | collective-permute-start | bytes 3538952 | tf_op jit(solution)/shard_map/ppermute | solution.py:51
  39.4 27.0 %collective-permute-start.1 = (bf16[768,768]{0,1:T(8,128)(2,1)S(1)}, bf16[768,768]{0,1:T(8,128)(2,1)S(1)}, u32[]{:S(2)}, u32[]{:S(2)}) collective-permute-start(bf16[768,768]{0,1:T(8,128)(2,1)S(1)} %collective-permute-done), channel_id=1, source_target_pairs={{0,2},{1,3},{2,0},{3,1},{4,6},{5,7},{6,4},{7,5},{8,10},{9,11},{10,... | collective-permute-start | bytes 3538952 | tf_op jit(solution)/shard_map/ppermute | solution.py:52
  66.4 1.7 copy-start.3
  68.1 10.5 %collective-permute-start.2 = (bf16[2,768,768]{1,2,0:T(8,128)(2,1)}, bf16[2,768,768]{1,2,0:T(8,128)(2,1)}, u32[]{:S(2)}, u32[]{:S(2)}) collective-permute-start(bf16[2,768,768]{1,2,0:T(8,128)(2,1)} %get-tuple-element.21), channel_id=1, source_target_pairs={{0,1},{1,0},{2,3},{3,2},{4,5},{5,4},{6,7},{7,6},{8,9},{9,8},{10,11... | collective-permute-start | bytes 7077896 | tf_op jit(solution)/shard_map/ppermute | solution.py:54
  83.0 6.8 %copy-start = (bf16[768,768]{1,0:T(8,128)(2,1)S(1)}, bf16[768,768]{1,0:T(8,128)(2,1)}, u32[]{:S(2)}) copy-start(bf16[768,768]{1,0:T(8,128)(2,1)} %get-tuple-element.13) | copy-start | bytes 3538948
  83.0 6.8 %copy-start.1 = (bf16[768,768]{1,0:T(8,128)(2,1)S(1)}, bf16[768,768]{1,0:T(8,128)(2,1)}, u32[]{:S(2)}) copy-start(bf16[768,768]{1,0:T(8,128)(2,1)} %get-tuple-element.14) | copy-start | bytes 3538948
  97.7 338.5 %all-reduce.5.cloned.1.call-start = ((), (), s32[]{:S(2)}) async-start(), calls=%async_computation.1 | async-start | bytes 1572864 | tf_op jit(solution)/shard_map/psum | solution.py:105
  221.4 25.4 %collective-permute-start.3 = (bf16[768,768]{1,0:T(8,128)(2,1)S(1)}, bf16[768,768]{1,0:T(8,128)(2,1)S(1)}, u32[]{:S(2)}, u32[]{:S(2)}) collective-permute-start(bf16[768,768]{1,0:T(8,128)(2,1)S(1)} %get-tuple-element.18), channel_id=1, source_target_pairs={{0,0},{1,1},{2,2},{3,3},{4,36},{5,37},{6,38},{7,39},{8,72},{9,73},... | collective-permute-start | bytes 3538952 | tf_op jit(solution)/shard_map/ppermute | solution.py:51
  246.8 22.7 %collective-permute-start.4 = (bf16[768,768]{1,0:T(8,128)(2,1)S(1)}, bf16[768,768]{1,0:T(8,128)(2,1)S(1)}, u32[]{:S(2)}, u32[]{:S(2)}) collective-permute-start(bf16[768,768]{1,0:T(8,128)(2,1)S(1)} %collective-permute-done.3), channel_id=1, source_target_pairs={{0,2},{1,3},{2,0},{3,1},{4,6},{5,7},{6,4},{7,5},{8,10},{9,11},{10,... | collective-permute-start | bytes 3538952 | tf_op jit(solution)/shard_map/ppermute | solution.py:52
  271.3 26.9 %collective-permute-start.5 = (bf16[2,768,768]{2,1,0:T(8,128)(2,1)}, bf16[2,768,768]{2,1,0:T(8,128)(2,1)}, u32[]{:S(2)}, u32[]{:S(2)}) collective-permute-start(bf16[2,768,768]{2,1,0:T(8,128)(2,1)} %get-tuple-element.17), channel_id=1, source_target_pairs={{0,1},{1,0},{2,3},{3,2},{4,5},{5,4},{6,7},{7,6},{8,9},{9,8},{10,11... | collective-permute-start | bytes 7077896 | tf_op jit(solution)/shard_map/ppermute | solution.py:54
  341.6 94.7 %copy-start.2 = (f32[3,256,256]{2,1,0:T(8,128)S(1)}, f32[3,256,256]{2,1,0:T(8,128)}, u32[]{:S(2)}) copy-start(f32[3,256,256]{2,1,0:T(8,128)} %param.9) | copy-start | bytes 2359300
Sparse Core Ops, SparseCore 0:
  97.9 119.3 all-reduce.2
  320.5 115.7 all-reduce.4

commit v5 on v3

--- a/solution.py
+++ b/solution.py
@@ -59,6 +59,24 @@
     return quad.reshape((4,) + block.shape)
 
 
+def row_sum(x):
+    n = lax.axis_size("prow")
+    q = lax.axis_index("prow")
+    bits = [1 << b for b in range(n.bit_length() - 1)][::-1]
+    seg = x
+    for m in bits:
+        half = seg.shape[0] // 2
+        upper = (q // m) % 2 == 1
+        keep = jnp.where(upper, seg[half:], seg[:half])
+        send = jnp.where(upper, seg[:half], seg[half:])
+        seg = keep + lax.ppermute(send, "prow", [(i, i ^ m) for i in range(n)])
+    for m in bits[::-1]:
+        upper = (q // m) % 2 == 1
+        got = lax.ppermute(seg, "prow", [(i, i ^ m) for i in range(n)])
+        seg = jnp.where(upper, jnp.concatenate([got, seg]), jnp.concatenate([seg, got]))
+    return seg
+
+
 def shards(ancestor_inv, tile_pattern, factor_block, row_blocks, diag_base):
     col_rows = ancestor_inv.shape[0]
     n_row = lax.axis_size("prow")
@@ -87,7 +105,8 @@
     contrib = jnp.einsum(
         "rsjk,rsjl->skl", lower_cols, column_cols, preferred_element_type=jnp.float32
     )
-    diagonal = diag_base - lax.psum(contrib, "prow")
+    flat = contrib.reshape(supers * kwidth, kwidth)
+    diagonal = diag_base - row_sum(flat).reshape(supers, kwidth, kwidth)
     return (column, row_out, diagonal)
 
 

time: 422 us -> 393 us (0.931)
  waiting for transfers between devices: 323 us -> 245 us
  starting transfers between devices: 8.19 us -> 52 us
    psum x1 -> x0, waiting for transfers between devices: 103 us -> none  [shards(): diagonal = diag_base - lax.psum(contrib, 'prow')]
    ppermute x0 -> x6, starting transfers between devices: none -> 44.1 us  [the longest x3 37 us: row_sum(): seg = keep + lax.ppermute(send, 'prow', [(i, i ^ m) for i in range(n)])]
    ppermute x0 -> x6, waiting for transfers between devices: none -> 24.3 us  [the longest x3 18.1 us: row_sum(): seg = keep + lax.ppermute(send, 'prow', [(i, i ^ m) for i in range(n)])]
  transfers between devices with their start and end apart: 8 -> 13, of which waited for: 7 -> 11; matrix products, arithmetic and copies ran while one was open for 7% -> 8% of each run, Pallas kernels for 0% -> 0%
where the time goes in v5:
time: 393 us; the launch traced here: 389 us
  waiting for transfers between devices  245 us (62%)
  starting transfers between devices  52 us (13%)
  local copies, waits for them, and re-layouts  38.3 us (10%)
  other arithmetic  24.8 us (6%)
  matrix products  14.5 us (4%)
  between operations  14.2 us (4%)
    psum x1, waiting for transfers between devices, shards(): summed = lax.psum(partial, 'prow')  120 us
    ppermute x2, waiting for transfers between devices, gather_cols(): mine = lax.ppermute(block, ALL, swap)  50.7 us
    ppermute x2, waiting for transfers between devices, gather_cols(): other = lax.ppermute(mine, ALL, far)  46.2 us
    ppermute x3, starting transfers between devices, row_sum(): seg = keep + lax.ppermute(send, 'prow', [(i, i ^ m) for i in range(n)])  37 us
    ppermute x3, waiting for transfers between devices, row_sum(): seg = keep + lax.ppermute(send, 'prow', [(i, i ^ m) for i in range(n)])  18.1 us
    select_n x2, local copies, waits for them, and re-layouts, gather_cols(): jnp.where(low == 0, jnp.stack([pair, twin], 1), jnp.stack([twin, pair], 1))  13.3 us
    select_n x2, other arithmetic, gather_cols(): jnp.where(low == 0, jnp.stack([pair, twin], 1), jnp.stack([twin, pair], 1))  11.2 us
    reshape x1, local copies, waits for them, and re-layouts, shards(): tiles4 = inverse_tiles.reshape(col_rows, n_sub, col_rows)  9.77 us
  transfers between devices with their start and end apart: 13, of which 11 were waited for; matrix products, arithmetic and copies ran while one was open for 8% of the time, Pallas kernels for 0%

profile of v5, /device:TPU:4, one launch (start us, length us, event | category | flops | bytes accessed | tf_op | source)
XLA Modules:
  0.0 389.0 jit_solution(4706856777314249166)
XLA Ops:
  7.2 0.0 all-reduce.2.cloned.1.call-start
  7.2 0.9 compare_reduce_fusion
  8.1 1.6 copy.35
  9.7 0.1 broadcast_multiply_fusion
  9.8 2.4 collective-permute-start
  12.2 27.2 %collective-permute-done = bf16[3,768,256]{1,2,0:T(8,128)(2,1)S(1)} collective-permute-done((bf16[3,768,256]{1,2,0:T(8,128)(2,1)S(1)}, bf16[3,768,256]{1,2,0:T(8,128)(2,1)S(1)}, u32[]{:S(2)}, u32[]{:S(2)}) %collective-permute-start) | collective-permute-done | bytes 1179680 | tf_op jit(solution)/shard_map/ppermute | solution.py:54
  39.4 1.9 collective-permute-start.1
  41.3 25.1 %collective-permute-done.1 = bf16[3,768,256]{1,2,0:T(8,128)(2,1)S(1)} collective-permute-done((bf16[3,768,256]{1,2,0:T(8,128)(2,1)S(1)}, bf16[3,768,256]{1,2,0:T(8,128)(2,1)S(1)}, u32[]{:S(2)}, u32[]{:S(2)}) %collective-permute-start.1) | collective-permute-done | bytes 1179680 | tf_op jit(solution)/shard_map/ppermute | solution.py:55
  66.4 0.0 copy-start.1
  66.4 1.8 maximum_select_fusion.2
  68.2 0.0 collective-permute-start.2
  68.2 0.0 copy-done.1
  68.2 0.7 broadcast_in_dim.2
  68.9 5.1 %bitcast_multiply_fusion = bf16[768,3072]{1,0:T(8,128)(2,1)} fusion(bf16[768,3072]{1,0:T(8,128)(2,1)} %param.5, bf16[96,8,24,128]{3,2,1,0:T(8,128)(2,1)S(1)} %bitcast.39), kind=kLoop, calls=%fused_computation | loop fusion | flops 2359296 | bytes 14155776 | tf_op jit(solution)/shard_map/mul | solution.py:92
  74.0 9.8 %reshape.180 = bf16[768,4,768]{2,1,0:T(4,128)(2,1)} reshape(bf16[768,3072]{1,0:T(8,128)(2,1)} %bitcast_multiply_fusion) | data formatting | bytes 9437184 | tf_op jit(solution)/shard_map/reshape | solution.py:96
  83.8 0.4 fusion.2
  84.2 0.0 collective-permute-done.2
  84.2 5.6 %maximum_select_fusion = bf16[2,2,3,768,256]{3,4,2,0,1:T(8,128)(2,1)} fusion(bf16[2,1,3,768,256]{3,4,2,0,1:T(8,128)(2,1)} %bitcast.6, bf16[2,1,3,768,256]{3,4,2,0,1:T(8,128)(2,1)S(1)} %fusion.2, pred[]{:T(512)S(6)} %eq.42), kind=kLoop, calls=%fused_computation.1 | loop fusion | flops 7077888 | bytes 9437185 | tf_op jit(solution)/shard_map/jit(_where)/select_n | solution.py:58
  89.8 6.7 %copy.38 = bf16[2,2,3,768,256]{4,3,2,1,0:T(8,128)(2,1)} copy(bf16[2,2,3,768,256]{3,4,2,0,1:T(8,128)(2,1)} %maximum_select_fusion) | data formatting | bytes 9437184 | tf_op jit(solution)/shard_map/jit(_where)/select_n | solution.py:58
  96.5 9.0 %fusion.3 = f32[3,768,256]{1,2,0:T(8,128)} fusion(bf16[4,3,768,256]{3,2,1,0:T(8,128)(2,1)} %bitcast.51, bf16[768,4,768,1]{2,1,0,3:T(4,128)(2,1)} %bitcast.53), kind=kOutput, calls=%fused_computation.12 | convolution fusion | flops 3623878656 | bytes 11796480 | tf_op jit(solution)/shard_map/irj,rsjk->sik/dot_general | solution.py:97
  105.5 0.0 all-reduce.2.cloned.1.call-update
  105.5 119.5 %all-reduce.2.cloned.1.call-done = f32[3,768,256]{1,2,0:T(8,128)} async-done(((f32[3,768,256]{1,2,0:T(8,128)}), f32[3,768,256]{1,2,0:T(8,128)}) %all-reduce.2.cloned.1.call-update) | async-done | bytes 2359312 | tf_op jit(solution)/shard_map/psum | solution.py:100
  225.0 1.9 multiply_convert_fusion
  226.9 1.9 collective-permute-start.3
  228.8 23.5 %collective-permute-done.3 = bf16[3,768,256]{1,2,0:T(8,128)(2,1)S(1)} collective-permute-done((bf16[3,768,256]{1,2,0:T(8,128)(2,1)S(1)}, bf16[3,768,256]{1,2,0:T(8,128)(2,1)S(1)}, u32[]{:S(2)}, u32[]{:S(2)}) %collective-permute-start.3) | collective-permute-done | bytes 1179680 | tf_op jit(solution)/shard_map/ppermute | solution.py:54
  252.3 1.6 collective-permute-start.4
  253.9 21.1 %collective-permute-done.4 = bf16[3,768,256]{1,2,0:T(8,128)(2,1)S(1)} collective-permute-done((bf16[3,768,256]{1,2,0:T(8,128)(2,1)S(1)}, bf16[3,768,256]{1,2,0:T(8,128)(2,1)S(1)}, u32[]{:S(2)}, u32[]{:S(2)}) %collective-permute-start.4) | collective-permute-done | bytes 1179680 | tf_op jit(solution)/shard_map/ppermute | solution.py:55
  275.0 1.8 maximum_select_fusion.4
  276.8 0.0 collective-permute-start.5
  276.8 0.4 maximum_select_fusion.3
  277.2 4.5 %collective-permute-done.5 = bf16[2,3,768,256]{2,3,1,0:T(8,128)(2,1)} collective-permute-done((bf16[2,3,768,256]{2,3,1,0:T(8,128)(2,1)}, bf16[2,3,768,256]{2,3,1,0:T(8,128)(2,1)}, u32[]{:S(2)}, u32[]{:S(2)}) %collective-permute-start.5) | collective-permute-done | bytes 2359328 | tf_op jit(solution)/shard_map/ppermute | solution.py:57
  281.7 5.6 %maximum_select_fusion.1 = bf16[2,2,3,768,256]{3,4,2,0,1:T(8,128)(2,1)} fusion(bf16[2,1,3,768,256]{3,4,2,0,1:T(8,128)(2,1)} %bitcast.15, bf16[2,1,3,768,256]{3,4,2,0,1:T(8,128)(2,1)S(1)} %maximum_select_fusion.3, pred[]{:T(512)S(6)} %eq.42), kind=kLoop, calls=%fused_computation.2 | loop fusion | flops 7077888 | bytes 9437185 | tf_op jit(solution)/shard_map/jit(_where)/select_n | solution.py:58
  287.3 6.7 %copy.41 = bf16[2,2,3,768,256]{4,3,2,1,0:T(8,128)(2,1)} copy(bf16[2,2,3,768,256]{3,4,2,0,1:T(8,128)(2,1)} %maximum_select_fusion.1) | data formatting | bytes 9437184 | tf_op jit(solution)/shard_map/jit(_where)/select_n | solution.py:58
  293.9 5.5 %fusion.10 = f32[3,256,256,1]{2,1,0,3:T(8,128)S(1)} fusion(bf16[4,3,768,256]{3,2,1,0:T(8,128)(2,1)} %bitcast.52, bf16[4,3,768,256]{3,2,1,0:T(8,128)(2,1)} %bitcast.40), kind=kOutput, calls=%fused_computation.35 | convolution fusion | flops 1207959552 | bytes 10223616 | tf_op jit(solution)/shard_map/rsjk,rsjl->skl/dot_general | solution.py:105
  299.5 0.1 slice_select_fusion
  299.5 0.1 collective-permute-start.6
  299.7 11.1 %collective-permute-done.6 = f32[384,256]{1,0:T(8,128)S(1)} collective-permute-done((f32[384,256]{1,0:T(8,128)S(1)}, f32[384,256]{1,0:T(8,128)S(1)}, u32[]{:S(2)}, u32[]{:S(2)}) %collective-permute-start.6) | collective-permute-done | bytes 393248 | tf_op jit(solution)/shard_map/ppermute | solution.py:72
  310.8 0.1 select_add_fusion
  310.9 34.2 %collective-permute-start.7 = (f32[192,256]{1,0:T(8,128)S(1)}, f32[192,256]{1,0:T(8,128)S(1)}, u32[]{:S(2)}, u32[]{:S(2)}) collective-permute-start(f32[192,256]{1,0:T(8,128)S(1)} %slice_select_fusion.1), channel_id=1, source_target_pairs={{0,64},{32,96},{64,0},{96,32},{128,192},{160,224},{192,128},{224,1... | collective-permute-start | bytes 589832 | tf_op jit(solution)/shard_map/ppermute | solution.py:72
  345.1 4.3 %collective-permute-done.7 = f32[192,256]{1,0:T(8,128)S(1)} collective-permute-done((f32[192,256]{1,0:T(8,128)S(1)}, f32[192,256]{1,0:T(8,128)S(1)}, u32[]{:S(2)}, u32[]{:S(2)}) %collective-permute-start.7) | collective-permute-done | bytes 196640 | tf_op jit(solution)/shard_map/ppermute | solution.py:72
  349.5 2.6 collective-permute-start.8
  352.1 2.6 collective-permute-done.8
  354.8 2.1 collective-permute-start.9
  356.9 2.6 collective-permute-done.9
  359.5 4.6 %collective-permute-start.10 = (f32[192,256]{1,0:T(8,128)S(1)}, f32[192,256]{1,0:T(8,128)S(1)}, u32[]{:S(2)}, u32[]{:S(2)}) collective-permute-start(f32[192,256]{1,0:T(8,128)S(1)} %maximum_select_fusion.7), channel_id=1, source_target_pairs={{0,64},{32,96},{64,0},{96,32},{128,192},{160,224},{192,128},{224,1... | collective-permute-start | bytes 589832 | tf_op jit(solution)/shard_map/ppermute | solution.py:75
  364.1 3.6 collective-permute-done.10
  367.8 0.4 collective-permute-start.11
  368.2 1.4 copy.44
  369.7 4.8 %copy.42 = bf16[3,256,4,768]{1,3,2,0:T(8,128)(2,1)} copy(bf16[3,256,4,768]{1,3,0,2:T(8,128)(2,1)} %bitcast.41) | data formatting | bytes 9437184 | tf_op jit(solution)/shard_map/transpose | solution.py:104
  374.4 0.0 copy-start
  374.4 6.7 %copy.45 = bf16[3,256,3072]{2,1,0:T(8,128)(2,1)} copy(bf16[3,256,3072]{1,2,0:T(8,128)(2,1)} %bitcast.42) | data formatting | bytes 9437184
  381.1 0.0 collective-permute-done.11
  381.1 0.1 maximum_select_fusion.5
  381.2 0.0 copy-done
  381.2 1.0 sub.28
  (9 shorter events, 0.2 us)
Async XLA Ops:
  7.2 217.9 %all-reduce.2.cloned.1.call-start = ((), (), s32[]{:S(2)}) async-start(), calls=%async_computation | async-start | bytes 4718592 | tf_op jit(solution)/shard_map/psum | solution.py:100
  9.8 29.6 %collective-permute-start = (bf16[3,768,256]{1,2,0:T(8,128)(2,1)S(1)}, bf16[3,768,256]{1,2,0:T(8,128)(2,1)S(1)}, u32[]{:S(2)}, u32[]{:S(2)}) collective-permute-start(bf16[3,768,256]{1,2,0:T(8,128)(2,1)S(1)} %broadcast_multiply_fusion), channel_id=1, source_target_pairs={{0,0},{1,1},{2,2},{3,3},{4,36},{5,37},{6,38},{7,39},{8,72},{9,73},... | collective-permute-start | bytes 3538952 | tf_op jit(solution)/shard_map/ppermute | solution.py:54
  39.4 27.0 %collective-permute-start.1 = (bf16[3,768,256]{1,2,0:T(8,128)(2,1)S(1)}, bf16[3,768,256]{1,2,0:T(8,128)(2,1)S(1)}, u32[]{:S(2)}, u32[]{:S(2)}) collective-permute-start(bf16[3,768,256]{1,2,0:T(8,128)(2,1)S(1)} %collective-permute-done), channel_id=1, source_target_pairs={{0,2},{1,3},{2,0},{3,1},{4,6},{5,7},{6,4},{7,5},{8,10},{9,11},{10,... | collective-permute-start | bytes 3538952 | tf_op jit(solution)/shard_map/ppermute | solution.py:55
  66.4 1.8 copy-start.1
  68.2 16.0 %collective-permute-start.2 = (bf16[2,3,768,256]{2,3,1,0:T(8,128)(2,1)}, bf16[2,3,768,256]{2,3,1,0:T(8,128)(2,1)}, u32[]{:S(2)}, u32[]{:S(2)}) collective-permute-start(bf16[2,3,768,256]{2,3,1,0:T(8,128)(2,1)} %maximum_select_fusion.2), channel_id=1, source_target_pairs={{0,1},{1,0},{2,3},{3,2},{4,5},{5,4},{6,7},{7,6},{8,9},{9,8},{10,11... | collective-permute-start | bytes 7077896 | tf_op jit(solution)/shard_map/ppermute | solution.py:57
  226.9 25.4 %collective-permute-start.3 = (bf16[3,768,256]{1,2,0:T(8,128)(2,1)S(1)}, bf16[3,768,256]{1,2,0:T(8,128)(2,1)S(1)}, u32[]{:S(2)}, u32[]{:S(2)}) collective-permute-start(bf16[3,768,256]{1,2,0:T(8,128)(2,1)S(1)} %multiply_convert_fusion), channel_id=1, source_target_pairs={{0,0},{1,1},{2,2},{3,3},{4,36},{5,37},{6,38},{7,39},{8,72},{9,73},... | collective-permute-start | bytes 3538952 | tf_op jit(solution)/shard_map/ppermute | solution.py:54
  252.3 22.7 %collective-permute-start.4 = (bf16[3,768,256]{1,2,0:T(8,128)(2,1)S(1)}, bf16[3,768,256]{1,2,0:T(8,128)(2,1)S(1)}, u32[]{:S(2)}, u32[]{:S(2)}) collective-permute-start(bf16[3,768,256]{1,2,0:T(8,128)(2,1)S(1)} %collective-permute-done.3), channel_id=1, source_target_pairs={{0,2},{1,3},{2,0},{3,1},{4,6},{5,7},{6,4},{7,5},{8,10},{9,11},{10,... | collective-permute-start | bytes 3538952 | tf_op jit(solution)/shard_map/ppermute | solution.py:55
  276.8 4.9 %collective-permute-start.5 = (bf16[2,3,768,256]{2,3,1,0:T(8,128)(2,1)}, bf16[2,3,768,256]{2,3,1,0:T(8,128)(2,1)}, u32[]{:S(2)}, u32[]{:S(2)}) collective-permute-start(bf16[2,3,768,256]{2,3,1,0:T(8,128)(2,1)} %maximum_select_fusion.4), channel_id=1, source_target_pairs={{0,1},{1,0},{2,3},{3,2},{4,5},{5,4},{6,7},{7,6},{8,9},{9,8},{10,11... | collective-permute-start | bytes 7077896 | tf_op jit(solution)/shard_map/ppermute | solution.py:57
  299.5 11.2 %collective-permute-start.6 = (f32[384,256]{1,0:T(8,128)S(1)}, f32[384,256]{1,0:T(8,128)S(1)}, u32[]{:S(2)}, u32[]{:S(2)}) collective-permute-start(f32[384,256]{1,0:T(8,128)S(1)} %slice_select_fusion), channel_id=1, source_target_pairs={{0,128},{32,160},{64,192},{96,224},{128,0},{160,32},{192,64},{224,... | collective-permute-start | bytes 1179656 | tf_op jit(solution)/shard_map/ppermute | solution.py:72
  310.9 38.6 %collective-permute-start.7 = (f32[192,256]{1,0:T(8,128)S(1)}, f32[192,256]{1,0:T(8,128)S(1)}, u32[]{:S(2)}, u32[]{:S(2)}) collective-permute-start(f32[192,256]{1,0:T(8,128)S(1)} %slice_select_fusion.1), channel_id=1, source_target_pairs={{0,64},{32,96},{64,0},{96,32},{128,192},{160,224},{192,128},{224,1... | collective-permute-start | bytes 589832 | tf_op jit(solution)/shard_map/ppermute | solution.py:72
  349.5 5.2 %collective-permute-start.8 = (f32[96,256]{1,0:T(8,128)S(1)}, f32[96,256]{1,0:T(8,128)S(1)}, u32[]{:S(2)}, u32[]{:S(2)}) collective-permute-start(f32[96,256]{1,0:T(8,128)S(1)} %slice_select_fusion.2), channel_id=1, source_target_pairs={{0,32},{32,0},{64,96},{96,64},{128,160},{160,128},{192,224},{224,1... | collective-permute-start | bytes 294920 | tf_op jit(solution)/shard_map/ppermute | solution.py:72
  354.8 4.7 %collective-permute-start.9 = (f32[96,256]{1,0:T(8,128)S(1)}, f32[96,256]{1,0:T(8,128)S(1)}, u32[]{:S(2)}, u32[]{:S(2)}) collective-permute-start(f32[96,256]{1,0:T(8,128)S(1)} %select_add_fusion.2), channel_id=1, source_target_pairs={{0,32},{32,0},{64,96},{96,64},{128,160},{160,128},{192,224},{224,1... | collective-permute-start | bytes 294920 | tf_op jit(solution)/shard_map/ppermute | solution.py:75
  359.5 8.3 %collective-permute-start.10 = (f32[192,256]{1,0:T(8,128)S(1)}, f32[192,256]{1,0:T(8,128)S(1)}, u32[]{:S(2)}, u32[]{:S(2)}) collective-permute-start(f32[192,256]{1,0:T(8,128)S(1)} %maximum_select_fusion.7), channel_id=1, source_target_pairs={{0,64},{32,96},{64,0},{96,32},{128,192},{160,224},{192,128},{224,1... | collective-permute-start | bytes 589832 | tf_op jit(solution)/shard_map/ppermute | solution.py:75
  367.8 13.3 %collective-permute-start.11 = (f32[384,256]{1,0:T(8,128)S(1)}, f32[384,256]{1,0:T(8,128)S(1)}, u32[]{:S(2)}, u32[]{:S(2)}) collective-permute-start(f32[384,256]{1,0:T(8,128)S(1)} %maximum_select_fusion.6), channel_id=1, source_target_pairs={{0,128},{32,160},{64,192},{96,224},{128,0},{160,32},{192,64},{224,... | collective-permute-start | bytes 1179656 | tf_op jit(solution)/shard_map/ppermute | solution.py:75
  374.4 6.8 %copy-start = (f32[3,256,256]{2,1,0:T(8,128)S(1)}, f32[3,256,256]{2,1,0:T(8,128)}, u32[]{:S(2)}) copy-start(f32[3,256,256]{2,1,0:T(8,128)} %param.9) | copy-start | bytes 2359300
Sparse Core Ops, SparseCore 0:
  105.6 119.3 all-reduce.1

commit v6 on v5

--- a/solution.py
+++ b/solution.py
@@ -59,10 +59,10 @@
     return quad.reshape((4,) + block.shape)
 
 
-def row_sum(x):
+def row_sum(x, order=None, between=None):
     n = lax.axis_size("prow")
     q = lax.axis_index("prow")
-    bits = [1 << b for b in range(n.bit_length() - 1)][::-1]
+    bits = order or [1 << b for b in range(n.bit_length() - 1)][::-1]
     seg = x
     for m in bits:
         half = seg.shape[0] // 2
@@ -70,6 +70,8 @@
         keep = jnp.where(upper, seg[half:], seg[:half])
         send = jnp.where(upper, seg[:half], seg[half:])
         seg = keep + lax.ppermute(send, "prow", [(i, i ^ m) for i in range(n)])
+    if between is not None:
+        seg = between(seg)
     for m in bits[::-1]:
         upper = (q // m) % 2 == 1
         got = lax.ppermute(seg, "prow", [(i, i ^ m) for i in range(n)])
@@ -97,9 +99,12 @@
     partial = jnp.einsum(
         "irj,rsjk->sik", tiles4, lower_cols, preferred_element_type=jnp.float32
     )
-    summed = lax.psum(partial, "prow")
-    col_exact = -summed * own_sel[:, :, None]
-    column = col_exact.astype(jnp.bfloat16)
+    n_row_bits = [1 << b for b in range(n_row.bit_length() - 1)]
+    order = n_row_bits[-1:] + n_row_bits[:-1] if len(n_row_bits) == 3 else None
+    summed = row_sum(
+        partial.reshape(supers * col_rows, kwidth), order, lambda seg: seg.astype(jnp.bfloat16)
+    ).reshape(supers, col_rows, kwidth)
+    column = -summed * own_sel[:, :, None].astype(jnp.bfloat16)
     column_cols = gather_cols(column, perm)
     row_out = jnp.transpose(column_cols, (1, 3, 0, 2)).reshape(supers, kwidth, n_sub * col_rows)
     contrib = jnp.einsum(

time: 393 us -> 343 us (0.87)
  waiting for transfers between devices: 245 us -> 193 us
  starting transfers between devices: 52 us -> 94.6 us
  between operations: 14.2 us -> 0.97 us
  local copies, waits for them, and re-layouts: 38.3 us -> 27.2 us
  other arithmetic: 24.8 us -> 16.6 us
  matrix products: 14.5 us -> 7.14 us
    psum x1 -> x0, waiting for transfers between devices: 120 us -> none  [shards(): summed = lax.psum(partial, 'prow')]
    ppermute x3 -> x6, waiting for transfers between devices: 18.1 us -> 65.9 us  [row_sum(): seg = keep + lax.ppermute(send, 'prow', [(i, i ^ m) for i in range(n)])]
    ppermute x3 -> x6, starting transfers between devices: 37 us -> 74.6 us  [row_sum(): seg = keep + lax.ppermute(send, 'prow', [(i, i ^ m) for i in range(n)])]
    ppermute x3 -> x6, waiting for transfers between devices: 6.25 us -> 27.2 us  [row_sum(): got = lax.ppermute(seg, 'prow', [(i, i ^ m) for i in range(n)])]
    select_n x2 -> x1, local copies, waits for them, and re-layouts: 13.3 us -> 0.32 us  [gather_cols(): jnp.where(low == 0, jnp.stack([pair, twin], 1), jnp.stack([twin, pair], 1))]
    select_n x2, other arithmetic: 11.2 us -> 3.89 us  [gather_cols(): jnp.where(low == 0, jnp.stack([pair, twin], 1), jnp.stack([twin, pair], 1))]
    ppermute x3 -> x6, starting transfers between devices: 7.15 us -> 11.3 us  [row_sum(): got = lax.ppermute(seg, 'prow', [(i, i ^ m) for i in range(n)])]
    unnamed x7 -> x19, local copies, waits for them, and re-layouts: 9.7 us -> 11.9 us
  transfers between devices with their start and end apart: 13 -> 18, of which waited for: 11 -> 16; matrix products, arithmetic and copies ran while one was open for 8% -> 7% of each run, Pallas kernels for 0% -> 0%
where the time goes in v6:
time: 343 us; the launch traced here: 339 us
  waiting for transfers between devices  193 us (56%)
  starting transfers between devices  94.6 us (28%)
  local copies, waits for them, and re-layouts  27.2 us (8%)
  other arithmetic  16.6 us (5%)
  matrix products  7.14 us (2%)
    ppermute x6, starting transfers between devices, row_sum(): seg = keep + lax.ppermute(send, 'prow', [(i, i ^ m) for i in range(n)])  74.6 us
    ppermute x6, waiting for transfers between devices, row_sum(): seg = keep + lax.ppermute(send, 'prow', [(i, i ^ m) for i in range(n)])  65.9 us
    ppermute x2, waiting for transfers between devices, gather_cols(): mine = lax.ppermute(block, ALL, swap)  49.8 us
    ppermute x2, waiting for transfers between devices, gather_cols(): other = lax.ppermute(mine, ALL, far)  45.9 us
    ppermute x6, waiting for transfers between devices, row_sum(): got = lax.ppermute(seg, 'prow', [(i, i ^ m) for i in range(n)])  27.2 us
    unnamed x19, local copies, waits for them, and re-layouts  11.9 us
    ppermute x6, starting transfers between devices, row_sum(): got = lax.ppermute(seg, 'prow', [(i, i ^ m) for i in range(n)])  11.3 us
    reshape x1, local copies, waits for them, and re-layouts, shards(): tiles4 = inverse_tiles.reshape(col_rows, n_sub, col_rows)  9.76 us
  transfers between devices with their start and end apart: 18, of which 16 were waited for; matrix products, arithmetic and copies ran while one was open for 7% of the time, Pallas kernels for 0%

profile of v6, /device:TPU:4, one launch (start us, length us, event | category | flops | bytes accessed | tf_op | source)
XLA Modules:
  0.0 339.4 jit_solution(4914718182795215881)
XLA Ops:
  0.7 0.9 compare_reduce_fusion
  1.5 1.6 broadcast_multiply_fusion.1
  3.2 2.4 collective-permute-start
  5.6 27.2 %collective-permute-done = bf16[3,768,256]{2,1,0:T(8,128)(2,1)S(1)} collective-permute-done((bf16[3,768,256]{2,1,0:T(8,128)(2,1)S(1)}, bf16[3,768,256]{2,1,0:T(8,128)(2,1)S(1)}, u32[]{:S(2)}, u32[]{:S(2)}) %collective-permute-start) | collective-permute-done | bytes 1179680 | tf_op jit(solution)/shard_map/ppermute | solution.py:54
  32.8 1.9 collective-permute-start.1
  34.7 25.1 %collective-permute-done.1 = bf16[3,768,256]{2,1,0:T(8,128)(2,1)S(1)} collective-permute-done((bf16[3,768,256]{2,1,0:T(8,128)(2,1)S(1)}, bf16[3,768,256]{2,1,0:T(8,128)(2,1)S(1)}, u32[]{:S(2)}, u32[]{:S(2)}) %collective-permute-start.1) | collective-permute-done | bytes 1179680 | tf_op jit(solution)/shard_map/ppermute | solution.py:55
  59.8 1.8 maximum_select_fusion.2
  61.7 0.7 broadcast_in_dim.2
  62.3 1.6 copy-done
  64.0 2.8 bitcast_multiply_fusion
  66.8 9.8 %reshape.187 = bf16[768,4,768]{2,1,0:T(4,128)(2,1)} reshape(bf16[768,3072]{1,0:T(8,128)(2,1)} %bitcast_multiply_fusion) | data formatting | bytes 9437184 | tf_op jit(solution)/shard_map/reshape | solution.py:98
  76.5 0.4 bitcast_select_fusion
  77.0 3.1 maximum_select_fusion
  80.1 2.2 copy-done.1
  82.3 5.3 %fusion.2 = f32[3,768,256]{1,2,0:T(8,128)} fusion(bf16[4,3,768,256]{3,2,1,0:T(8,128)(2,1)S(1)} %bitcast.49, bf16[768,4,768,1]{2,1,0,3:T(4,128)(2,1)S(1)} %bitcast.55), kind=kOutput, calls=%fused_computation.9 | convolution fusion | flops 3623878656 | bytes 11796480 | tf_op jit(solution)/shard_map/irj,rsjk->sik/dot_general | solution.py:99
  87.6 2.0 copy.33
  89.6 0.2 slice_select_fusion
  89.8 0.1 collective-permute-start.3
  89.9 28.5 %collective-permute-done.3 = f32[1152,256]{1,0:T(8,128)} collective-permute-done((f32[1152,256]{1,0:T(8,128)S(1)}, f32[1152,256]{1,0:T(8,128)}, u32[]{:S(2)}, u32[]{:S(2)}) %collective-permute-start.3) | collective-permute-done | bytes 1179680 | tf_op jit(solution)/shard_map/ppermute | solution.py:72
  118.4 1.5 select_add_fusion
  119.9 0.1 slice_select_fusion.1
  120.0 31.0 %collective-permute-start.4 = (f32[576,256]{1,0:T(8,128)S(1)}, f32[576,256]{1,0:T(8,128)S(1)}, u32[]{:S(2)}, u32[]{:S(2)}) collective-permute-start(f32[576,256]{1,0:T(8,128)S(1)} %slice_select_fusion.1), channel_id=1, source_target_pairs={{0,32},{32,0},{64,96},{96,64},{128,160},{160,128},{192,224},{224,1... | collective-permute-start | bytes 1769480 | tf_op jit(solution)/shard_map/ppermute | solution.py:72
  151.0 13.1 %collective-permute-done.4 = f32[576,256]{1,0:T(8,128)S(1)} collective-permute-done((f32[576,256]{1,0:T(8,128)S(1)}, f32[576,256]{1,0:T(8,128)S(1)}, u32[]{:S(2)}, u32[]{:S(2)}) %collective-permute-start.4) | collective-permute-done | bytes 589856 | tf_op jit(solution)/shard_map/ppermute | solution.py:72
  164.1 0.1 select_add_fusion.1
  164.3 5.1 %collective-permute-start.5 = (f32[288,256]{1,0:T(8,128)S(1)}, f32[288,256]{1,0:T(8,128)S(1)}, u32[]{:S(2)}, u32[]{:S(2)}) collective-permute-start(f32[288,256]{1,0:T(8,128)S(1)} %slice_select_fusion.3), channel_id=1, source_target_pairs={{0,64},{32,96},{64,0},{96,32},{128,192},{160,224},{192,128},{224,1... | collective-permute-start | bytes 884744 | tf_op jit(solution)/shard_map/ppermute | solution.py:72
  169.4 6.2 %collective-permute-done.5 = f32[288,256]{1,0:T(8,128)S(1)} collective-permute-done((f32[288,256]{1,0:T(8,128)S(1)}, f32[288,256]{1,0:T(8,128)S(1)}, u32[]{:S(2)}, u32[]{:S(2)}) %collective-permute-start.5) | collective-permute-done | bytes 294944 | tf_op jit(solution)/shard_map/ppermute | solution.py:72
  175.7 3.3 collective-permute-start.6
  179.0 3.7 %collective-permute-done.6 = bf16[288,256]{1,0:T(8,128)(2,1)S(1)} collective-permute-done((bf16[288,256]{1,0:T(8,128)(2,1)S(1)}, bf16[288,256]{1,0:T(8,128)(2,1)S(1)}, u32[]{:S(2)}, u32[]{:S(2)}) %collective-permute-start.6) | collective-permute-done | bytes 147488 | tf_op jit(solution)/shard_map/ppermute | solution.py:77
  182.7 0.1 maximum_select_fusion.9
  182.8 0.7 collective-permute-start.7
  183.5 6.1 %collective-permute-done.7 = bf16[576,256]{1,0:T(8,128)(2,1)S(1)} collective-permute-done((bf16[576,256]{1,0:T(8,128)(2,1)S(1)}, bf16[576,256]{1,0:T(8,128)(2,1)S(1)}, u32[]{:S(2)}, u32[]{:S(2)}) %collective-permute-start.7) | collective-permute-done | bytes 294944 | tf_op jit(solution)/shard_map/ppermute | solution.py:77
  189.6 0.3 maximum_select_fusion.7
  189.9 0.6 collective-permute-start.8
  190.4 11.1 %collective-permute-done.8 = bf16[1152,256]{1,0:T(8,128)(2,1)S(1)} collective-permute-done((bf16[1152,256]{1,0:T(8,128)(2,1)S(1)}, bf16[1152,256]{1,0:T(8,128)(2,1)S(1)}, u32[]{:S(2)}, u32[]{:S(2)}) %collective-permute-start.8) | collective-permute-done | bytes 589856 | tf_op jit(solution)/shard_map/ppermute | solution.py:77
  201.5 0.4 fusion.5
  202.0 0.4 broadcast_multiply_fusion
  202.4 2.6 collective-permute-start.9
  205.0 22.7 %collective-permute-done.9 = bf16[3,768,256]{2,1,0:T(8,128)(2,1)S(1)} collective-permute-done((bf16[3,768,256]{2,1,0:T(8,128)(2,1)S(1)}, bf16[3,768,256]{2,1,0:T(8,128)(2,1)S(1)}, u32[]{:S(2)}, u32[]{:S(2)}) %collective-permute-start.9) | collective-permute-done | bytes 1179680 | tf_op jit(solution)/shard_map/ppermute | solution.py:54
  227.6 1.7 collective-permute-start.10
  229.3 20.8 %collective-permute-done.10 = bf16[3,768,256]{2,1,0:T(8,128)(2,1)S(1)} collective-permute-done((bf16[3,768,256]{2,1,0:T(8,128)(2,1)S(1)}, bf16[3,768,256]{2,1,0:T(8,128)(2,1)S(1)}, u32[]{:S(2)}, u32[]{:S(2)}) %collective-permute-start.10) | collective-permute-done | bytes 1179680 | tf_op jit(solution)/shard_map/ppermute | solution.py:55
  250.1 0.4 maximum_select_fusion.4
  250.5 0.1 collective-permute-start.11
  250.6 0.4 maximum_select_fusion.3
  251.0 4.1 %collective-permute-done.11 = bf16[2,3,768,256]{3,2,1,0:T(8,128)(2,1)S(1)} collective-permute-done((bf16[2,3,768,256]{3,2,1,0:T(8,128)(2,1)S(1)}, bf16[2,3,768,256]{3,2,1,0:T(8,128)(2,1)S(1)}, u32[]{:S(2)}, u32[]{:S(2)}) %collective-permute-start.11) | collective-permute-done | bytes 2359328 | tf_op jit(solution)/shard_map/ppermute | solution.py:57
  255.2 0.7 maximum_select_fusion.1
  255.9 0.3 copy.34
  256.3 1.1 slice-done
  257.3 0.3 slice-done.1
  257.6 1.8 fusion.9
  259.5 0.1 collective-permute-start.12
  259.6 11.1 %collective-permute-done.12 = f32[384,256]{1,0:T(8,128)S(1)} collective-permute-done((f32[384,256]{1,0:T(8,128)S(1)}, f32[384,256]{1,0:T(8,128)S(1)}, u32[]{:S(2)}, u32[]{:S(2)}) %collective-permute-start.12) | collective-permute-done | bytes 393248 | tf_op jit(solution)/shard_map/ppermute | solution.py:72
  270.8 0.1 select_add_fusion.2
  270.9 33.9 %collective-permute-start.13 = (f32[192,256]{1,0:T(8,128)S(1)}, f32[192,256]{1,0:T(8,128)S(1)}, u32[]{:S(2)}, u32[]{:S(2)}) collective-permute-start(f32[192,256]{1,0:T(8,128)S(1)} %slice_select_fusion.4), channel_id=1, source_target_pairs={{0,64},{32,96},{64,0},{96,32},{128,192},{160,224},{192,128},{224,1... | collective-permute-start | bytes 589832 | tf_op jit(solution)/shard_map/ppermute | solution.py:72
  304.8 4.3 %collective-permute-done.13 = f32[192,256]{1,0:T(8,128)S(1)} collective-permute-done((f32[192,256]{1,0:T(8,128)S(1)}, f32[192,256]{1,0:T(8,128)S(1)}, u32[]{:S(2)}, u32[]{:S(2)}) %collective-permute-start.13) | collective-permute-done | bytes 196640 | tf_op jit(solution)/shard_map/ppermute | solution.py:72
  309.2 4.4 %collective-permute-start.14 = (f32[96,256]{1,0:T(8,128)S(1)}, f32[96,256]{1,0:T(8,128)S(1)}, u32[]{:S(2)}, u32[]{:S(2)}) collective-permute-start(f32[96,256]{1,0:T(8,128)S(1)} %slice_select_fusion.5), channel_id=1, source_target_pairs={{0,32},{32,0},{64,96},{96,64},{128,160},{160,128},{192,224},{224,1... | collective-permute-start | bytes 294920 | tf_op jit(solution)/shard_map/ppermute | solution.py:72
  313.6 2.6 collective-permute-done.14
  316.2 2.1 collective-permute-start.15
  318.3 2.6 collective-permute-done.15
  320.9 4.1 %collective-permute-start.16 = (f32[192,256]{1,0:T(8,128)S(1)}, f32[192,256]{1,0:T(8,128)S(1)}, u32[]{:S(2)}, u32[]{:S(2)}) collective-permute-start(f32[192,256]{1,0:T(8,128)S(1)} %maximum_select_fusion.10), channel_id=1, source_target_pairs={{0,64},{32,96},{64,0},{96,32},{128,192},{160,224},{192,128},{224,1... | collective-permute-start | bytes 589832 | tf_op jit(solution)/shard_map/ppermute | solution.py:77
  325.0 3.6 %collective-permute-done.16 = f32[192,256]{1,0:T(8,128)S(1)} collective-permute-done((f32[192,256]{1,0:T(8,128)S(1)}, f32[192,256]{1,0:T(8,128)S(1)}, u32[]{:S(2)}, u32[]{:S(2)}) %collective-permute-start.16) | collective-permute-done | bytes 196640 | tf_op jit(solution)/shard_map/ppermute | solution.py:77
  328.7 0.4 collective-permute-start.17
  329.2 2.5 copy.35
  331.7 6.7 %copy.37 = bf16[3,256,3072]{2,1,0:T(8,128)(2,1)} copy(bf16[3,256,3072]{1,2,0:T(8,128)(2,1)} %bitcast.40) | data formatting | bytes 9437184
  338.4 1.0 sub.34
  (32 shorter events, 0.4 us)
Async XLA Ops:
  3.2 29.6 %collective-permute-start = (bf16[3,768,256]{2,1,0:T(8,128)(2,1)S(1)}, bf16[3,768,256]{2,1,0:T(8,128)(2,1)S(1)}, u32[]{:S(2)}, u32[]{:S(2)}) collective-permute-start(bf16[3,768,256]{2,1,0:T(8,128)(2,1)S(1)} %broadcast_multiply_fusion.1), channel_id=1, source_target_pairs={{0,0},{1,1},{2,2},{3,3},{4,36},{5,37},{6,38},{7,39},{8,72},{9,73},... | collective-permute-start | bytes 3538952 | tf_op jit(solution)/shard_map/ppermute | solution.py:54
  32.8 27.0 %collective-permute-start.1 = (bf16[3,768,256]{2,1,0:T(8,128)(2,1)S(1)}, bf16[3,768,256]{2,1,0:T(8,128)(2,1)S(1)}, u32[]{:S(2)}, u32[]{:S(2)}) collective-permute-start(bf16[3,768,256]{2,1,0:T(8,128)(2,1)S(1)} %collective-permute-done), channel_id=1, source_target_pairs={{0,2},{1,3},{2,0},{3,1},{4,6},{5,7},{6,4},{7,5},{8,10},{9,11},{10,... | collective-permute-start | bytes 3538952 | tf_op jit(solution)/shard_map/ppermute | solution.py:55
  59.8 1.8 copy-start.4
  61.6 15.3 %collective-permute-start.2 = (bf16[2,3,768,256]{3,2,1,0:T(8,128)(2,1)}, bf16[2,3,768,256]{3,2,1,0:T(8,128)(2,1)}, u32[]{:S(2)}, u32[]{:S(2)}) collective-permute-start(bf16[2,3,768,256]{3,2,1,0:T(8,128)(2,1)} %maximum_select_fusion.2), channel_id=1, source_target_pairs={{0,1},{1,0},{2,3},{3,2},{4,5},{5,4},{6,7},{7,6},{8,9},{9,8},{10,11... | collective-permute-start | bytes 7077896 | tf_op jit(solution)/shard_map/ppermute | solution.py:57
  61.6 2.3 copy-start
  76.5 5.7 %slice-start.2 = ((s8[4718592]{0:T(1024)(128)(4,1)}), s8[4194304]{0:T(1024)(128)(4,1)S(1)}, s32[]{:S(2)}) async-start(s8[4718592]{0:T(1024)(128)(4,1)} %bitcast.53), calls=%async_computation.2 | async-start | bytes 8388608
  76.9 5.3 %slice-start.3 = ((s8[4718592]{0:T(1024)(128)(4,1)}), s8[524288]{0:T(1024)(128)(4,1)S(1)}, s32[]{:S(2)}) async-start(s8[4718592]{0:T(1024)(128)(4,1)} %bitcast.53), calls=%async_computation.3 | async-start | bytes 1048576
  80.1 2.2 copy-start.1
  89.8 28.6 %collective-permute-start.3 = (f32[1152,256]{1,0:T(8,128)S(1)}, f32[1152,256]{1,0:T(8,128)}, u32[]{:S(2)}, u32[]{:S(2)}) collective-permute-start(f32[1152,256]{1,0:T(8,128)S(1)} %slice_select_fusion), channel_id=1, source_target_pairs={{0,128},{32,160},{64,192},{96,224},{128,0},{160,32},{192,64},{224,... | collective-permute-start | bytes 3538952 | tf_op jit(solution)/shard_map/ppermute | solution.py:72
  120.0 44.1 %collective-permute-start.4 = (f32[576,256]{1,0:T(8,128)S(1)}, f32[576,256]{1,0:T(8,128)S(1)}, u32[]{:S(2)}, u32[]{:S(2)}) collective-permute-start(f32[576,256]{1,0:T(8,128)S(1)} %slice_select_fusion.1), channel_id=1, source_target_pairs={{0,32},{32,0},{64,96},{96,64},{128,160},{160,128},{192,224},{224,1... | collective-permute-start | bytes 1769480 | tf_op jit(solution)/shard_map/ppermute | solution.py:72
  164.3 11.3 %collective-permute-start.5 = (f32[288,256]{1,0:T(8,128)S(1)}, f32[288,256]{1,0:T(8,128)S(1)}, u32[]{:S(2)}, u32[]{:S(2)}) collective-permute-start(f32[288,256]{1,0:T(8,128)S(1)} %slice_select_fusion.3), channel_id=1, source_target_pairs={{0,64},{32,96},{64,0},{96,32},{128,192},{160,224},{192,128},{224,1... | collective-permute-start | bytes 884744 | tf_op jit(solution)/shard_map/ppermute | solution.py:72
  175.7 7.0 %collective-permute-start.6 = (bf16[288,256]{1,0:T(8,128)(2,1)S(1)}, bf16[288,256]{1,0:T(8,128)(2,1)S(1)}, u32[]{:S(2)}, u32[]{:S(2)}) collective-permute-start(bf16[288,256]{1,0:T(8,128)(2,1)S(1)} %add_convert_fusion), channel_id=1, source_target_pairs={{0,64},{32,96},{64,0},{96,32},{128,192},{160,224},{192,128},{224,1... | collective-permute-start | bytes 442376 | tf_op jit(solution)/shard_map/ppermute | solution.py:77
  182.8 6.8 %collective-permute-start.7 = (bf16[576,256]{1,0:T(8,128)(2,1)S(1)}, bf16[576,256]{1,0:T(8,128)(2,1)S(1)}, u32[]{:S(2)}, u32[]{:S(2)}) collective-permute-start(bf16[576,256]{1,0:T(8,128)(2,1)S(1)} %maximum_select_fusion.9), channel_id=1, source_target_pairs={{0,32},{32,0},{64,96},{96,64},{128,160},{160,128},{192,224},{224,1... | collective-permute-start | bytes 884744 | tf_op jit(solution)/shard_map/ppermute | solution.py:77
  189.9 11.7 %collective-permute-start.8 = (bf16[1152,256]{1,0:T(8,128)(2,1)S(1)}, bf16[1152,256]{1,0:T(8,128)(2,1)S(1)}, u32[]{:S(2)}, u32[]{:S(2)}) collective-permute-start(bf16[1152,256]{1,0:T(8,128)(2,1)S(1)} %maximum_select_fusion.7), channel_id=1, source_target_pairs={{0,128},{32,160},{64,192},{96,224},{128,0},{160,32},{192,64},{224,... | collective-permute-start | bytes 1769480 | tf_op jit(solution)/shard_map/ppermute | solution.py:77
  202.3 48.2 %copy-start.2 = (bf16[3,768,256]{2,1,0:T(8,128)(2,1)}, bf16[3,768,256]{2,1,0:T(8,128)(2,1)S(1)}, u32[]{:S(2)}) copy-start(bf16[3,768,256]{2,1,0:T(8,128)(2,1)S(1)} %broadcast_multiply_fusion) | copy-start | bytes 3538948
  202.4 25.3 %collective-permute-start.9 = (bf16[3,768,256]{2,1,0:T(8,128)(2,1)S(1)}, bf16[3,768,256]{2,1,0:T(8,128)(2,1)S(1)}, u32[]{:S(2)}, u32[]{:S(2)}) collective-permute-start(bf16[3,768,256]{2,1,0:T(8,128)(2,1)S(1)} %broadcast_multiply_fusion), channel_id=1, source_target_pairs={{0,0},{1,1},{2,2},{3,3},{4,36},{5,37},{6,38},{7,39},{8,72},{9,73},... | collective-permute-start | bytes 3538952 | tf_op jit(solution)/shard_map/ppermute | solution.py:54
  227.6 22.5 %collective-permute-start.10 = (bf16[3,768,256]{2,1,0:T(8,128)(2,1)S(1)}, bf16[3,768,256]{2,1,0:T(8,128)(2,1)S(1)}, u32[]{:S(2)}, u32[]{:S(2)}) collective-permute-start(bf16[3,768,256]{2,1,0:T(8,128)(2,1)S(1)} %collective-permute-done.9), channel_id=1, source_target_pairs={{0,2},{1,3},{2,0},{3,1},{4,6},{5,7},{6,4},{7,5},{8,10},{9,11},{10,... | collective-permute-start | bytes 3538952 | tf_op jit(solution)/shard_map/ppermute | solution.py:55
  250.5 4.6 %collective-permute-start.11 = (bf16[2,3,768,256]{3,2,1,0:T(8,128)(2,1)S(1)}, bf16[2,3,768,256]{3,2,1,0:T(8,128)(2,1)S(1)}, u32[]{:S(2)}, u32[]{:S(2)}) collective-permute-start(bf16[2,3,768,256]{3,2,1,0:T(8,128)(2,1)S(1)} %maximum_select_fusion.4), channel_id=1, source_target_pairs={{0,1},{1,0},{2,3},{3,2},{4,5},{5,4},{6,7},{7,6},{8,9},{9,8},{10,11... | collective-permute-start | bytes 7077896 | tf_op jit(solution)/shard_map/ppermute | solution.py:57
  255.1 2.2 slice-start
  255.9 1.7 slice-start.1
  259.5 11.2 %collective-permute-start.12 = (f32[384,256]{1,0:T(8,128)S(1)}, f32[384,256]{1,0:T(8,128)S(1)}, u32[]{:S(2)}, u32[]{:S(2)}) collective-permute-start(f32[384,256]{1,0:T(8,128)S(1)} %slice_select_fusion.2), channel_id=1, source_target_pairs={{0,128},{32,160},{64,192},{96,224},{128,0},{160,32},{192,64},{224,... | collective-permute-start | bytes 1179656 | tf_op jit(solution)/shard_map/ppermute | solution.py:72
  270.9 38.2 %collective-permute-start.13 = (f32[192,256]{1,0:T(8,128)S(1)}, f32[192,256]{1,0:T(8,128)S(1)}, u32[]{:S(2)}, u32[]{:S(2)}) collective-permute-start(f32[192,256]{1,0:T(8,128)S(1)} %slice_select_fusion.4), channel_id=1, source_target_pairs={{0,64},{32,96},{64,0},{96,32},{128,192},{160,224},{192,128},{224,1... | collective-permute-start | bytes 589832 | tf_op jit(solution)/shard_map/ppermute | solution.py:72
  309.2 7.0 %collective-permute-start.14 = (f32[96,256]{1,0:T(8,128)S(1)}, f32[96,256]{1,0:T(8,128)S(1)}, u32[]{:S(2)}, u32[]{:S(2)}) collective-permute-start(f32[96,256]{1,0:T(8,128)S(1)} %slice_select_fusion.5), channel_id=1, source_target_pairs={{0,32},{32,0},{64,96},{96,64},{128,160},{160,128},{192,224},{224,1... | collective-permute-start | bytes 294920 | tf_op jit(solution)/shard_map/ppermute | solution.py:72
  316.2 4.7 %collective-permute-start.15 = (f32[96,256]{1,0:T(8,128)S(1)}, f32[96,256]{1,0:T(8,128)S(1)}, u32[]{:S(2)}, u32[]{:S(2)}) collective-permute-start(f32[96,256]{1,0:T(8,128)S(1)} %select_add_fusion.4), channel_id=1, source_target_pairs={{0,32},{32,0},{64,96},{96,64},{128,160},{160,128},{192,224},{224,1... | collective-permute-start | bytes 294920 | tf_op jit(solution)/shard_map/ppermute | solution.py:77
  320.9 7.8 %collective-permute-start.16 = (f32[192,256]{1,0:T(8,128)S(1)}, f32[192,256]{1,0:T(8,128)S(1)}, u32[]{:S(2)}, u32[]{:S(2)}) collective-permute-start(f32[192,256]{1,0:T(8,128)S(1)} %maximum_select_fusion.10), channel_id=1, source_target_pairs={{0,64},{32,96},{64,0},{96,32},{128,192},{160,224},{192,128},{224,1... | collective-permute-start | bytes 589832 | tf_op jit(solution)/shard_map/ppermute | solution.py:77
  328.7 9.6 %collective-permute-start.17 = (f32[384,256]{1,0:T(8,128)S(1)}, f32[384,256]{1,0:T(8,128)S(1)}, u32[]{:S(2)}, u32[]{:S(2)}) collective-permute-start(f32[384,256]{1,0:T(8,128)S(1)} %maximum_select_fusion.8), channel_id=1, source_target_pairs={{0,128},{32,160},{64,192},{96,224},{128,0},{160,32},{192,64},{224,... | collective-permute-start | bytes 1179656 | tf_op jit(solution)/shard_map/ppermute | solution.py:77
  331.7 6.8 %copy-start.3 = (f32[3,256,256]{2,1,0:T(8,128)S(1)}, f32[3,256,256]{2,1,0:T(8,128)}, u32[]{:S(2)}) copy-start(f32[3,256,256]{2,1,0:T(8,128)} %param.9) | copy-start | bytes 2359300

commit v7 on v6

--- a/solution.py
+++ b/solution.py
@@ -95,9 +95,9 @@
     own_sel = structure_rows(row_blocks, pcol_idx * col_rows, col_rows)
     local_lower = factor_block * own_sel[:, :, None].astype(jnp.bfloat16)
     lower_cols = gather_cols(local_lower, perm)
-    tiles4 = inverse_tiles.reshape(col_rows, n_sub, col_rows)
+    lower_flat = jnp.transpose(lower_cols, (1, 0, 2, 3)).reshape(supers, n_sub * col_rows, kwidth)
     partial = jnp.einsum(
-        "irj,rsjk->sik", tiles4, lower_cols, preferred_element_type=jnp.float32
+        "ij,sjk->sik", inverse_tiles, lower_flat, preferred_element_type=jnp.float32
     )
     n_row_bits = [1 << b for b in range(n_row.bit_length() - 1)]
     order = n_row_bits[-1:] + n_row_bits[:-1] if len(n_row_bits) == 3 else None

time: 343 us -> 330 us (0.962)
  local copies, waits for them, and re-layouts: 27.2 us -> 15.8 us
    reshape x1 -> x0, local copies, waits for them, and re-layouts: 9.76 us -> none  [shards(): tiles4 = inverse_tiles.reshape(col_rows, n_sub, col_rows)]
    ppermute x2, waiting for transfers between devices: 4.13 us -> 8.59 us  [gather_cols(): twin = lax.ppermute(pair, ALL, near)]
    unnamed x19 -> x17, local copies, waits for them, and re-layouts: 11.9 us -> 9.93 us
  transfers between devices with their start and end apart: 18 -> 18, of which waited for: 16 -> 17; matrix products, arithmetic and copies ran while one was open for 7% -> 3% of each run, Pallas kernels for 0% -> 0%
where the time goes in v7:
time: 330 us; the launch traced here: 327 us
  waiting for transfers between devices  196 us (59%)
  starting transfers between devices  93.4 us (28%)
  local copies, waits for them, and re-layouts  15.8 us (5%)
  other arithmetic  13.8 us (4%)
  matrix products  7.14 us (2%)
    ppermute x6, starting transfers between devices, row_sum(): seg = keep + lax.ppermute(send, 'prow', [(i, i ^ m) for i in range(n)])  74 us
    ppermute x6, waiting for transfers between devices, row_sum(): seg = keep + lax.ppermute(send, 'prow', [(i, i ^ m) for i in range(n)])  64.8 us
    ppermute x2, waiting for transfers between devices, gather_cols(): mine = lax.ppermute(block, ALL, swap)  49.4 us
    ppermute x2, waiting for transfers between devices, gather_cols(): other = lax.ppermute(mine, ALL, far)  45.5 us
    ppermute x6, waiting for transfers between devices, row_sum(): got = lax.ppermute(seg, 'prow', [(i, i ^ m) for i in range(n)])  27.5 us
    ppermute x6, starting transfers between devices, row_sum(): got = lax.ppermute(seg, 'prow', [(i, i ^ m) for i in range(n)])  10.5 us
    unnamed x17, local copies, waits for them, and re-layouts  9.93 us
    ppermute x2, waiting for transfers between devices, gather_cols(): twin = lax.ppermute(pair, ALL, near)  8.59 us
  transfers between devices with their start and end apart: 18, of which 17 were waited for; matrix products, arithmetic and copies ran while one was open for 3% of the time, Pallas kernels for 0%

profile of v7, /device:TPU:4, one launch (start us, length us, event | category | flops | bytes accessed | tf_op | source)
XLA Modules:
  0.0 326.8 jit_solution(7120881353075515641)
XLA Ops:
  0.7 0.9 compare_reduce_fusion
  1.5 1.6 broadcast_multiply_fusion.1
  3.2 2.4 collective-permute-start
  5.6 27.2 %collective-permute-done = bf16[3,768,256]{2,1,0:T(8,128)(2,1)S(1)} collective-permute-done((bf16[3,768,256]{2,1,0:T(8,128)(2,1)S(1)}, bf16[3,768,256]{2,1,0:T(8,128)(2,1)S(1)}, u32[]{:S(2)}, u32[]{:S(2)}) %collective-permute-start) | collective-permute-done | bytes 1179680 | tf_op jit(solution)/shard_map/ppermute | solution.py:54
  32.8 1.9 collective-permute-start.1
  34.7 25.1 %collective-permute-done.1 = bf16[3,768,256]{2,1,0:T(8,128)(2,1)S(1)} collective-permute-done((bf16[3,768,256]{2,1,0:T(8,128)(2,1)S(1)}, bf16[3,768,256]{2,1,0:T(8,128)(2,1)S(1)}, u32[]{:S(2)}, u32[]{:S(2)}) %collective-permute-start.1) | collective-permute-done | bytes 1179680 | tf_op jit(solution)/shard_map/ppermute | solution.py:55
  59.8 1.8 maximum_select_fusion.2
  61.6 0.4 bitcast_select_fusion
  62.0 4.5 %collective-permute-done.2 = bf16[2,3,768,256]{3,2,1,0:T(8,128)(2,1)} collective-permute-done((bf16[2,3,768,256]{3,2,1,0:T(8,128)(2,1)}, bf16[2,3,768,256]{3,2,1,0:T(8,128)(2,1)}, u32[]{:S(2)}, u32[]{:S(2)}) %collective-permute-start.2) | collective-permute-done | bytes 2359328 | tf_op jit(solution)/shard_map/ppermute | solution.py:57
  66.5 3.1 maximum_select_fusion
  69.6 0.3 copy.30
  70.0 1.8 copy-done
  71.8 0.7 broadcast_in_dim.2
  72.5 5.3 %fusion.4 = f32[3,768,256]{1,2,0:T(8,128)} fusion(bf16[3,3072,256]{2,1,0:T(8,128)(2,1)S(1)} %bitcast.62, bf16[768,3072]{1,0:T(8,128)(2,1)S(1)} %bitcast.70, bf16[96,8,24,128]{3,2,1,0:T(8,128)(2,1)S(1)} %bitcast.63), kind=kOutput, calls=%fused_computation.10 | convolution fusion | flops 3626237952 | bytes 16515072 | tf_op jit(solution)/shard_map/ij,sjk->sik/dot_general | solution.py:99
  77.8 2.0 copy.32
  79.9 0.2 slice_select_fusion
  80.0 0.1 collective-permute-start.3
  80.1 28.1 %collective-permute-done.3 = f32[1152,256]{1,0:T(8,128)} collective-permute-done((f32[1152,256]{1,0:T(8,128)S(1)}, f32[1152,256]{1,0:T(8,128)}, u32[]{:S(2)}, u32[]{:S(2)}) %collective-permute-start.3) | collective-permute-done | bytes 1179680 | tf_op jit(solution)/shard_map/ppermute | solution.py:72
  108.2 1.5 select_add_fusion
  109.7 0.1 slice_select_fusion.1
  109.8 31.0 %collective-permute-start.4 = (f32[576,256]{1,0:T(8,128)S(1)}, f32[576,256]{1,0:T(8,128)S(1)}, u32[]{:S(2)}, u32[]{:S(2)}) collective-permute-start(f32[576,256]{1,0:T(8,128)S(1)} %slice_select_fusion.1), channel_id=1, source_target_pairs={{0,32},{32,0},{64,96},{96,64},{128,160},{160,128},{192,224},{224,1... | collective-permute-start | bytes 1769480 | tf_op jit(solution)/shard_map/ppermute | solution.py:72
  140.8 12.8 %collective-permute-done.4 = f32[576,256]{1,0:T(8,128)S(1)} collective-permute-done((f32[576,256]{1,0:T(8,128)S(1)}, f32[576,256]{1,0:T(8,128)S(1)}, u32[]{:S(2)}, u32[]{:S(2)}) %collective-permute-start.4) | collective-permute-done | bytes 589856 | tf_op jit(solution)/shard_map/ppermute | solution.py:72
  153.6 0.1 select_add_fusion.1
  153.7 4.9 %collective-permute-start.5 = (f32[288,256]{1,0:T(8,128)S(1)}, f32[288,256]{1,0:T(8,128)S(1)}, u32[]{:S(2)}, u32[]{:S(2)}) collective-permute-start(f32[288,256]{1,0:T(8,128)S(1)} %slice_select_fusion.3), channel_id=1, source_target_pairs={{0,64},{32,96},{64,0},{96,32},{128,192},{160,224},{192,128},{224,1... | collective-permute-start | bytes 884744 | tf_op jit(solution)/shard_map/ppermute | solution.py:72
  158.6 5.9 %collective-permute-done.5 = f32[288,256]{1,0:T(8,128)S(1)} collective-permute-done((f32[288,256]{1,0:T(8,128)S(1)}, f32[288,256]{1,0:T(8,128)S(1)}, u32[]{:S(2)}, u32[]{:S(2)}) %collective-permute-start.5) | collective-permute-done | bytes 294944 | tf_op jit(solution)/shard_map/ppermute | solution.py:72
  164.6 3.3 %collective-permute-start.6 = (bf16[288,256]{1,0:T(8,128)(2,1)S(1)}, bf16[288,256]{1,0:T(8,128)(2,1)S(1)}, u32[]{:S(2)}, u32[]{:S(2)}) collective-permute-start(bf16[288,256]{1,0:T(8,128)(2,1)S(1)} %add_convert_fusion), channel_id=1, source_target_pairs={{0,64},{32,96},{64,0},{96,32},{128,192},{160,224},{192,128},{224,1... | collective-permute-start | bytes 442376 | tf_op jit(solution)/shard_map/ppermute | solution.py:77
  167.9 3.9 %collective-permute-done.6 = bf16[288,256]{1,0:T(8,128)(2,1)S(1)} collective-permute-done((bf16[288,256]{1,0:T(8,128)(2,1)S(1)}, bf16[288,256]{1,0:T(8,128)(2,1)S(1)}, u32[]{:S(2)}, u32[]{:S(2)}) %collective-permute-start.6) | collective-permute-done | bytes 147488 | tf_op jit(solution)/shard_map/ppermute | solution.py:77
  171.8 0.1 maximum_select_fusion.9
  171.9 0.7 collective-permute-start.7
  172.6 6.3 %collective-permute-done.7 = bf16[576,256]{1,0:T(8,128)(2,1)S(1)} collective-permute-done((bf16[576,256]{1,0:T(8,128)(2,1)S(1)}, bf16[576,256]{1,0:T(8,128)(2,1)S(1)}, u32[]{:S(2)}, u32[]{:S(2)}) %collective-permute-start.7) | collective-permute-done | bytes 294944 | tf_op jit(solution)/shard_map/ppermute | solution.py:77
  178.9 0.3 maximum_select_fusion.7
  179.2 0.6 collective-permute-start.8
  179.7 10.7 %collective-permute-done.8 = bf16[1152,256]{1,0:T(8,128)(2,1)S(1)} collective-permute-done((bf16[1152,256]{1,0:T(8,128)(2,1)S(1)}, bf16[1152,256]{1,0:T(8,128)(2,1)S(1)}, u32[]{:S(2)}, u32[]{:S(2)}) %collective-permute-start.8) | collective-permute-done | bytes 589856 | tf_op jit(solution)/shard_map/ppermute | solution.py:77
  190.5 0.4 fusion.7
  190.9 0.4 broadcast_multiply_fusion
  191.3 2.6 collective-permute-start.9
  193.9 22.3 %collective-permute-done.9 = bf16[3,768,256]{2,1,0:T(8,128)(2,1)S(1)} collective-permute-done((bf16[3,768,256]{2,1,0:T(8,128)(2,1)S(1)}, bf16[3,768,256]{2,1,0:T(8,128)(2,1)S(1)}, u32[]{:S(2)}, u32[]{:S(2)}) %collective-permute-start.9) | collective-permute-done | bytes 1179680 | tf_op jit(solution)/shard_map/ppermute | solution.py:54
  216.2 1.8 collective-permute-start.10
  217.9 20.4 %collective-permute-done.10 = bf16[3,768,256]{2,1,0:T(8,128)(2,1)S(1)} collective-permute-done((bf16[3,768,256]{2,1,0:T(8,128)(2,1)S(1)}, bf16[3,768,256]{2,1,0:T(8,128)(2,1)S(1)}, u32[]{:S(2)}, u32[]{:S(2)}) %collective-permute-start.10) | collective-permute-done | bytes 1179680 | tf_op jit(solution)/shard_map/ppermute | solution.py:55
  238.3 0.4 maximum_select_fusion.4
  238.7 0.1 collective-permute-start.11
  238.8 0.4 maximum_select_fusion.3
  239.2 4.1 %collective-permute-done.11 = bf16[2,3,768,256]{3,2,1,0:T(8,128)(2,1)S(1)} collective-permute-done((bf16[2,3,768,256]{3,2,1,0:T(8,128)(2,1)S(1)}, bf16[2,3,768,256]{3,2,1,0:T(8,128)(2,1)S(1)}, u32[]{:S(2)}, u32[]{:S(2)}) %collective-permute-start.11) | collective-permute-done | bytes 2359328 | tf_op jit(solution)/shard_map/ppermute | solution.py:57
  243.3 0.7 maximum_select_fusion.1
  244.1 0.3 copy.33
  244.4 1.1 slice-done
  245.5 0.3 slice-done.1
  245.8 1.8 fusion.11
  247.7 0.1 collective-permute-start.12
  247.8 11.1 %collective-permute-done.12 = f32[384,256]{1,0:T(8,128)S(1)} collective-permute-done((f32[384,256]{1,0:T(8,128)S(1)}, f32[384,256]{1,0:T(8,128)S(1)}, u32[]{:S(2)}, u32[]{:S(2)}) %collective-permute-start.12) | collective-permute-done | bytes 393248 | tf_op jit(solution)/shard_map/ppermute | solution.py:72
  259.0 0.1 select_add_fusion.2
  259.1 33.0 %collective-permute-start.13 = (f32[192,256]{1,0:T(8,128)S(1)}, f32[192,256]{1,0:T(8,128)S(1)}, u32[]{:S(2)}, u32[]{:S(2)}) collective-permute-start(f32[192,256]{1,0:T(8,128)S(1)} %slice_select_fusion.4), channel_id=1, source_target_pairs={{0,64},{32,96},{64,0},{96,32},{128,192},{160,224},{192,128},{224,1... | collective-permute-start | bytes 589832 | tf_op jit(solution)/shard_map/ppermute | solution.py:72
  292.1 4.3 %collective-permute-done.13 = f32[192,256]{1,0:T(8,128)S(1)} collective-permute-done((f32[192,256]{1,0:T(8,128)S(1)}, f32[192,256]{1,0:T(8,128)S(1)}, u32[]{:S(2)}, u32[]{:S(2)}) %collective-permute-start.13) | collective-permute-done | bytes 196640 | tf_op jit(solution)/shard_map/ppermute | solution.py:72
  296.5 4.9 %collective-permute-start.14 = (f32[96,256]{1,0:T(8,128)S(1)}, f32[96,256]{1,0:T(8,128)S(1)}, u32[]{:S(2)}, u32[]{:S(2)}) collective-permute-start(f32[96,256]{1,0:T(8,128)S(1)} %slice_select_fusion.5), channel_id=1, source_target_pairs={{0,32},{32,0},{64,96},{96,64},{128,160},{160,128},{192,224},{224,1... | collective-permute-start | bytes 294920 | tf_op jit(solution)/shard_map/ppermute | solution.py:72
  301.4 2.6 collective-permute-done.14
  304.0 2.1 collective-permute-start.15
  306.1 2.6 collective-permute-done.15
  308.7 3.3 %collective-permute-start.16 = (f32[192,256]{1,0:T(8,128)S(1)}, f32[192,256]{1,0:T(8,128)S(1)}, u32[]{:S(2)}, u32[]{:S(2)}) collective-permute-start(f32[192,256]{1,0:T(8,128)S(1)} %maximum_select_fusion.10), channel_id=1, source_target_pairs={{0,64},{32,96},{64,0},{96,32},{128,192},{160,224},{192,128},{224,1... | collective-permute-start | bytes 589832 | tf_op jit(solution)/shard_map/ppermute | solution.py:77
  312.0 4.0 %collective-permute-done.16 = f32[192,256]{1,0:T(8,128)S(1)} collective-permute-done((f32[192,256]{1,0:T(8,128)S(1)}, f32[192,256]{1,0:T(8,128)S(1)}, u32[]{:S(2)}, u32[]{:S(2)}) %collective-permute-start.16) | collective-permute-done | bytes 196640 | tf_op jit(solution)/shard_map/ppermute | solution.py:77
  316.0 0.6 collective-permute-start.17
  316.6 2.5 copy.34
  319.1 6.7 %copy.36 = bf16[3,256,3072]{2,1,0:T(8,128)(2,1)} copy(bf16[3,256,3072]{1,2,0:T(8,128)(2,1)} %bitcast.53) | data formatting | bytes 9437184
  325.8 0.1 maximum_select_fusion.6
  325.8 1.0 sub.34
  (29 shorter events, 0.4 us)
Async XLA Ops:
  3.2 29.6 %collective-permute-start = (bf16[3,768,256]{2,1,0:T(8,128)(2,1)S(1)}, bf16[3,768,256]{2,1,0:T(8,128)(2,1)S(1)}, u32[]{:S(2)}, u32[]{:S(2)}) collective-permute-start(bf16[3,768,256]{2,1,0:T(8,128)(2,1)S(1)} %broadcast_multiply_fusion.1), channel_id=1, source_target_pairs={{0,0},{1,1},{2,2},{3,3},{4,36},{5,37},{6,38},{7,39},{8,72},{9,73},... | collective-permute-start | bytes 3538952 | tf_op jit(solution)/shard_map/ppermute | solution.py:54
  32.8 27.0 %collective-permute-start.1 = (bf16[3,768,256]{2,1,0:T(8,128)(2,1)S(1)}, bf16[3,768,256]{2,1,0:T(8,128)(2,1)S(1)}, u32[]{:S(2)}, u32[]{:S(2)}) collective-permute-start(bf16[3,768,256]{2,1,0:T(8,128)(2,1)S(1)} %collective-permute-done), channel_id=1, source_target_pairs={{0,2},{1,3},{2,0},{3,1},{4,6},{5,7},{6,4},{7,5},{8,10},{9,11},{10,... | collective-permute-start | bytes 3538952 | tf_op jit(solution)/shard_map/ppermute | solution.py:55
  59.8 1.8 copy-start.3
  61.6 4.9 %collective-permute-start.2 = (bf16[2,3,768,256]{3,2,1,0:T(8,128)(2,1)}, bf16[2,3,768,256]{3,2,1,0:T(8,128)(2,1)}, u32[]{:S(2)}, u32[]{:S(2)}) collective-permute-start(bf16[2,3,768,256]{3,2,1,0:T(8,128)(2,1)} %maximum_select_fusion.2), channel_id=1, source_target_pairs={{0,1},{1,0},{2,3},{3,2},{4,5},{5,4},{6,7},{7,6},{8,9},{9,8},{10,11... | collective-permute-start | bytes 7077896 | tf_op jit(solution)/shard_map/ppermute | solution.py:57
  66.5 6.0 %slice-start.2 = ((s8[4718592]{0:T(1024)(128)(4,1)}), s8[4194304]{0:T(1024)(128)(4,1)S(1)}, s32[]{:S(2)}) async-start(s8[4718592]{0:T(1024)(128)(4,1)} %bitcast.69), calls=%async_computation.2 | async-start | bytes 8388608
  69.6 2.2 copy-start
  69.6 2.9 slice-start.3
  80.0 28.2 %collective-permute-start.3 = (f32[1152,256]{1,0:T(8,128)S(1)}, f32[1152,256]{1,0:T(8,128)}, u32[]{:S(2)}, u32[]{:S(2)}) collective-permute-start(f32[1152,256]{1,0:T(8,128)S(1)} %slice_select_fusion), channel_id=1, source_target_pairs={{0,128},{32,160},{64,192},{96,224},{128,0},{160,32},{192,64},{224,... | collective-permute-start | bytes 3538952 | tf_op jit(solution)/shard_map/ppermute | solution.py:72
  109.8 43.8 %collective-permute-start.4 = (f32[576,256]{1,0:T(8,128)S(1)}, f32[576,256]{1,0:T(8,128)S(1)}, u32[]{:S(2)}, u32[]{:S(2)}) collective-permute-start(f32[576,256]{1,0:T(8,128)S(1)} %slice_select_fusion.1), channel_id=1, source_target_pairs={{0,32},{32,0},{64,96},{96,64},{128,160},{160,128},{192,224},{224,1... | collective-permute-start | bytes 1769480 | tf_op jit(solution)/shard_map/ppermute | solution.py:72
  153.7 10.8 %collective-permute-start.5 = (f32[288,256]{1,0:T(8,128)S(1)}, f32[288,256]{1,0:T(8,128)S(1)}, u32[]{:S(2)}, u32[]{:S(2)}) collective-permute-start(f32[288,256]{1,0:T(8,128)S(1)} %slice_select_fusion.3), channel_id=1, source_target_pairs={{0,64},{32,96},{64,0},{96,32},{128,192},{160,224},{192,128},{224,1... | collective-permute-start | bytes 884744 | tf_op jit(solution)/shard_map/ppermute | solution.py:72
  164.6 7.2 %collective-permute-start.6 = (bf16[288,256]{1,0:T(8,128)(2,1)S(1)}, bf16[288,256]{1,0:T(8,128)(2,1)S(1)}, u32[]{:S(2)}, u32[]{:S(2)}) collective-permute-start(bf16[288,256]{1,0:T(8,128)(2,1)S(1)} %add_convert_fusion), channel_id=1, source_target_pairs={{0,64},{32,96},{64,0},{96,32},{128,192},{160,224},{192,128},{224,1... | collective-permute-start | bytes 442376 | tf_op jit(solution)/shard_map/ppermute | solution.py:77
  171.9 7.0 %collective-permute-start.7 = (bf16[576,256]{1,0:T(8,128)(2,1)S(1)}, bf16[576,256]{1,0:T(8,128)(2,1)S(1)}, u32[]{:S(2)}, u32[]{:S(2)}) collective-permute-start(bf16[576,256]{1,0:T(8,128)(2,1)S(1)} %maximum_select_fusion.9), channel_id=1, source_target_pairs={{0,32},{32,0},{64,96},{96,64},{128,160},{160,128},{192,224},{224,1... | collective-permute-start | bytes 884744 | tf_op jit(solution)/shard_map/ppermute | solution.py:77
  179.2 11.3 %collective-permute-start.8 = (bf16[1152,256]{1,0:T(8,128)(2,1)S(1)}, bf16[1152,256]{1,0:T(8,128)(2,1)S(1)}, u32[]{:S(2)}, u32[]{:S(2)}) collective-permute-start(bf16[1152,256]{1,0:T(8,128)(2,1)S(1)} %maximum_select_fusion.7), channel_id=1, source_target_pairs={{0,128},{32,160},{64,192},{96,224},{128,0},{160,32},{192,64},{224,... | collective-permute-start | bytes 1769480 | tf_op jit(solution)/shard_map/ppermute | solution.py:77
  191.3 47.4 %copy-start.1 = (bf16[3,768,256]{2,1,0:T(8,128)(2,1)}, bf16[3,768,256]{2,1,0:T(8,128)(2,1)S(1)}, u32[]{:S(2)}) copy-start(bf16[3,768,256]{2,1,0:T(8,128)(2,1)S(1)} %broadcast_multiply_fusion) | copy-start | bytes 3538948
  191.3 24.9 %collective-permute-start.9 = (bf16[3,768,256]{2,1,0:T(8,128)(2,1)S(1)}, bf16[3,768,256]{2,1,0:T(8,128)(2,1)S(1)}, u32[]{:S(2)}, u32[]{:S(2)}) collective-permute-start(bf16[3,768,256]{2,1,0:T(8,128)(2,1)S(1)} %broadcast_multiply_fusion), channel_id=1, source_target_pairs={{0,0},{1,1},{2,2},{3,3},{4,36},{5,37},{6,38},{7,39},{8,72},{9,73},... | collective-permute-start | bytes 3538952 | tf_op jit(solution)/shard_map/ppermute | solution.py:54
  216.2 22.2 %collective-permute-start.10 = (bf16[3,768,256]{2,1,0:T(8,128)(2,1)S(1)}, bf16[3,768,256]{2,1,0:T(8,128)(2,1)S(1)}, u32[]{:S(2)}, u32[]{:S(2)}) collective-permute-start(bf16[3,768,256]{2,1,0:T(8,128)(2,1)S(1)} %collective-permute-done.9), channel_id=1, source_target_pairs={{0,2},{1,3},{2,0},{3,1},{4,6},{5,7},{6,4},{7,5},{8,10},{9,11},{10,... | collective-permute-start | bytes 3538952 | tf_op jit(solution)/shard_map/ppermute | solution.py:55
  238.7 4.6 %collective-permute-start.11 = (bf16[2,3,768,256]{3,2,1,0:T(8,128)(2,1)S(1)}, bf16[2,3,768,256]{3,2,1,0:T(8,128)(2,1)S(1)}, u32[]{:S(2)}, u32[]{:S(2)}) collective-permute-start(bf16[2,3,768,256]{3,2,1,0:T(8,128)(2,1)S(1)} %maximum_select_fusion.4), channel_id=1, source_target_pairs={{0,1},{1,0},{2,3},{3,2},{4,5},{5,4},{6,7},{7,6},{8,9},{9,8},{10,11... | collective-permute-start | bytes 7077896 | tf_op jit(solution)/shard_map/ppermute | solution.py:57
  243.3 2.2 slice-start
  244.1 1.7 slice-start.1
  247.7 11.2 %collective-permute-start.12 = (f32[384,256]{1,0:T(8,128)S(1)}, f32[384,256]{1,0:T(8,128)S(1)}, u32[]{:S(2)}, u32[]{:S(2)}) collective-permute-start(f32[384,256]{1,0:T(8,128)S(1)} %slice_select_fusion.2), channel_id=1, source_target_pairs={{0,128},{32,160},{64,192},{96,224},{128,0},{160,32},{192,64},{224,... | collective-permute-start | bytes 1179656 | tf_op jit(solution)/shard_map/ppermute | solution.py:72
  259.1 37.4 %collective-permute-start.13 = (f32[192,256]{1,0:T(8,128)S(1)}, f32[192,256]{1,0:T(8,128)S(1)}, u32[]{:S(2)}, u32[]{:S(2)}) collective-permute-start(f32[192,256]{1,0:T(8,128)S(1)} %slice_select_fusion.4), channel_id=1, source_target_pairs={{0,64},{32,96},{64,0},{96,32},{128,192},{160,224},{192,128},{224,1... | collective-permute-start | bytes 589832 | tf_op jit(solution)/shard_map/ppermute | solution.py:72
  296.5 7.5 %collective-permute-start.14 = (f32[96,256]{1,0:T(8,128)S(1)}, f32[96,256]{1,0:T(8,128)S(1)}, u32[]{:S(2)}, u32[]{:S(2)}) collective-permute-start(f32[96,256]{1,0:T(8,128)S(1)} %slice_select_fusion.5), channel_id=1, source_target_pairs={{0,32},{32,0},{64,96},{96,64},{128,160},{160,128},{192,224},{224,1... | collective-permute-start | bytes 294920 | tf_op jit(solution)/shard_map/ppermute | solution.py:72
  304.0 4.7 %collective-permute-start.15 = (f32[96,256]{1,0:T(8,128)S(1)}, f32[96,256]{1,0:T(8,128)S(1)}, u32[]{:S(2)}, u32[]{:S(2)}) collective-permute-start(f32[96,256]{1,0:T(8,128)S(1)} %select_add_fusion.4), channel_id=1, source_target_pairs={{0,32},{32,0},{64,96},{96,64},{128,160},{160,128},{192,224},{224,1... | collective-permute-start | bytes 294920 | tf_op jit(solution)/shard_map/ppermute | solution.py:77
  308.7 7.3 %collective-permute-start.16 = (f32[192,256]{1,0:T(8,128)S(1)}, f32[192,256]{1,0:T(8,128)S(1)}, u32[]{:S(2)}, u32[]{:S(2)}) collective-permute-start(f32[192,256]{1,0:T(8,128)S(1)} %maximum_select_fusion.10), channel_id=1, source_target_pairs={{0,64},{32,96},{64,0},{96,32},{128,192},{160,224},{192,128},{224,1... | collective-permute-start | bytes 589832 | tf_op jit(solution)/shard_map/ppermute | solution.py:77
  316.0 9.7 %collective-permute-start.17 = (f32[384,256]{1,0:T(8,128)S(1)}, f32[384,256]{1,0:T(8,128)S(1)}, u32[]{:S(2)}, u32[]{:S(2)}) collective-permute-start(f32[384,256]{1,0:T(8,128)S(1)} %maximum_select_fusion.8), channel_id=1, source_target_pairs={{0,128},{32,160},{64,192},{96,224},{128,0},{160,32},{192,64},{224,... | collective-permute-start | bytes 1179656 | tf_op jit(solution)/shard_map/ppermute | solution.py:77
  319.1 6.8 %copy-start.2 = (f32[3,256,256]{2,1,0:T(8,128)S(1)}, f32[3,256,256]{2,1,0:T(8,128)}, u32[]{:S(2)}) copy-start(f32[3,256,256]{2,1,0:T(8,128)} %param.9) | copy-start | bytes 2359300

commit v8 on v7

--- a/solution.py
+++ b/solution.py
@@ -46,17 +46,16 @@
     ]
 
 
-def gather_cols(block, perms):
+def gather_cols(block, perms, axis=0):
     swap, far, near = perms
     sub = lax.axis_index("pr")
     high = sub // 2
     low = sub % 2
     mine = lax.ppermute(block, ALL, swap)
     other = lax.ppermute(mine, ALL, far)
-    pair = jnp.where(high == 0, jnp.stack([mine, other]), jnp.stack([other, mine]))
+    pair = jnp.where(high == 0, jnp.stack([mine, other], axis), jnp.stack([other, mine], axis))
     twin = lax.ppermute(pair, ALL, near)
-    quad = jnp.where(low == 0, jnp.stack([pair, twin], 1), jnp.stack([twin, pair], 1))
-    return quad.reshape((4,) + block.shape)
+    return jnp.where(low == 0, jnp.stack([pair, twin], axis + 1), jnp.stack([twin, pair], axis + 1))
 
 
 def row_sum(x, order=None, between=None):
@@ -94,7 +93,7 @@
     inverse_tiles = ancestor_inv * expand_tiles(tile_pattern)
     own_sel = structure_rows(row_blocks, pcol_idx * col_rows, col_rows)
     local_lower = factor_block * own_sel[:, :, None].astype(jnp.bfloat16)
-    lower_cols = gather_cols(local_lower, perm)
+    lower_cols = gather_cols(local_lower, perm).reshape((n_sub,) + local_lower.shape)
     lower_flat = jnp.transpose(lower_cols, (1, 0, 2, 3)).reshape(supers, n_sub * col_rows, kwidth)
     partial = jnp.einsum(
         "ij,sjk->sik", inverse_tiles, lower_flat, preferred_element_type=jnp.float32
@@ -105,10 +104,13 @@
         partial.reshape(supers * col_rows, kwidth), order, lambda seg: seg.astype(jnp.bfloat16)
     ).reshape(supers, col_rows, kwidth)
     column = -summed * own_sel[:, :, None].astype(jnp.bfloat16)
-    column_cols = gather_cols(column, perm)
-    row_out = jnp.transpose(column_cols, (1, 3, 0, 2)).reshape(supers, kwidth, n_sub * col_rows)
+    column_rows = gather_cols(jnp.swapaxes(column, 1, 2), perm, 2)
+    row_out = column_rows.reshape(supers, kwidth, n_sub * col_rows)
     contrib = jnp.einsum(
-        "rsjk,rsjl->skl", lower_cols, column_cols, preferred_element_type=jnp.float32
+        "tsjk,sltj->skl",
+        lower_cols,
+        column_rows.reshape(supers, kwidth, n_sub, col_rows),
+        preferred_element_type=jnp.float32,
     )
     flat = contrib.reshape(supers * kwidth, kwidth)
     diagonal = diag_base - row_sum(flat).reshape(supers, kwidth, kwidth)

time: 330 us -> 342 us (1.036)
  local copies, waits for them, and re-layouts: 15.8 us -> 20.7 us
  matrix products: 7.14 us -> 10.9 us
    select_n x1 -> x2, local copies, waits for them, and re-layouts: 0.32 us -> 9.17 us  [gather_cols(): jnp.where(low == 0, jnp.stack([pair, twin], axis + 1), jnp.stack([twin, p...]
    dot_general x1, matrix products: 1.84 us -> 5.65 us  [shards(): jnp.einsum('tsjk,sltj->skl', lower_cols, column_rows.reshape(supers, kwid...]
    unnamed x17 -> x15, local copies, waits for them, and re-layouts: 9.93 us -> 8.5 us
where the time goes in v8:
time: 342 us; the launch traced here: 339 us
  waiting for transfers between devices  196 us (57%)
  starting transfers between devices  93.3 us (27%)
  local copies, waits for them, and re-layouts  20.7 us (6%)
  other arithmetic  16.9 us (5%)
  matrix products  10.9 us (3%)
    ppermute x6, starting transfers between devices, row_sum(): seg = keep + lax.ppermute(send, 'prow', [(i, i ^ m) for i in range(n)])  73.7 us
    ppermute x6, waiting for transfers between devices, row_sum(): seg = keep + lax.ppermute(send, 'prow', [(i, i ^ m) for i in range(n)])  64.8 us
    ppermute x2, waiting for transfers between devices, gather_cols(): mine = lax.ppermute(block, ALL, swap)  49.4 us
    ppermute x2, waiting for transfers between devices, gather_cols(): other = lax.ppermute(mine, ALL, far)  45.5 us
    ppermute x6, waiting for transfers between devices, row_sum(): got = lax.ppermute(seg, 'prow', [(i, i ^ m) for i in range(n)])  27.6 us
    ppermute x6, starting transfers between devices, row_sum(): got = lax.ppermute(seg, 'prow', [(i, i ^ m) for i in range(n)])  10.7 us
    select_n x2, local copies, waits for them, and re-layouts, gather_cols(): jnp.where(low == 0, jnp.stack([pair, twin], axis + 1), jnp.stack([twin, p...  9.17 us
    ppermute x2, waiting for transfers between devices, gather_cols(): twin = lax.ppermute(pair, ALL, near)  8.59 us
  transfers between devices with their start and end apart: 18, of which 17 were waited for; matrix products, arithmetic and copies ran while one was open for 3% of the time, Pallas kernels for 0%

profile of v8, /device:TPU:4, one launch (start us, length us, event | category | flops | bytes accessed | tf_op | source)
XLA Modules:
  0.0 338.7 jit_solution(16243851510297866227)
XLA Ops:
  0.7 0.9 compare_reduce_fusion
  1.5 1.6 broadcast_multiply_fusion.1
  3.2 2.4 collective-permute-start
  5.6 27.2 %collective-permute-done = bf16[3,768,256]{2,1,0:T(8,128)(2,1)S(1)} collective-permute-done((bf16[3,768,256]{2,1,0:T(8,128)(2,1)S(1)}, bf16[3,768,256]{2,1,0:T(8,128)(2,1)S(1)}, u32[]{:S(2)}, u32[]{:S(2)}) %collective-permute-start) | collective-permute-done | bytes 1179680 | tf_op jit(solution)/shard_map/ppermute | solution.py:54
  32.8 1.9 collective-permute-start.1
  34.7 25.1 %collective-permute-done.1 = bf16[3,768,256]{2,1,0:T(8,128)(2,1)S(1)} collective-permute-done((bf16[3,768,256]{2,1,0:T(8,128)(2,1)S(1)}, bf16[3,768,256]{2,1,0:T(8,128)(2,1)S(1)}, u32[]{:S(2)}, u32[]{:S(2)}) %collective-permute-start.1) | collective-permute-done | bytes 1179680 | tf_op jit(solution)/shard_map/ppermute | solution.py:55
  59.8 1.8 maximum_select_fusion.3
  61.6 0.4 maximum_select_fusion.2
  62.0 4.5 %collective-permute-done.2 = bf16[2,3,768,256]{3,2,1,0:T(8,128)(2,1)} collective-permute-done((bf16[2,3,768,256]{3,2,1,0:T(8,128)(2,1)}, bf16[2,3,768,256]{3,2,1,0:T(8,128)(2,1)}, u32[]{:S(2)}, u32[]{:S(2)}) %collective-permute-start.2) | collective-permute-done | bytes 2359328 | tf_op jit(solution)/shard_map/ppermute | solution.py:57
  66.5 3.1 maximum_select_fusion
  69.6 0.3 copy.22
  70.0 1.8 copy-done
  71.8 0.7 broadcast_in_dim.2
  72.5 5.3 %fusion.6 = f32[3,768,256]{1,2,0:T(8,128)} fusion(bf16[3,3072,256]{2,1,0:T(8,128)(2,1)S(1)} %bitcast.59, bf16[768,3072]{1,0:T(8,128)(2,1)S(1)} %bitcast.67, bf16[96,8,24,128]{3,2,1,0:T(8,128)(2,1)S(1)} %bitcast.60), kind=kOutput, calls=%fused_computation.12 | convolution fusion | flops 3626237952 | bytes 16515072 | tf_op jit(solution)/shard_map/ij,sjk->sik/dot_general | solution.py:98
  77.7 2.0 copy.24
  79.8 0.2 slice_select_fusion
  79.9 0.1 collective-permute-start.3
  80.0 28.1 %collective-permute-done.3 = f32[1152,256]{1,0:T(8,128)} collective-permute-done((f32[1152,256]{1,0:T(8,128)S(1)}, f32[1152,256]{1,0:T(8,128)}, u32[]{:S(2)}, u32[]{:S(2)}) %collective-permute-start.3) | collective-permute-done | bytes 1179680 | tf_op jit(solution)/shard_map/ppermute | solution.py:71
  108.1 1.5 select_add_fusion
  109.6 0.1 slice_select_fusion.1
  109.7 31.0 %collective-permute-start.4 = (f32[576,256]{1,0:T(8,128)S(1)}, f32[576,256]{1,0:T(8,128)S(1)}, u32[]{:S(2)}, u32[]{:S(2)}) collective-permute-start(f32[576,256]{1,0:T(8,128)S(1)} %slice_select_fusion.1), channel_id=1, source_target_pairs={{0,32},{32,0},{64,96},{96,64},{128,160},{160,128},{192,224},{224,1... | collective-permute-start | bytes 1769480 | tf_op jit(solution)/shard_map/ppermute | solution.py:71
  140.7 12.8 %collective-permute-done.4 = f32[576,256]{1,0:T(8,128)S(1)} collective-permute-done((f32[576,256]{1,0:T(8,128)S(1)}, f32[576,256]{1,0:T(8,128)S(1)}, u32[]{:S(2)}, u32[]{:S(2)}) %collective-permute-start.4) | collective-permute-done | bytes 589856 | tf_op jit(solution)/shard_map/ppermute | solution.py:71
  153.5 0.1 select_add_fusion.1
  153.7 4.9 %collective-permute-start.5 = (f32[288,256]{1,0:T(8,128)S(1)}, f32[288,256]{1,0:T(8,128)S(1)}, u32[]{:S(2)}, u32[]{:S(2)}) collective-permute-start(f32[288,256]{1,0:T(8,128)S(1)} %slice_select_fusion.3), channel_id=1, source_target_pairs={{0,64},{32,96},{64,0},{96,32},{128,192},{160,224},{192,128},{224,1... | collective-permute-start | bytes 884744 | tf_op jit(solution)/shard_map/ppermute | solution.py:71
  158.6 5.9 %collective-permute-done.5 = f32[288,256]{1,0:T(8,128)S(1)} collective-permute-done((f32[288,256]{1,0:T(8,128)S(1)}, f32[288,256]{1,0:T(8,128)S(1)}, u32[]{:S(2)}, u32[]{:S(2)}) %collective-permute-start.5) | collective-permute-done | bytes 294944 | tf_op jit(solution)/shard_map/ppermute | solution.py:71
  164.4 0.1 add_convert_fusion
  164.5 3.3 collective-permute-start.6
  167.8 3.9 %collective-permute-done.6 = bf16[288,256]{1,0:T(8,128)(2,1)S(1)} collective-permute-done((bf16[288,256]{1,0:T(8,128)(2,1)S(1)}, bf16[288,256]{1,0:T(8,128)(2,1)S(1)}, u32[]{:S(2)}, u32[]{:S(2)}) %collective-permute-start.6) | collective-permute-done | bytes 147488 | tf_op jit(solution)/shard_map/ppermute | solution.py:76
  171.7 0.1 maximum_select_fusion.10
  171.8 0.7 collective-permute-start.7
  172.5 6.3 %collective-permute-done.7 = bf16[576,256]{1,0:T(8,128)(2,1)S(1)} collective-permute-done((bf16[576,256]{1,0:T(8,128)(2,1)S(1)}, bf16[576,256]{1,0:T(8,128)(2,1)S(1)}, u32[]{:S(2)}, u32[]{:S(2)}) %collective-permute-start.7) | collective-permute-done | bytes 294944 | tf_op jit(solution)/shard_map/ppermute | solution.py:76
  178.8 0.3 maximum_select_fusion.8
  179.1 0.6 collective-permute-start.8
  179.7 10.7 %collective-permute-done.8 = bf16[1152,256]{1,0:T(8,128)(2,1)S(1)} collective-permute-done((bf16[1152,256]{1,0:T(8,128)(2,1)S(1)}, bf16[1152,256]{1,0:T(8,128)(2,1)S(1)}, u32[]{:S(2)}, u32[]{:S(2)}) %collective-permute-start.8) | collective-permute-done | bytes 589856 | tf_op jit(solution)/shard_map/ppermute | solution.py:76
  190.4 0.4 fusion.9
  190.8 0.4 fusion.15
  191.2 2.6 collective-permute-start.9
  193.8 22.3 %collective-permute-done.9 = bf16[3,256,768]{1,2,0:T(8,128)(2,1)S(1)} collective-permute-done((bf16[3,256,768]{1,2,0:T(8,128)(2,1)S(1)}, bf16[3,256,768]{1,2,0:T(8,128)(2,1)S(1)}, u32[]{:S(2)}, u32[]{:S(2)}) %collective-permute-start.9) | collective-permute-done | bytes 1179680 | tf_op jit(solution)/shard_map/ppermute | solution.py:54
  216.1 1.8 collective-permute-start.10
  217.9 20.4 %collective-permute-done.10 = bf16[3,256,768]{1,2,0:T(8,128)(2,1)S(1)} collective-permute-done((bf16[3,256,768]{1,2,0:T(8,128)(2,1)S(1)}, bf16[3,256,768]{1,2,0:T(8,128)(2,1)S(1)}, u32[]{:S(2)}, u32[]{:S(2)}) %collective-permute-start.10) | collective-permute-done | bytes 1179680 | tf_op jit(solution)/shard_map/ppermute | solution.py:55
  238.3 0.4 maximum_select_fusion.5
  238.6 0.1 collective-permute-start.11
  238.7 0.4 maximum_select_fusion.4
  239.1 4.1 %collective-permute-done.11 = bf16[3,256,2,768]{1,3,0,2:T(8,128)(2,1)S(1)} collective-permute-done((bf16[3,256,2,768]{1,3,0,2:T(8,128)(2,1)S(1)}, bf16[3,256,2,768]{1,3,0,2:T(8,128)(2,1)S(1)}, u32[]{:S(2)}, u32[]{:S(2)}) %collective-permute-start.11) | collective-permute-done | bytes 2359328 | tf_op jit(solution)/shard_map/ppermute | solution.py:57
  243.3 2.5 maximum_select_fusion.1
  245.8 6.7 %copy.26 = bf16[3,256,2,2,768]{4,1,3,2,0:T(8,128)(2,1)} copy(bf16[3,256,2,2,768]{1,4,0,2,3:T(8,128)(2,1)} %maximum_select_fusion.1) | data formatting | bytes 9437184 | tf_op jit(solution)/shard_map/jit(_where)/select_n | solution.py:58
  252.5 5.7 %fusion.4 = f32[3,256,256,1]{2,1,0,3:T(8,128)S(1)} fusion(bf16[4,3,768,256]{3,2,1,0:T(8,128)(2,1)} %bitcast.47, bf16[3,256,4,768]{3,1,2,0:T(8,128)(2,1)} %bitcast.61), kind=kOutput, calls=%fused_computation.6 | convolution fusion | flops 1207959552 | bytes 10223616 | tf_op jit(solution)/shard_map/tsjk,sltj->skl/dot_general | solution.py:109
  258.2 0.1 collective-permute-start.12
  258.3 11.1 %collective-permute-done.12 = f32[384,256]{1,0:T(8,128)S(1)} collective-permute-done((f32[384,256]{1,0:T(8,128)S(1)}, f32[384,256]{1,0:T(8,128)S(1)}, u32[]{:S(2)}, u32[]{:S(2)}) %collective-permute-start.12) | collective-permute-done | bytes 393248 | tf_op jit(solution)/shard_map/ppermute | solution.py:71
  269.5 0.1 select_add_fusion.2
  269.6 33.0 %collective-permute-start.13 = (f32[192,256]{1,0:T(8,128)S(1)}, f32[192,256]{1,0:T(8,128)S(1)}, u32[]{:S(2)}, u32[]{:S(2)}) collective-permute-start(f32[192,256]{1,0:T(8,128)S(1)} %slice_select_fusion.4), channel_id=1, source_target_pairs={{0,64},{32,96},{64,0},{96,32},{128,192},{160,224},{192,128},{224,1... | collective-permute-start | bytes 589832 | tf_op jit(solution)/shard_map/ppermute | solution.py:71
  302.6 4.3 %collective-permute-done.13 = f32[192,256]{1,0:T(8,128)S(1)} collective-permute-done((f32[192,256]{1,0:T(8,128)S(1)}, f32[192,256]{1,0:T(8,128)S(1)}, u32[]{:S(2)}, u32[]{:S(2)}) %collective-permute-start.13) | collective-permute-done | bytes 196640 | tf_op jit(solution)/shard_map/ppermute | solution.py:71
  307.0 4.6 %collective-permute-start.14 = (f32[96,256]{1,0:T(8,128)S(1)}, f32[96,256]{1,0:T(8,128)S(1)}, u32[]{:S(2)}, u32[]{:S(2)}) collective-permute-start(f32[96,256]{1,0:T(8,128)S(1)} %slice_select_fusion.5), channel_id=1, source_target_pairs={{0,32},{32,0},{64,96},{96,64},{128,160},{160,128},{192,224},{224,1... | collective-permute-start | bytes 294920 | tf_op jit(solution)/shard_map/ppermute | solution.py:71
  311.6 2.6 collective-permute-done.14
  314.2 2.1 collective-permute-start.15
  316.4 2.6 collective-permute-done.15
  319.0 3.2 collective-permute-start.16
  322.2 4.1 %collective-permute-done.16 = f32[192,256]{1,0:T(8,128)S(1)} collective-permute-done((f32[192,256]{1,0:T(8,128)S(1)}, f32[192,256]{1,0:T(8,128)S(1)}, u32[]{:S(2)}, u32[]{:S(2)}) %collective-permute-start.16) | collective-permute-done | bytes 196640 | tf_op jit(solution)/shard_map/ppermute | solution.py:76
  326.3 0.8 collective-permute-start.17
  327.1 1.4 broadcast_multiply_fusion
  328.5 2.5 copy.25
  331.0 6.7 %copy.29 = bf16[3,256,3072]{2,1,0:T(8,128)(2,1)} copy(bf16[3,256,3072]{1,2,0:T(8,128)(2,1)} %bitcast.48) | data formatting | bytes 9437184
  337.7 0.1 maximum_select_fusion.7
  337.8 1.0 sub.34
  (28 shorter events, 0.3 us)
Async XLA Ops:
  3.2 29.6 %collective-permute-start = (bf16[3,768,256]{2,1,0:T(8,128)(2,1)S(1)}, bf16[3,768,256]{2,1,0:T(8,128)(2,1)S(1)}, u32[]{:S(2)}, u32[]{:S(2)}) collective-permute-start(bf16[3,768,256]{2,1,0:T(8,128)(2,1)S(1)} %broadcast_multiply_fusion.1), channel_id=1, source_target_pairs={{0,0},{1,1},{2,2},{3,3},{4,36},{5,37},{6,38},{7,39},{8,72},{9,73},... | collective-permute-start | bytes 3538952 | tf_op jit(solution)/shard_map/ppermute | solution.py:54
  32.8 27.0 %collective-permute-start.1 = (bf16[3,768,256]{2,1,0:T(8,128)(2,1)S(1)}, bf16[3,768,256]{2,1,0:T(8,128)(2,1)S(1)}, u32[]{:S(2)}, u32[]{:S(2)}) collective-permute-start(bf16[3,768,256]{2,1,0:T(8,128)(2,1)S(1)} %collective-permute-done), channel_id=1, source_target_pairs={{0,2},{1,3},{2,0},{3,1},{4,6},{5,7},{6,4},{7,5},{8,10},{9,11},{10,... | collective-permute-start | bytes 3538952 | tf_op jit(solution)/shard_map/ppermute | solution.py:55
  59.8 1.8 copy-start.2
  61.6 4.9 %collective-permute-start.2 = (bf16[2,3,768,256]{3,2,1,0:T(8,128)(2,1)}, bf16[2,3,768,256]{3,2,1,0:T(8,128)(2,1)}, u32[]{:S(2)}, u32[]{:S(2)}) collective-permute-start(bf16[2,3,768,256]{3,2,1,0:T(8,128)(2,1)} %maximum_select_fusion.3), channel_id=1, source_target_pairs={{0,1},{1,0},{2,3},{3,2},{4,5},{5,4},{6,7},{7,6},{8,9},{9,8},{10,11... | collective-permute-start | bytes 7077896 | tf_op jit(solution)/shard_map/ppermute | solution.py:57
  66.5 6.0 %slice-start.2 = ((s8[4718592]{0:T(1024)(128)(4,1)}), s8[4194304]{0:T(1024)(128)(4,1)S(1)}, s32[]{:S(2)}) async-start(s8[4718592]{0:T(1024)(128)(4,1)} %bitcast.66), calls=%async_computation.2 | async-start | bytes 8388608
  69.6 2.1 copy-start
  69.6 2.8 slice-start.3
  79.9 28.2 %collective-permute-start.3 = (f32[1152,256]{1,0:T(8,128)S(1)}, f32[1152,256]{1,0:T(8,128)}, u32[]{:S(2)}, u32[]{:S(2)}) collective-permute-start(f32[1152,256]{1,0:T(8,128)S(1)} %slice_select_fusion), channel_id=1, source_target_pairs={{0,128},{32,160},{64,192},{96,224},{128,0},{160,32},{192,64},{224,... | collective-permute-start | bytes 3538952 | tf_op jit(solution)/shard_map/ppermute | solution.py:71
  109.7 43.8 %collective-permute-start.4 = (f32[576,256]{1,0:T(8,128)S(1)}, f32[576,256]{1,0:T(8,128)S(1)}, u32[]{:S(2)}, u32[]{:S(2)}) collective-permute-start(f32[576,256]{1,0:T(8,128)S(1)} %slice_select_fusion.1), channel_id=1, source_target_pairs={{0,32},{32,0},{64,96},{96,64},{128,160},{160,128},{192,224},{224,1... | collective-permute-start | bytes 1769480 | tf_op jit(solution)/shard_map/ppermute | solution.py:71
  153.7 10.8 %collective-permute-start.5 = (f32[288,256]{1,0:T(8,128)S(1)}, f32[288,256]{1,0:T(8,128)S(1)}, u32[]{:S(2)}, u32[]{:S(2)}) collective-permute-start(f32[288,256]{1,0:T(8,128)S(1)} %slice_select_fusion.3), channel_id=1, source_target_pairs={{0,64},{32,96},{64,0},{96,32},{128,192},{160,224},{192,128},{224,1... | collective-permute-start | bytes 884744 | tf_op jit(solution)/shard_map/ppermute | solution.py:71
  164.5 7.2 %collective-permute-start.6 = (bf16[288,256]{1,0:T(8,128)(2,1)S(1)}, bf16[288,256]{1,0:T(8,128)(2,1)S(1)}, u32[]{:S(2)}, u32[]{:S(2)}) collective-permute-start(bf16[288,256]{1,0:T(8,128)(2,1)S(1)} %add_convert_fusion), channel_id=1, source_target_pairs={{0,64},{32,96},{64,0},{96,32},{128,192},{160,224},{192,128},{224,1... | collective-permute-start | bytes 442376 | tf_op jit(solution)/shard_map/ppermute | solution.py:76
  171.8 7.0 %collective-permute-start.7 = (bf16[576,256]{1,0:T(8,128)(2,1)S(1)}, bf16[576,256]{1,0:T(8,128)(2,1)S(1)}, u32[]{:S(2)}, u32[]{:S(2)}) collective-permute-start(bf16[576,256]{1,0:T(8,128)(2,1)S(1)} %maximum_select_fusion.10), channel_id=1, source_target_pairs={{0,32},{32,0},{64,96},{96,64},{128,160},{160,128},{192,224},{224,1... | collective-permute-start | bytes 884744 | tf_op jit(solution)/shard_map/ppermute | solution.py:76
  179.1 11.3 %collective-permute-start.8 = (bf16[1152,256]{1,0:T(8,128)(2,1)S(1)}, bf16[1152,256]{1,0:T(8,128)(2,1)S(1)}, u32[]{:S(2)}, u32[]{:S(2)}) collective-permute-start(bf16[1152,256]{1,0:T(8,128)(2,1)S(1)} %maximum_select_fusion.8), channel_id=1, source_target_pairs={{0,128},{32,160},{64,192},{96,224},{128,0},{160,32},{192,64},{224,... | collective-permute-start | bytes 1769480 | tf_op jit(solution)/shard_map/ppermute | solution.py:76
  191.2 24.9 %collective-permute-start.9 = (bf16[3,256,768]{1,2,0:T(8,128)(2,1)S(1)}, bf16[3,256,768]{1,2,0:T(8,128)(2,1)S(1)}, u32[]{:S(2)}, u32[]{:S(2)}) collective-permute-start(bf16[3,256,768]{1,2,0:T(8,128)(2,1)S(1)} %fusion.15), channel_id=1, source_target_pairs={{0,0},{1,1},{2,2},{3,3},{4,36},{5,37},{6,38},{7,39},{8,72},{9,73},... | collective-permute-start | bytes 3538952 | tf_op jit(solution)/shard_map/ppermute | solution.py:54
  216.1 22.2 %collective-permute-start.10 = (bf16[3,256,768]{1,2,0:T(8,128)(2,1)S(1)}, bf16[3,256,768]{1,2,0:T(8,128)(2,1)S(1)}, u32[]{:S(2)}, u32[]{:S(2)}) collective-permute-start(bf16[3,256,768]{1,2,0:T(8,128)(2,1)S(1)} %collective-permute-done.9), channel_id=1, source_target_pairs={{0,2},{1,3},{2,0},{3,1},{4,6},{5,7},{6,4},{7,5},{8,10},{9,11},{10,... | collective-permute-start | bytes 3538952 | tf_op jit(solution)/shard_map/ppermute | solution.py:55
  238.6 4.6 %collective-permute-start.11 = (bf16[3,256,2,768]{1,3,0,2:T(8,128)(2,1)S(1)}, bf16[3,256,2,768]{1,3,0,2:T(8,128)(2,1)S(1)}, u32[]{:S(2)}, u32[]{:S(2)}) collective-permute-start(bf16[3,256,2,768]{1,3,0,2:T(8,128)(2,1)S(1)} %maximum_select_fusion.5), channel_id=1, source_target_pairs={{0,1},{1,0},{2,3},{3,2},{4,5},{5,4},{6,7},{7,6},{8,9},{9,8},{10,11... | collective-permute-start | bytes 7077896 | tf_op jit(solution)/shard_map/ppermute | solution.py:57
  252.5 76.0 %slice-start = ((s8[4718592]{0:T(1024)(128)(4,1)}), s8[4194304]{0:T(1024)(128)(4,1)S(1)}, s32[]{:S(2)}) async-start(s8[4718592]{0:T(1024)(128)(4,1)} %bitcast.42), calls=%async_computation | async-start | bytes 8388608
  252.5 76.0 %slice-start.1 = ((s8[4718592]{0:T(1024)(128)(4,1)}), s8[524288]{0:T(1024)(128)(4,1)S(1)}, s32[]{:S(2)}) async-start(s8[4718592]{0:T(1024)(128)(4,1)} %bitcast.42), calls=%async_computation.1 | async-start | bytes 1048576
  258.2 11.2 %collective-permute-start.12 = (f32[384,256]{1,0:T(8,128)S(1)}, f32[384,256]{1,0:T(8,128)S(1)}, u32[]{:S(2)}, u32[]{:S(2)}) collective-permute-start(f32[384,256]{1,0:T(8,128)S(1)} %slice_select_fusion.2), channel_id=1, source_target_pairs={{0,128},{32,160},{64,192},{96,224},{128,0},{160,32},{192,64},{224,... | collective-permute-start | bytes 1179656 | tf_op jit(solution)/shard_map/ppermute | solution.py:71
  269.6 37.4 %collective-permute-start.13 = (f32[192,256]{1,0:T(8,128)S(1)}, f32[192,256]{1,0:T(8,128)S(1)}, u32[]{:S(2)}, u32[]{:S(2)}) collective-permute-start(f32[192,256]{1,0:T(8,128)S(1)} %slice_select_fusion.4), channel_id=1, source_target_pairs={{0,64},{32,96},{64,0},{96,32},{128,192},{160,224},{192,128},{224,1... | collective-permute-start | bytes 589832 | tf_op jit(solution)/shard_map/ppermute | solution.py:71
  307.0 7.2 %collective-permute-start.14 = (f32[96,256]{1,0:T(8,128)S(1)}, f32[96,256]{1,0:T(8,128)S(1)}, u32[]{:S(2)}, u32[]{:S(2)}) collective-permute-start(f32[96,256]{1,0:T(8,128)S(1)} %slice_select_fusion.5), channel_id=1, source_target_pairs={{0,32},{32,0},{64,96},{96,64},{128,160},{160,128},{192,224},{224,1... | collective-permute-start | bytes 294920 | tf_op jit(solution)/shard_map/ppermute | solution.py:71
  314.2 4.7 %collective-permute-start.15 = (f32[96,256]{1,0:T(8,128)S(1)}, f32[96,256]{1,0:T(8,128)S(1)}, u32[]{:S(2)}, u32[]{:S(2)}) collective-permute-start(f32[96,256]{1,0:T(8,128)S(1)} %select_add_fusion.4), channel_id=1, source_target_pairs={{0,32},{32,0},{64,96},{96,64},{128,160},{160,128},{192,224},{224,1... | collective-permute-start | bytes 294920 | tf_op jit(solution)/shard_map/ppermute | solution.py:76
  319.0 7.3 %collective-permute-start.16 = (f32[192,256]{1,0:T(8,128)S(1)}, f32[192,256]{1,0:T(8,128)S(1)}, u32[]{:S(2)}, u32[]{:S(2)}) collective-permute-start(f32[192,256]{1,0:T(8,128)S(1)} %maximum_select_fusion.11), channel_id=1, source_target_pairs={{0,64},{32,96},{64,0},{96,32},{128,192},{160,224},{192,128},{224,1... | collective-permute-start | bytes 589832 | tf_op jit(solution)/shard_map/ppermute | solution.py:76
  326.3 11.4 %collective-permute-start.17 = (f32[384,256]{1,0:T(8,128)S(1)}, f32[384,256]{1,0:T(8,128)S(1)}, u32[]{:S(2)}, u32[]{:S(2)}) collective-permute-start(f32[384,256]{1,0:T(8,128)S(1)} %maximum_select_fusion.9), channel_id=1, source_target_pairs={{0,128},{32,160},{64,192},{96,224},{128,0},{160,32},{192,64},{224,... | collective-permute-start | bytes 1179656 | tf_op jit(solution)/shard_map/ppermute | solution.py:76
  331.0 6.8 %copy-start.1 = (f32[3,256,256]{2,1,0:T(8,128)S(1)}, f32[3,256,256]{2,1,0:T(8,128)}, u32[]{:S(2)}) copy-start(f32[3,256,256]{2,1,0:T(8,128)} %param.9) | copy-start | bytes 2359300

commit v9 on v7

--- a/solution.py
+++ b/solution.py
@@ -111,7 +111,7 @@
         "rsjk,rsjl->skl", lower_cols, column_cols, preferred_element_type=jnp.float32
     )
     flat = contrib.reshape(supers * kwidth, kwidth)
-    diagonal = diag_base - row_sum(flat).reshape(supers, kwidth, kwidth)
+    diagonal = diag_base - row_sum(flat, order).reshape(supers, kwidth, kwidth)
     return (column, row_out, diagonal)
 
 

time: 330 us -> 331 us (level)
  no operation moved by 1% of the time
where the time goes in v9:
time: 331 us; the launch traced here: 328 us
  waiting for transfers between devices  197 us (60%)
  starting transfers between devices  92.6 us (28%)
  local copies, waits for them, and re-layouts  15.8 us (5%)
  other arithmetic  13.8 us (4%)
  matrix products  7.14 us (2%)
    ppermute x6, starting transfers between devices, row_sum(): seg = keep + lax.ppermute(send, 'prow', [(i, i ^ m) for i in range(n)])  73.4 us
    ppermute x6, waiting for transfers between devices, row_sum(): seg = keep + lax.ppermute(send, 'prow', [(i, i ^ m) for i in range(n)])  65.7 us
    ppermute x2, waiting for transfers between devices, gather_cols(): mine = lax.ppermute(block, ALL, swap)  49.4 us
    ppermute x2, waiting for transfers between devices, gather_cols(): other = lax.ppermute(mine, ALL, far)  45.5 us
    ppermute x6, waiting for transfers between devices, row_sum(): got = lax.ppermute(seg, 'prow', [(i, i ^ m) for i in range(n)])  28.1 us
    ppermute x6, starting transfers between devices, row_sum(): got = lax.ppermute(seg, 'prow', [(i, i ^ m) for i in range(n)])  10.4 us
    unnamed x17, local copies, waits for them, and re-layouts  9.93 us
    ppermute x2, waiting for transfers between devices, gather_cols(): twin = lax.ppermute(pair, ALL, near)  8.59 us
  transfers between devices with their start and end apart: 18, of which 17 were waited for; matrix products, arithmetic and copies ran while one was open for 3% of the time, Pallas kernels for 0%

profile of v9, /device:TPU:4, one launch (start us, length us, event | category | flops | bytes accessed | tf_op | source)
XLA Modules:
  0.0 327.6 jit_solution(5854594742264983393)
XLA Ops:
  0.7 0.9 compare_reduce_fusion
  1.5 1.6 broadcast_multiply_fusion.1
  3.2 2.4 collective-permute-start
  5.6 27.2 %collective-permute-done = bf16[3,768,256]{2,1,0:T(8,128)(2,1)S(1)} collective-permute-done((bf16[3,768,256]{2,1,0:T(8,128)(2,1)S(1)}, bf16[3,768,256]{2,1,0:T(8,128)(2,1)S(1)}, u32[]{:S(2)}, u32[]{:S(2)}) %collective-permute-start) | collective-permute-done | bytes 1179680 | tf_op jit(solution)/shard_map/ppermute | solution.py:54
  32.8 1.9 collective-permute-start.1
  34.7 25.1 %collective-permute-done.1 = bf16[3,768,256]{2,1,0:T(8,128)(2,1)S(1)} collective-permute-done((bf16[3,768,256]{2,1,0:T(8,128)(2,1)S(1)}, bf16[3,768,256]{2,1,0:T(8,128)(2,1)S(1)}, u32[]{:S(2)}, u32[]{:S(2)}) %collective-permute-start.1) | collective-permute-done | bytes 1179680 | tf_op jit(solution)/shard_map/ppermute | solution.py:55
  59.8 1.8 maximum_select_fusion.2
  61.6 0.4 bitcast_select_fusion
  62.0 4.5 %collective-permute-done.2 = bf16[2,3,768,256]{3,2,1,0:T(8,128)(2,1)} collective-permute-done((bf16[2,3,768,256]{3,2,1,0:T(8,128)(2,1)}, bf16[2,3,768,256]{3,2,1,0:T(8,128)(2,1)}, u32[]{:S(2)}, u32[]{:S(2)}) %collective-permute-start.2) | collective-permute-done | bytes 2359328 | tf_op jit(solution)/shard_map/ppermute | solution.py:57
  66.5 3.1 maximum_select_fusion
  69.6 0.3 copy.30
  70.0 1.8 copy-done
  71.8 0.7 broadcast_in_dim.2
  72.5 5.3 %fusion.4 = f32[3,768,256]{1,2,0:T(8,128)} fusion(bf16[3,3072,256]{2,1,0:T(8,128)(2,1)S(1)} %bitcast.62, bf16[768,3072]{1,0:T(8,128)(2,1)S(1)} %bitcast.70, bf16[96,8,24,128]{3,2,1,0:T(8,128)(2,1)S(1)} %bitcast.63), kind=kOutput, calls=%fused_computation.10 | convolution fusion | flops 3626237952 | bytes 16515072 | tf_op jit(solution)/shard_map/ij,sjk->sik/dot_general | solution.py:99
  77.8 2.0 copy.32
  79.9 0.2 slice_select_fusion
  80.0 0.1 collective-permute-start.3
  80.1 28.1 %collective-permute-done.3 = f32[1152,256]{1,0:T(8,128)} collective-permute-done((f32[1152,256]{1,0:T(8,128)S(1)}, f32[1152,256]{1,0:T(8,128)}, u32[]{:S(2)}, u32[]{:S(2)}) %collective-permute-start.3) | collective-permute-done | bytes 1179680 | tf_op jit(solution)/shard_map/ppermute | solution.py:72
  108.2 1.5 select_add_fusion
  109.7 0.1 slice_select_fusion.1
  109.8 31.0 %collective-permute-start.4 = (f32[576,256]{1,0:T(8,128)S(1)}, f32[576,256]{1,0:T(8,128)S(1)}, u32[]{:S(2)}, u32[]{:S(2)}) collective-permute-start(f32[576,256]{1,0:T(8,128)S(1)} %slice_select_fusion.1), channel_id=1, source_target_pairs={{0,32},{32,0},{64,96},{96,64},{128,160},{160,128},{192,224},{224,1... | collective-permute-start | bytes 1769480 | tf_op jit(solution)/shard_map/ppermute | solution.py:72
  140.8 12.8 %collective-permute-done.4 = f32[576,256]{1,0:T(8,128)S(1)} collective-permute-done((f32[576,256]{1,0:T(8,128)S(1)}, f32[576,256]{1,0:T(8,128)S(1)}, u32[]{:S(2)}, u32[]{:S(2)}) %collective-permute-start.4) | collective-permute-done | bytes 589856 | tf_op jit(solution)/shard_map/ppermute | solution.py:72
  153.6 0.1 select_add_fusion.1
  153.7 4.9 %collective-permute-start.5 = (f32[288,256]{1,0:T(8,128)S(1)}, f32[288,256]{1,0:T(8,128)S(1)}, u32[]{:S(2)}, u32[]{:S(2)}) collective-permute-start(f32[288,256]{1,0:T(8,128)S(1)} %slice_select_fusion.3), channel_id=1, source_target_pairs={{0,64},{32,96},{64,0},{96,32},{128,192},{160,224},{192,128},{224,1... | collective-permute-start | bytes 884744 | tf_op jit(solution)/shard_map/ppermute | solution.py:72
  158.6 5.9 %collective-permute-done.5 = f32[288,256]{1,0:T(8,128)S(1)} collective-permute-done((f32[288,256]{1,0:T(8,128)S(1)}, f32[288,256]{1,0:T(8,128)S(1)}, u32[]{:S(2)}, u32[]{:S(2)}) %collective-permute-start.5) | collective-permute-done | bytes 294944 | tf_op jit(solution)/shard_map/ppermute | solution.py:72
  164.6 3.3 %collective-permute-start.6 = (bf16[288,256]{1,0:T(8,128)(2,1)S(1)}, bf16[288,256]{1,0:T(8,128)(2,1)S(1)}, u32[]{:S(2)}, u32[]{:S(2)}) collective-permute-start(bf16[288,256]{1,0:T(8,128)(2,1)S(1)} %add_convert_fusion), channel_id=1, source_target_pairs={{0,64},{32,96},{64,0},{96,32},{128,192},{160,224},{192,128},{224,1... | collective-permute-start | bytes 442376 | tf_op jit(solution)/shard_map/ppermute | solution.py:77
  167.9 3.9 %collective-permute-done.6 = bf16[288,256]{1,0:T(8,128)(2,1)S(1)} collective-permute-done((bf16[288,256]{1,0:T(8,128)(2,1)S(1)}, bf16[288,256]{1,0:T(8,128)(2,1)S(1)}, u32[]{:S(2)}, u32[]{:S(2)}) %collective-permute-start.6) | collective-permute-done | bytes 147488 | tf_op jit(solution)/shard_map/ppermute | solution.py:77
  171.8 0.1 maximum_select_fusion.9
  171.9 0.7 collective-permute-start.7
  172.6 6.3 %collective-permute-done.7 = bf16[576,256]{1,0:T(8,128)(2,1)S(1)} collective-permute-done((bf16[576,256]{1,0:T(8,128)(2,1)S(1)}, bf16[576,256]{1,0:T(8,128)(2,1)S(1)}, u32[]{:S(2)}, u32[]{:S(2)}) %collective-permute-start.7) | collective-permute-done | bytes 294944 | tf_op jit(solution)/shard_map/ppermute | solution.py:77
  178.9 0.3 maximum_select_fusion.7
  179.2 0.6 collective-permute-start.8
  179.7 10.7 %collective-permute-done.8 = bf16[1152,256]{1,0:T(8,128)(2,1)S(1)} collective-permute-done((bf16[1152,256]{1,0:T(8,128)(2,1)S(1)}, bf16[1152,256]{1,0:T(8,128)(2,1)S(1)}, u32[]{:S(2)}, u32[]{:S(2)}) %collective-permute-start.8) | collective-permute-done | bytes 589856 | tf_op jit(solution)/shard_map/ppermute | solution.py:77
  190.5 0.4 fusion.7
  190.9 0.4 broadcast_multiply_fusion
  191.3 2.6 collective-permute-start.9
  193.9 22.3 %collective-permute-done.9 = bf16[3,768,256]{2,1,0:T(8,128)(2,1)S(1)} collective-permute-done((bf16[3,768,256]{2,1,0:T(8,128)(2,1)S(1)}, bf16[3,768,256]{2,1,0:T(8,128)(2,1)S(1)}, u32[]{:S(2)}, u32[]{:S(2)}) %collective-permute-start.9) | collective-permute-done | bytes 1179680 | tf_op jit(solution)/shard_map/ppermute | solution.py:54
  216.2 1.8 collective-permute-start.10
  217.9 20.4 %collective-permute-done.10 = bf16[3,768,256]{2,1,0:T(8,128)(2,1)S(1)} collective-permute-done((bf16[3,768,256]{2,1,0:T(8,128)(2,1)S(1)}, bf16[3,768,256]{2,1,0:T(8,128)(2,1)S(1)}, u32[]{:S(2)}, u32[]{:S(2)}) %collective-permute-start.10) | collective-permute-done | bytes 1179680 | tf_op jit(solution)/shard_map/ppermute | solution.py:55
  238.3 0.4 maximum_select_fusion.4
  238.7 0.1 collective-permute-start.11
  238.8 0.4 maximum_select_fusion.3
  239.2 4.1 %collective-permute-done.11 = bf16[2,3,768,256]{3,2,1,0:T(8,128)(2,1)S(1)} collective-permute-done((bf16[2,3,768,256]{3,2,1,0:T(8,128)(2,1)S(1)}, bf16[2,3,768,256]{3,2,1,0:T(8,128)(2,1)S(1)}, u32[]{:S(2)}, u32[]{:S(2)}) %collective-permute-start.11) | collective-permute-done | bytes 2359328 | tf_op jit(solution)/shard_map/ppermute | solution.py:57
  243.3 0.7 maximum_select_fusion.1
  244.1 0.3 copy.33
  244.4 1.1 slice-done
  245.5 0.3 slice-done.1
  245.8 1.8 fusion.11
  247.7 0.1 collective-permute-start.12
  247.8 11.1 %collective-permute-done.12 = f32[384,256]{1,0:T(8,128)S(1)} collective-permute-done((f32[384,256]{1,0:T(8,128)S(1)}, f32[384,256]{1,0:T(8,128)S(1)}, u32[]{:S(2)}, u32[]{:S(2)}) %collective-permute-start.12) | collective-permute-done | bytes 393248 | tf_op jit(solution)/shard_map/ppermute | solution.py:72
  259.0 0.1 select_add_fusion.2
  259.1 34.5 %collective-permute-start.13 = (f32[192,256]{1,0:T(8,128)S(1)}, f32[192,256]{1,0:T(8,128)S(1)}, u32[]{:S(2)}, u32[]{:S(2)}) collective-permute-start(f32[192,256]{1,0:T(8,128)S(1)} %slice_select_fusion.4), channel_id=1, source_target_pairs={{0,32},{32,0},{64,96},{96,64},{128,160},{160,128},{192,224},{224,1... | collective-permute-start | bytes 589832 | tf_op jit(solution)/shard_map/ppermute | solution.py:72
  293.6 4.3 %collective-permute-done.13 = f32[192,256]{1,0:T(8,128)S(1)} collective-permute-done((f32[192,256]{1,0:T(8,128)S(1)}, f32[192,256]{1,0:T(8,128)S(1)}, u32[]{:S(2)}, u32[]{:S(2)}) %collective-permute-start.13) | collective-permute-done | bytes 196640 | tf_op jit(solution)/shard_map/ppermute | solution.py:72
  298.0 2.7 collective-permute-start.14
  300.7 3.5 %collective-permute-done.14 = f32[96,256]{1,0:T(8,128)S(1)} collective-permute-done((f32[96,256]{1,0:T(8,128)S(1)}, f32[96,256]{1,0:T(8,128)S(1)}, u32[]{:S(2)}, u32[]{:S(2)}) %collective-permute-start.14) | collective-permute-done | bytes 98336 | tf_op jit(solution)/shard_map/ppermute | solution.py:72
  304.3 2.7 collective-permute-start.15
  307.0 3.5 %collective-permute-done.15 = f32[96,256]{1,0:T(8,128)S(1)} collective-permute-done((f32[96,256]{1,0:T(8,128)S(1)}, f32[96,256]{1,0:T(8,128)S(1)}, u32[]{:S(2)}, u32[]{:S(2)}) %collective-permute-start.15) | collective-permute-done | bytes 98336 | tf_op jit(solution)/shard_map/ppermute | solution.py:77
  310.5 2.5 collective-permute-start.16
  313.0 3.6 %collective-permute-done.16 = f32[192,256]{1,0:T(8,128)S(1)} collective-permute-done((f32[192,256]{1,0:T(8,128)S(1)}, f32[192,256]{1,0:T(8,128)S(1)}, u32[]{:S(2)}, u32[]{:S(2)}) %collective-permute-start.16) | collective-permute-done | bytes 196640 | tf_op jit(solution)/shard_map/ppermute | solution.py:77
  316.6 0.7 collective-permute-start.17
  317.3 2.5 copy.34
  319.8 6.7 %copy.36 = bf16[3,256,3072]{2,1,0:T(8,128)(2,1)} copy(bf16[3,256,3072]{1,2,0:T(8,128)(2,1)} %bitcast.53) | data formatting | bytes 9437184
  326.5 0.1 maximum_select_fusion.6
  326.6 1.0 sub.34
  (29 shorter events, 0.4 us)
Async XLA Ops:
  3.2 29.6 %collective-permute-start = (bf16[3,768,256]{2,1,0:T(8,128)(2,1)S(1)}, bf16[3,768,256]{2,1,0:T(8,128)(2,1)S(1)}, u32[]{:S(2)}, u32[]{:S(2)}) collective-permute-start(bf16[3,768,256]{2,1,0:T(8,128)(2,1)S(1)} %broadcast_multiply_fusion.1), channel_id=1, source_target_pairs={{0,0},{1,1},{2,2},{3,3},{4,36},{5,37},{6,38},{7,39},{8,72},{9,73},... | collective-permute-start | bytes 3538952 | tf_op jit(solution)/shard_map/ppermute | solution.py:54
  32.8 27.0 %collective-permute-start.1 = (bf16[3,768,256]{2,1,0:T(8,128)(2,1)S(1)}, bf16[3,768,256]{2,1,0:T(8,128)(2,1)S(1)}, u32[]{:S(2)}, u32[]{:S(2)}) collective-permute-start(bf16[3,768,256]{2,1,0:T(8,128)(2,1)S(1)} %collective-permute-done), channel_id=1, source_target_pairs={{0,2},{1,3},{2,0},{3,1},{4,6},{5,7},{6,4},{7,5},{8,10},{9,11},{10,... | collective-permute-start | bytes 3538952 | tf_op jit(solution)/shard_map/ppermute | solution.py:55
  59.8 1.8 copy-start.3
  61.6 4.9 %collective-permute-start.2 = (bf16[2,3,768,256]{3,2,1,0:T(8,128)(2,1)}, bf16[2,3,768,256]{3,2,1,0:T(8,128)(2,1)}, u32[]{:S(2)}, u32[]{:S(2)}) collective-permute-start(bf16[2,3,768,256]{3,2,1,0:T(8,128)(2,1)} %maximum_select_fusion.2), channel_id=1, source_target_pairs={{0,1},{1,0},{2,3},{3,2},{4,5},{5,4},{6,7},{7,6},{8,9},{9,8},{10,11... | collective-permute-start | bytes 7077896 | tf_op jit(solution)/shard_map/ppermute | solution.py:57
  66.5 6.0 %slice-start.2 = ((s8[4718592]{0:T(1024)(128)(4,1)}), s8[4194304]{0:T(1024)(128)(4,1)S(1)}, s32[]{:S(2)}) async-start(s8[4718592]{0:T(1024)(128)(4,1)} %bitcast.69), calls=%async_computation.2 | async-start | bytes 8388608
  69.6 2.2 copy-start
  69.6 2.9 slice-start.3
  80.0 28.2 %collective-permute-start.3 = (f32[1152,256]{1,0:T(8,128)S(1)}, f32[1152,256]{1,0:T(8,128)}, u32[]{:S(2)}, u32[]{:S(2)}) collective-permute-start(f32[1152,256]{1,0:T(8,128)S(1)} %slice_select_fusion), channel_id=1, source_target_pairs={{0,128},{32,160},{64,192},{96,224},{128,0},{160,32},{192,64},{224,... | collective-permute-start | bytes 3538952 | tf_op jit(solution)/shard_map/ppermute | solution.py:72
  109.8 43.8 %collective-permute-start.4 = (f32[576,256]{1,0:T(8,128)S(1)}, f32[576,256]{1,0:T(8,128)S(1)}, u32[]{:S(2)}, u32[]{:S(2)}) collective-permute-start(f32[576,256]{1,0:T(8,128)S(1)} %slice_select_fusion.1), channel_id=1, source_target_pairs={{0,32},{32,0},{64,96},{96,64},{128,160},{160,128},{192,224},{224,1... | collective-permute-start | bytes 1769480 | tf_op jit(solution)/shard_map/ppermute | solution.py:72
  153.7 10.8 %collective-permute-start.5 = (f32[288,256]{1,0:T(8,128)S(1)}, f32[288,256]{1,0:T(8,128)S(1)}, u32[]{:S(2)}, u32[]{:S(2)}) collective-permute-start(f32[288,256]{1,0:T(8,128)S(1)} %slice_select_fusion.3), channel_id=1, source_target_pairs={{0,64},{32,96},{64,0},{96,32},{128,192},{160,224},{192,128},{224,1... | collective-permute-start | bytes 884744 | tf_op jit(solution)/shard_map/ppermute | solution.py:72
  164.6 7.2 %collective-permute-start.6 = (bf16[288,256]{1,0:T(8,128)(2,1)S(1)}, bf16[288,256]{1,0:T(8,128)(2,1)S(1)}, u32[]{:S(2)}, u32[]{:S(2)}) collective-permute-start(bf16[288,256]{1,0:T(8,128)(2,1)S(1)} %add_convert_fusion), channel_id=1, source_target_pairs={{0,64},{32,96},{64,0},{96,32},{128,192},{160,224},{192,128},{224,1... | collective-permute-start | bytes 442376 | tf_op jit(solution)/shard_map/ppermute | solution.py:77
  171.9 7.0 %collective-permute-start.7 = (bf16[576,256]{1,0:T(8,128)(2,1)S(1)}, bf16[576,256]{1,0:T(8,128)(2,1)S(1)}, u32[]{:S(2)}, u32[]{:S(2)}) collective-permute-start(bf16[576,256]{1,0:T(8,128)(2,1)S(1)} %maximum_select_fusion.9), channel_id=1, source_target_pairs={{0,32},{32,0},{64,96},{96,64},{128,160},{160,128},{192,224},{224,1... | collective-permute-start | bytes 884744 | tf_op jit(solution)/shard_map/ppermute | solution.py:77
  179.2 11.3 %collective-permute-start.8 = (bf16[1152,256]{1,0:T(8,128)(2,1)S(1)}, bf16[1152,256]{1,0:T(8,128)(2,1)S(1)}, u32[]{:S(2)}, u32[]{:S(2)}) collective-permute-start(bf16[1152,256]{1,0:T(8,128)(2,1)S(1)} %maximum_select_fusion.7), channel_id=1, source_target_pairs={{0,128},{32,160},{64,192},{96,224},{128,0},{160,32},{192,64},{224,... | collective-permute-start | bytes 1769480 | tf_op jit(solution)/shard_map/ppermute | solution.py:77
  191.3 47.4 %copy-start.1 = (bf16[3,768,256]{2,1,0:T(8,128)(2,1)}, bf16[3,768,256]{2,1,0:T(8,128)(2,1)S(1)}, u32[]{:S(2)}) copy-start(bf16[3,768,256]{2,1,0:T(8,128)(2,1)S(1)} %broadcast_multiply_fusion) | copy-start | bytes 3538948
  191.3 24.9 %collective-permute-start.9 = (bf16[3,768,256]{2,1,0:T(8,128)(2,1)S(1)}, bf16[3,768,256]{2,1,0:T(8,128)(2,1)S(1)}, u32[]{:S(2)}, u32[]{:S(2)}) collective-permute-start(bf16[3,768,256]{2,1,0:T(8,128)(2,1)S(1)} %broadcast_multiply_fusion), channel_id=1, source_target_pairs={{0,0},{1,1},{2,2},{3,3},{4,36},{5,37},{6,38},{7,39},{8,72},{9,73},... | collective-permute-start | bytes 3538952 | tf_op jit(solution)/shard_map/ppermute | solution.py:54
  216.2 22.2 %collective-permute-start.10 = (bf16[3,768,256]{2,1,0:T(8,128)(2,1)S(1)}, bf16[3,768,256]{2,1,0:T(8,128)(2,1)S(1)}, u32[]{:S(2)}, u32[]{:S(2)}) collective-permute-start(bf16[3,768,256]{2,1,0:T(8,128)(2,1)S(1)} %collective-permute-done.9), channel_id=1, source_target_pairs={{0,2},{1,3},{2,0},{3,1},{4,6},{5,7},{6,4},{7,5},{8,10},{9,11},{10,... | collective-permute-start | bytes 3538952 | tf_op jit(solution)/shard_map/ppermute | solution.py:55
  238.7 4.6 %collective-permute-start.11 = (bf16[2,3,768,256]{3,2,1,0:T(8,128)(2,1)S(1)}, bf16[2,3,768,256]{3,2,1,0:T(8,128)(2,1)S(1)}, u32[]{:S(2)}, u32[]{:S(2)}) collective-permute-start(bf16[2,3,768,256]{3,2,1,0:T(8,128)(2,1)S(1)} %maximum_select_fusion.4), channel_id=1, source_target_pairs={{0,1},{1,0},{2,3},{3,2},{4,5},{5,4},{6,7},{7,6},{8,9},{9,8},{10,11... | collective-permute-start | bytes 7077896 | tf_op jit(solution)/shard_map/ppermute | solution.py:57
  243.3 2.2 slice-start
  244.1 1.7 slice-start.1
  247.7 11.2 %collective-permute-start.12 = (f32[384,256]{1,0:T(8,128)S(1)}, f32[384,256]{1,0:T(8,128)S(1)}, u32[]{:S(2)}, u32[]{:S(2)}) collective-permute-start(f32[384,256]{1,0:T(8,128)S(1)} %slice_select_fusion.2), channel_id=1, source_target_pairs={{0,128},{32,160},{64,192},{96,224},{128,0},{160,32},{192,64},{224,... | collective-permute-start | bytes 1179656 | tf_op jit(solution)/shard_map/ppermute | solution.py:72
  259.1 38.9 %collective-permute-start.13 = (f32[192,256]{1,0:T(8,128)S(1)}, f32[192,256]{1,0:T(8,128)S(1)}, u32[]{:S(2)}, u32[]{:S(2)}) collective-permute-start(f32[192,256]{1,0:T(8,128)S(1)} %slice_select_fusion.4), channel_id=1, source_target_pairs={{0,32},{32,0},{64,96},{96,64},{128,160},{160,128},{192,224},{224,1... | collective-permute-start | bytes 589832 | tf_op jit(solution)/shard_map/ppermute | solution.py:72
  298.0 6.2 %collective-permute-start.14 = (f32[96,256]{1,0:T(8,128)S(1)}, f32[96,256]{1,0:T(8,128)S(1)}, u32[]{:S(2)}, u32[]{:S(2)}) collective-permute-start(f32[96,256]{1,0:T(8,128)S(1)} %slice_select_fusion.5), channel_id=1, source_target_pairs={{0,64},{32,96},{64,0},{96,32},{128,192},{160,224},{192,128},{224,1... | collective-permute-start | bytes 294920 | tf_op jit(solution)/shard_map/ppermute | solution.py:72
  304.3 6.2 %collective-permute-start.15 = (f32[96,256]{1,0:T(8,128)S(1)}, f32[96,256]{1,0:T(8,128)S(1)}, u32[]{:S(2)}, u32[]{:S(2)}) collective-permute-start(f32[96,256]{1,0:T(8,128)S(1)} %select_add_fusion.4), channel_id=1, source_target_pairs={{0,64},{32,96},{64,0},{96,32},{128,192},{160,224},{192,128},{224,1... | collective-permute-start | bytes 294920 | tf_op jit(solution)/shard_map/ppermute | solution.py:77
  310.5 6.1 %collective-permute-start.16 = (f32[192,256]{1,0:T(8,128)S(1)}, f32[192,256]{1,0:T(8,128)S(1)}, u32[]{:S(2)}, u32[]{:S(2)}) collective-permute-start(f32[192,256]{1,0:T(8,128)S(1)} %maximum_select_fusion.10), channel_id=1, source_target_pairs={{0,32},{32,0},{64,96},{96,64},{128,160},{160,128},{192,224},{224,1... | collective-permute-start | bytes 589832 | tf_op jit(solution)/shard_map/ppermute | solution.py:77
  316.6 9.8 %collective-permute-start.17 = (f32[384,256]{1,0:T(8,128)S(1)}, f32[384,256]{1,0:T(8,128)S(1)}, u32[]{:S(2)}, u32[]{:S(2)}) collective-permute-start(f32[384,256]{1,0:T(8,128)S(1)} %maximum_select_fusion.8), channel_id=1, source_target_pairs={{0,128},{32,160},{64,192},{96,224},{128,0},{160,32},{192,64},{224,... | collective-permute-start | bytes 1179656 | tf_op jit(solution)/shard_map/ppermute | solution.py:77
  319.8 6.8 %copy-start.2 = (f32[3,256,256]{2,1,0:T(8,128)S(1)}, f32[3,256,256]{2,1,0:T(8,128)}, u32[]{:S(2)}) copy-start(f32[3,256,256]{2,1,0:T(8,128)} %param.9) | copy-start | bytes 2359300
